TPU v7x, 128 devices: a whole 4x4x4 slice. The times are simulated.
128 devices in a mesh: pipe: 4 (over x), expert: 32 (over z, y, core).
Axes of the slice: x: 4, y: 4, z: 4, core: 2. Of those that a mesh axis runs over, the one named last changes fastest.
Arguments:
- out_grad: bfloat16 [4, 4096, 2560], P('pipe', 'expert'), may hold values from -1.5 to 1.5
- layer_input: bfloat16 [4, 4096, 2560], P('pipe', 'expert'), may hold values from -6 to 6
- route_ids: int32 [4, 4096, 6], P('pipe', 'expert'), may hold values from 0 to 31, all different within a row; in each aligned block of 128 rows (0 to 127, 128 to 255, ..., all dimensions but the last counted through in order) at most 28 rows name the same one
- route_probs: float32 [4, 4096, 6], P('pipe', 'expert'), may hold values from 0.03 to 0.5
- gate_weight: bfloat16 [4, 32, 2560, 768], P('pipe', 'expert'), may hold values from -0.125 to 0.125
- up_weight: bfloat16 [4, 32, 2560, 768], P('pipe', 'expert'), may hold values from -0.125 to 0.125
- down_weight: bfloat16 [4, 32, 768, 2560], P('pipe', 'expert'), may hold values from -0.21875 to 0.21875
Outputs:
- prev_grad: bfloat16 [4, 4096, 2560], P('pipe', 'expert')
- gate_grad: bfloat16 [4, 4096, 6], P('pipe', 'expert')
Inputs may be any that keep to these rules, and one draw needn't show every extreme that they name: `route_ids`: each token names 6 different experts; the 128 tokens of one aligned block name one expert at most 28 times, and some block reaches 28.
All inputs are finite; a program needn't handle non-finite values.
Results may differ from a plain program's by a relative error of at most 0.004.
Values may be sent and summed in bfloat16 or wider, within the bound.
No kernel may reach another device: no remote copies, remote signals or barrier semaphores. Data moves between devices by JAX's collectives and lax.ppermute only.
A program may use at most 128 MiB of HBM per device.

v0:
```python
import jax
import jax.numpy as jnp
from jax import lax
from jax.sharding import PartitionSpec as P


def passed_along(value, axis, steps):
    count = lax.axis_size(axis)
    first, last = (max(0, -steps), min(count, count - steps))
    return lax.ppermute(value, axis, [(source, source + steps) for source in range(first, last)])


def expert_rows(grad_rows, input_rows, gate_matrix, up_matrix, down_matrix):
    gate_pre = jnp.dot(input_rows, gate_matrix, preferred_element_type=jnp.float32)
    up_pre = jnp.dot(input_rows, up_matrix, preferred_element_type=jnp.float32)
    hidden_grad = lax.dot_general(
        grad_rows, down_matrix, (((1,), (1,)), ((), ())), preferred_element_type=jnp.float32
    )
    sigmoid = jax.nn.sigmoid(gate_pre)
    active = gate_pre * sigmoid
    gate_value = jnp.sum(hidden_grad * active * up_pre, axis=-1).astype(jnp.bfloat16)
    gate_part = (hidden_grad * up_pre * sigmoid * (1.0 + gate_pre * (1.0 - sigmoid))).astype(
        jnp.bfloat16
    )
    up_part = (hidden_grad * active).astype(jnp.bfloat16)
    input_back = lax.dot_general(
        gate_part, gate_matrix, (((1,), (1,)), ((), ())), preferred_element_type=jnp.float32
    ) + lax.dot_general(
        up_part, up_matrix, (((1,), (1,)), ((), ())), preferred_element_type=jnp.float32
    )
    return input_back.astype(jnp.bfloat16), gate_value


def body(out_grad, layer_input, route_ids, route_probs, gate_weight, up_weight, down_weight):
    grad_tokens = out_grad[0]
    input_tokens = layer_input[0]
    chosen = route_ids[0]
    slot_probs = route_probs[0]
    gate_matrix = gate_weight[0, 0]
    up_matrix = up_weight[0, 0]
    down_matrix = down_weight[0, 0]
    peer_count = lax.axis_size("expert")
    token_count, top_count = chosen.shape
    model_width = grad_tokens.shape[1]
    capacity = min(token_count, 7 * token_count * top_count // (6 * peer_count))
    rows = peer_count * capacity

    flat_ids = chosen.reshape(-1)
    one_hot = (flat_ids[:, None] == jnp.arange(peer_count, dtype=jnp.int32)[None, :]).astype(
        jnp.int32
    )
    places = jnp.sum(one_hot * jnp.cumsum(one_hot, axis=0), axis=1) - 1
    target = (flat_ids * capacity + places).reshape(token_count, top_count)

    hits = target[:, :, None] == jnp.arange(rows, dtype=jnp.int32)[None, None, :]
    pick = jnp.any(hits, axis=1).astype(jnp.bfloat16)
    both = jnp.concatenate([grad_tokens, input_tokens], axis=1)
    send = lax.dot_general(
        pick, both, (((0,), (0,)), ((), ())), preferred_element_type=jnp.float32
    ).astype(jnp.bfloat16)
    send = send.reshape(peer_count, capacity, 2 * model_width)
    arrived = lax.all_to_all(send, "expert", 0, 0, tiled=True)
    arrived = arrived.reshape(rows, 2 * model_width)
    back, gate_value = expert_rows(
        arrived[:, :model_width], arrived[:, model_width:], gate_matrix, up_matrix, down_matrix
    )
    returned = lax.all_to_all(
        back.reshape(peer_count, capacity, model_width), "expert", 0, 0, tiled=True
    ).reshape(rows, model_width)
    gate_back = lax.all_to_all(
        gate_value.reshape(peer_count, capacity), "expert", 0, 0, tiled=True
    ).reshape(rows)

    weights = jnp.sum(jnp.where(hits, slot_probs[:, :, None], 0.0), axis=1)
    combined = grad_tokens.astype(jnp.float32) + jnp.dot(
        weights,
        returned.astype(jnp.float32),
        precision=lax.Precision.HIGHEST,
        preferred_element_type=jnp.float32,
    )
    gate_slot = gate_back[target.reshape(-1)].reshape(token_count, top_count)
    passed = passed_along(combined.astype(jnp.bfloat16), "pipe", -1)
    return (passed[None], gate_slot[None])


def solution(mesh):
    placed = (
        P("pipe", "expert", None),
        P("pipe", "expert", None),
        P("pipe", "expert", None),
        P("pipe", "expert", None),
        P("pipe", "expert", None, None),
        P("pipe", "expert", None, None),
        P("pipe", "expert", None, None),
    )
    return jax.shard_map(
        body,
        mesh=mesh,
        in_specs=placed,
        out_specs=(P("pipe", "expert", None), P("pipe", "expert", None)),
        check_vma=False,
    )
```

profile of v0, /device:TPU:0, one launch (start us, length us, event | category | flops | bytes accessed | tf_op | source)
XLA Modules:
  0.0 319.8 jit_solution(16845030359533198077)
XLA Ops:
  0.6 0.8 copy.24
  1.4 0.1 eq.42
  1.6 0.1 eq.38
  1.7 1.7 reduce-window.6
  3.5 0.3 slice_reduce_fusion
  3.7 0.1 fusion.20
  3.9 0.1 sub.12
  4.0 0.1 copy.28
  4.1 0.5 fusion.13
  4.6 7.4 %convolution_convert_fusion = bf16[896,5120]{1,0:T(8,128)(2,1)} fusion(pred[128,896]{1,0:T(8,128)(4,1)S(1)} %fusion.13, bf16[128,2560]{1,0:T(8,128)(2,1)} %bitcast.44, bf16[128,2560]{1,0:T(8,128)(2,1)} %bitcast.43), kind=kOutput, calls=%fused_computation.2 | convolution fusion | flops 1181614080 | bytes 10600448 | tf_op jit(solution)/shard_map/dot_general | solution.py:58
  12.0 13.1 %reshape.102 = bf16[32,28,5120]{2,1,0:T(8,128)(2,1)} reshape(bf16[896,5120]{1,0:T(8,128)(2,1)} %convolution_convert_fusion) | data formatting | bytes 18350080 | tf_op jit(solution)/shard_map/reshape | solution.py:61
  25.1 126.9 %all_to_all.16 = bf16[32,28,5120]{2,1,0:T(8,128)(2,1)} all-to-all(bf16[32,28,5120]{2,1,0:T(8,128)(2,1)} %reshape.102), channel_id=1, replica_groups=mesh['pipe'=4,'expert'=32] {'expert'}, dimensions={0} | all-to-all | bytes 18350080 | tf_op jit(solution)/shard_map/all_to_all | solution.py:62
  152.0 13.2 %reshape.103 = bf16[896,5120]{1,0:T(8,128)(2,1)} reshape(bf16[32,28,5120]{2,1,0:T(8,128)(2,1)} %all_to_all.16) | data formatting | bytes 18350080 | tf_op jit(solution)/shard_map/reshape | solution.py:63
  165.1 0.0 copy-start
  165.1 0.0 copy-start.3
  165.2 9.4 %fusion = f32[896,768]{0,1:T(8,128)} fusion(bf16[896,5120]{1,0:T(8,128)(2,1)} %reshape.103, bf16[1,1,768,2560]{3,2,1,0:T(8,128)(2,1)} %param.13), kind=kOutput, calls=%fused_computation.3 | convolution fusion | flops 3523215360 | bytes 11272192 | tf_op jit(solution)/shard_map/dot_general | solution.py:16
  174.5 0.0 copy-done
  174.5 0.0 copy-done.3
  174.6 0.0 copy-start.4
  174.6 5.9 %fusion.2 = f32[896,768]{0,1:T(8,128)} fusion(bf16[896,5120]{1,0:T(8,128)(2,1)S(1)} %copy-done, bf16[1,1,2560,768]{3,2,1,0:T(8,128)(2,1)S(1)} %copy-done.3), kind=kOutput, calls=%fused_computation.5 | convolution fusion | flops 3523215360 | bytes 11272192 | tf_op jit(solution)/shard_map/dot_general | solution.py:14
  180.5 0.0 copy-done.4
  180.5 7.8 %multiply_reduce_fusion = (bf16[896]{0:T(1024)(128)(2,1)S(1)}, f32[896,768]{0,1:T(8,128)}) fusion(f32[896,768]{0,1:T(8,128)} %fusion, f32[896,768]{0,1:T(8,128)} %fusion.2, bf16[1,1,2560,768]{3,2,1,0:T(8,128)(2,1)S(1)} %copy-done.4, bf16[896,5120]{1,0:T(8,128)(2,1)S(1)} %copy-done), kind=kOutput, calls=%fused_computation.17 | convolution fusion | flops 3528031232 | bytes 16779008 | tf_op jit(solution)/shard_map/dot_general | solution.py:15
  188.2 11.1 %fusion.6 = f32[896,2560]{1,0:T(8,128)} fusion(bf16[1,1,2560,768]{3,2,1,0:T(8,128)(2,1)S(1)} %copy-done.3, f32[896,768]{0,1:T(8,128)} %fusion.2, f32[896,768]{0,1:T(8,128)} %fusion, f32[896,768]{0,1:T(8,128)} %get-tuple-element.9), kind=kOutput, calls=%fused_computation.9 | convolution fusion | flops 3530096640 | bytes 21364736 | tf_op jit(solution)/shard_map/dot_general | solution.py:26
  199.4 10.5 %add_convert_fusion = bf16[896,2560]{1,0:T(8,128)(2,1)} fusion(f32[896,2560]{1,0:T(8,128)} %fusion.6, bf16[1,1,2560,768]{3,2,1,0:T(8,128)(2,1)S(1)} %copy-done.4, f32[896,768]{0,1:T(8,128)} %fusion, f32[896,768]{0,1:T(8,128)} %fusion.2), kind=kOutput, calls=%fused_computation.1 | convolution fusion | flops 3531931648 | bytes 23199744 | tf_op jit(solution)/shard_map/dot_general | solution.py:28
  209.9 7.2 %reshape.104 = bf16[32,28,2560]{2,1,0:T(8,128)(2,1)} reshape(bf16[896,2560]{1,0:T(8,128)(2,1)} %add_convert_fusion) | data formatting | bytes 9175040 | tf_op jit(solution)/shard_map/reshape | solution.py:68
  217.0 0.0 copy-start.2
  217.0 5.0 %all-to-all-start.1 = ((bf16[32,28,2560]{2,1,0:T(8,128)(2,1)}), bf16[32,28,2560]{2,1,0:T(8,128)(2,1)}, u32[]{:S(2)}, u32[]{:S(2)}) async-start(bf16[32,28,2560]{2,1,0:T(8,128)(2,1)} %reshape.104), calls=%async_computation.1 | async-start | bytes 10485760 | tf_op jit(solution)/shard_map/all_to_all | solution.py:67
  222.0 0.0 copy-done.2
  222.1 0.3 select_reduce_fusion
  222.4 0.0 copy-start.1
  222.4 65.5 %all-to-all-done.1 = bf16[32,28,2560]{2,1,0:T(8,128)(2,1)} async-done(((bf16[32,28,2560]{2,1,0:T(8,128)(2,1)}), bf16[32,28,2560]{2,1,0:T(8,128)(2,1)}, u32[]{:S(2)}, u32[]{:S(2)}) %all-to-all-start.1) | async-done | bytes 4587552 | tf_op jit(solution)/shard_map/all_to_all | solution.py:67
  287.9 7.2 %reshape.105 = bf16[896,2560]{1,0:T(8,128)(2,1)} reshape(bf16[32,28,2560]{2,1,0:T(8,128)(2,1)} %all-to-all-done.1) | data formatting | bytes 9175040 | tf_op jit(solution)/shard_map/reshape | solution.py:69
  295.1 0.0 copy-done.1
  295.1 4.5 %fusion.12 = bf16[128,2560]{1,0:T(8,128)(2,1)S(1)} fusion(f32[128,896]{1,0:T(8,128)S(1)} %select_reduce_fusion, bf16[896,2560]{1,0:T(8,128)(2,1)} %reshape.105, bf16[1,128,2560]{2,1,0:T(8,128)(2,1)S(1)} %copy-done.1), kind=kOutput, calls=%fused_computation.16 | convolution fusion | flops 3524198400 | bytes 6356992 | tf_op jit(solution)/shard_map/dot_general | solution.py:75
  299.6 1.3 collective-permute-start
  300.9 0.1 mul.59
  301.1 0.7 convert_element_type.48
  301.8 3.8 %all-to-all-start.2 = ((bf16[32,1,28]{2,1,0:T(2,128)(2,1)}), bf16[32,1,28]{2,1,0:T(2,128)(2,1)S(1)}, u32[]{:S(2)}, u32[]{:S(2)}) async-start(bf16[32,1,28]{2,1,0:T(2,128)(2,1)} %convert_element_type.48), calls=%async_computation.2 | async-start | bytes 32768 | tf_op jit(solution)/shard_map/all_to_all | solution.py:70
  305.7 7.3 %all-to-all-done.2 = bf16[32,1,28]{2,1,0:T(2,128)(2,1)S(1)} async-done(((bf16[32,1,28]{2,1,0:T(2,128)(2,1)}), bf16[32,1,28]{2,1,0:T(2,128)(2,1)S(1)}, u32[]{:S(2)}, u32[]{:S(2)}) %all-to-all-start.2) | async-done | bytes 1824 | tf_op jit(solution)/shard_map/all_to_all | solution.py:70
  313.0 0.1 reduce.1
  313.0 0.1 reshape.106
  313.1 5.0 %gather_fusion = bf16[768]{0:T(1024)(128)(2,1)S(1)} fusion(bf16[896]{0:T(1024)(128)(2,1)S(1)} %reshape.106, s32[1024]{0:T(1024)S(1)} %pad_clamp_fusion), kind=kCustom, calls=%fused_computation | custom fusion | bytes 6144 | tf_op jit(solution)/shard_map/gather | solution.py:81
  318.2 0.1 broadcast_in_dim_reshape.4
  318.3 0.7 copy.30
  319.0 0.0 collective-permute-done
  319.0 0.8 copy.37
  (8 shorter events, 0.1 us)
Async XLA Ops:
  165.1 9.4 %copy-start = (bf16[896,5120]{1,0:T(8,128)(2,1)S(1)}, bf16[896,5120]{1,0:T(8,128)(2,1)}, u32[]{:S(2)}) copy-start(bf16[896,5120]{1,0:T(8,128)(2,1)} %reshape.103) | copy-start | bytes 27525124
  165.1 9.4 %copy-start.3 = (bf16[1,1,2560,768]{3,2,1,0:T(8,128)(2,1)S(1)}, bf16[1,1,2560,768]{3,2,1,0:T(8,128)(2,1)}, u32[]{:S(2)}) copy-start(bf16[1,1,2560,768]{3,2,1,0:T(8,128)(2,1)} %param.11) | copy-start | bytes 11796484
  174.6 5.9 %copy-start.4 = (bf16[1,1,2560,768]{3,2,1,0:T(8,128)(2,1)S(1)}, bf16[1,1,2560,768]{3,2,1,0:T(8,128)(2,1)}, u32[]{:S(2)}) copy-start(bf16[1,1,2560,768]{3,2,1,0:T(8,128)(2,1)} %param.12) | copy-start | bytes 11796484
  217.0 5.0 %copy-start.2 = (f32[1,128,6]{1,0,2:T(1,128)S(1)}, f32[1,128,6]{1,0,2:T(1,128)}, u32[]{:S(2)}) copy-start(f32[1,128,6]{1,0,2:T(1,128)} %param.10) | copy-start | bytes 9220
  217.0 70.9 %all-to-all-start.1 = ((bf16[32,28,2560]{2,1,0:T(8,128)(2,1)}), bf16[32,28,2560]{2,1,0:T(8,128)(2,1)}, u32[]{:S(2)}, u32[]{:S(2)}) async-start(bf16[32,28,2560]{2,1,0:T(8,128)(2,1)} %reshape.104), calls=%async_computation.1 | async-start | bytes 10485760 | tf_op jit(solution)/shard_map/all_to_all | solution.py:67
  222.4 72.7 %copy-start.1 = (bf16[1,128,2560]{2,1,0:T(8,128)(2,1)S(1)}, bf16[1,128,2560]{2,1,0:T(8,128)(2,1)}, u32[]{:S(2)}) copy-start(bf16[1,128,2560]{2,1,0:T(8,128)(2,1)} %param.7) | copy-start | bytes 1966084
  299.6 19.4 %collective-permute-start = (bf16[128,2560]{1,0:T(8,128)(2,1)S(1)}, bf16[128,2560]{1,0:T(8,128)(2,1)S(1)}, u32[]{:S(2)}, u32[]{:S(2)}) collective-permute-start(bf16[128,2560]{1,0:T(8,128)(2,1)S(1)} %fusion.12), channel_id=1, source_target_pairs={{32,0},{64,32},{96,64},{33,1},{65,33},{97,65},{34,2},{66,34},{98,6... | collective-permute-start | bytes 1966088 | tf_op jit(solution)/shard_map/ppermute | solution.py:10
  301.8 11.1 %all-to-all-start.2 = ((bf16[32,1,28]{2,1,0:T(2,128)(2,1)}), bf16[32,1,28]{2,1,0:T(2,128)(2,1)S(1)}, u32[]{:S(2)}, u32[]{:S(2)}) async-start(bf16[32,1,28]{2,1,0:T(2,128)(2,1)} %convert_element_type.48), calls=%async_computation.2 | async-start | bytes 32768 | tf_op jit(solution)/shard_map/all_to_all | solution.py:70
where the time goes:
time: 323 us; the launch traced here: 320 us
  blocking collectives  127 us (39%)
  waiting for transfers between devices  72.8 us (23%)
  matrix products  56.7 us (18%)
  local copies, waits for them, and re-layouts  49.8 us (15%)
  starting transfers between devices  10.1 us (3%)
    all_to_all x1, blocking collectives, body(): arrived = lax.all_to_all(send, 'expert', 0, 0, tiled=True)  127 us
    all_to_all x1, waiting for transfers between devices, body(): lax.all_to_all(back.reshape(peer_count, capacity, model_width), 'expert',...  65.5 us
    reshape x1, local copies, waits for them, and re-layouts, body(): arrived = arrived.reshape(rows, 2 * model_width)  13.2 us
    reshape x1, local copies, waits for them, and re-layouts, body(): send = send.reshape(peer_count, capacity, 2 * model_width)  13.1 us
    dot_general x1, matrix products, expert_rows(): lax.dot_general(gate_part, gate_matrix, (((1,), (1,)), ((), ())), preferr...  11.1 us
    dot_general x1, matrix products, expert_rows(): lax.dot_general(up_part, up_matrix, (((1,), (1,)), ((), ())), preferred_e...  10.5 us
    dot_general x1, matrix products, expert_rows(): lax.dot_general(grad_rows, down_matrix, (((1,), (1,)), ((), ())), preferr...  9.4 us
    dot_general x1, matrix products, expert_rows(): up_pre = jnp.dot(input_rows, up_matrix, preferred_element_type=jnp.float32)  7.76 us
  transfers between devices with their start and end apart: 3, of which 2 were waited for; matrix products, arithmetic and copies ran while one was open for 2% of the time, Pallas kernels for 0%

commit v1 on v0

--- a/solution.py
+++ b/solution.py
@@ -43,42 +43,68 @@
     token_count, top_count = chosen.shape
     model_width = grad_tokens.shape[1]
     capacity = min(token_count, 7 * token_count * top_count // (6 * peer_count))
-    rows = peer_count * capacity
+    chunk = -(-(capacity + 1) // 16) * 8
+    rows = peer_count * chunk
 
     flat_ids = chosen.reshape(-1)
     one_hot = (flat_ids[:, None] == jnp.arange(peer_count, dtype=jnp.int32)[None, :]).astype(
         jnp.int32
     )
-    places = jnp.sum(one_hot * jnp.cumsum(one_hot, axis=0), axis=1) - 1
-    target = (flat_ids * capacity + places).reshape(token_count, top_count)
+    places = (jnp.sum(one_hot * jnp.cumsum(one_hot, axis=0), axis=1) - 1).reshape(
+        token_count, top_count
+    )
+    ids = chosen
+    lanes = jnp.arange(rows, dtype=jnp.int32)[None, None, :]
+    both = jnp.concatenate([grad_tokens, input_tokens], axis=1)
+    gate_row = chunk - 1
 
-    hits = target[:, :, None] == jnp.arange(rows, dtype=jnp.int32)[None, None, :]
-    pick = jnp.any(hits, axis=1).astype(jnp.bfloat16)
-    both = jnp.concatenate([grad_tokens, input_tokens], axis=1)
-    send = lax.dot_general(
-        pick, both, (((0,), (0,)), ((), ())), preferred_element_type=jnp.float32
-    ).astype(jnp.bfloat16)
-    send = send.reshape(peer_count, capacity, 2 * model_width)
-    arrived = lax.all_to_all(send, "expert", 0, 0, tiled=True)
-    arrived = arrived.reshape(rows, 2 * model_width)
-    back, gate_value = expert_rows(
-        arrived[:, :model_width], arrived[:, model_width:], gate_matrix, up_matrix, down_matrix
+    def dispatch(part):
+        local = places - part * chunk
+        inside = (local >= 0) & (local < chunk)
+        target = jnp.where(inside, ids * chunk + local, -1)
+        hits = target[:, :, None] == lanes
+        pick = jnp.any(hits, axis=1).astype(jnp.bfloat16)
+        send = lax.dot_general(
+            pick, both, (((0,), (0,)), ((), ())), preferred_element_type=jnp.float32
+        ).astype(jnp.bfloat16)
+        weights = jnp.sum(jnp.where(hits, slot_probs[:, :, None], 0.0), axis=1)
+        return send.reshape(peer_count, chunk, 2 * model_width), weights
+
+    send_a, weights_a = dispatch(0)
+    send_b, weights_b = dispatch(1)
+    arrived_a = lax.all_to_all(send_a, "expert", 0, 0, tiled=True).reshape(rows, 2 * model_width)
+    arrived_b = lax.all_to_all(send_b, "expert", 0, 0, tiled=True).reshape(rows, 2 * model_width)
+    back_a, gate_a = expert_rows(
+        arrived_a[:, :model_width], arrived_a[:, model_width:], gate_matrix, up_matrix, down_matrix
     )
-    returned = lax.all_to_all(
-        back.reshape(peer_count, capacity, model_width), "expert", 0, 0, tiled=True
+    returned_a = lax.all_to_all(
+        back_a.reshape(peer_count, chunk, model_width), "expert", 0, 0, tiled=True
     ).reshape(rows, model_width)
-    gate_back = lax.all_to_all(
-        gate_value.reshape(peer_count, capacity), "expert", 0, 0, tiled=True
-    ).reshape(rows)
+    back_b, gate_b = expert_rows(
+        arrived_b[:, :model_width], arrived_b[:, model_width:], gate_matrix, up_matrix, down_matrix
+    )
+    gates = jnp.concatenate(
+        [gate_a.reshape(peer_count, chunk), gate_b.reshape(peer_count, chunk)], axis=1
+    )
+    gates = jnp.pad(gates, ((0, 0), (0, model_width - 2 * chunk)))
+    back_b = jnp.concatenate(
+        [back_b.reshape(peer_count, chunk, model_width)[:, :gate_row], gates[:, None, :]], axis=1
+    )
+    returned_b = lax.all_to_all(back_b, "expert", 0, 0, tiled=True)
+    gate_table = returned_b[:, gate_row, : 2 * chunk].reshape(-1)
+    returned_b = returned_b.reshape(rows, model_width)
 
-    weights = jnp.sum(jnp.where(hits, slot_probs[:, :, None], 0.0), axis=1)
-    combined = grad_tokens.astype(jnp.float32) + jnp.dot(
-        weights,
-        returned.astype(jnp.float32),
-        precision=lax.Precision.HIGHEST,
-        preferred_element_type=jnp.float32,
-    )
-    gate_slot = gate_back[target.reshape(-1)].reshape(token_count, top_count)
+    def weighted(weights, returned):
+        return jnp.dot(
+            weights,
+            returned.astype(jnp.float32),
+            precision=lax.Precision.HIGHEST,
+            preferred_element_type=jnp.float32,
+        )
+
+    combined = grad_tokens.astype(jnp.float32) + weighted(weights_a, returned_a)
+    combined = combined + weighted(weights_b, returned_b)
+    gate_slot = gate_table[(ids * 2 * chunk + places).reshape(-1)].reshape(token_count, top_count)
     passed = passed_along(combined.astype(jnp.bfloat16), "pipe", -1)
     return (passed[None], gate_slot[None])
 

time: 323 us -> 280 us (0.87)
  blocking collectives: 127 us -> 0 us
  waiting for transfers between devices: 72.8 us -> 175 us
  local copies, waits for them, and re-layouts: 49.8 us -> 12 us
  starting transfers between devices: 10.1 us -> 23.2 us
  matrix products: 56.7 us -> 62.8 us
    all_to_all x1 -> x0, blocking collectives: 127 us -> none  [body(): arrived = lax.all_to_all(send, 'expert', 0, 0, tiled=True)]
    all_to_all x2 -> x4, waiting for transfers between devices: 72.8 us -> 166 us  [the longest x1 61.6 us: body(): lax.all_to_all(send_a, 'expert', 0, 0, tiled=True)]
    reshape x5 -> x0, local copies, waits for them, and re-layouts: 40.7 us -> none  [the longest x1 13.2 us: body(): arrived = arrived.reshape(rows, 2 * model_width)]
    all_to_all x2 -> x4, starting transfers between devices: 8.82 us -> 21.9 us  [the longest x1 8.56 us: body(): lax.all_to_all(send_a, 'expert', 0, 0, tiled=True)]
    ppermute x1, waiting for transfers between devices: 0.01 us -> 9.01 us  [passed_along(): lax.ppermute(value, axis, [(source, source + steps) for source in range(f...]
    dot_general x1 -> x2, matrix products: 5.93 us -> 10.6 us  [expert_rows(): jnp.dot(input_rows, gate_matrix, preferred_element_type=jnp.float32)]
    dot_general x1 -> x2, matrix products: 10.5 us -> 6 us  [expert_rows(): lax.dot_general(up_part, up_matrix, (((1,), (1,)), ((), ())), preferred_e...]
    dot_general x1 -> x2, matrix products: 7.76 us -> 11.3 us  [expert_rows(): up_pre = jnp.dot(input_rows, up_matrix, preferred_element_type=jnp.float32)]
  transfers between devices with their start and end apart: 3 -> 5, of which waited for: 2 -> 5; matrix products, arithmetic and copies ran while one was open for 2% -> 16% of each run, Pallas kernels for 0% -> 0%
where the time goes in v1:
time: 280 us; the launch traced here: 279 us
  waiting for transfers between devices  175 us (62%)
  matrix products  62.8 us (22%)
  starting transfers between devices  23.2 us (8%)
  local copies, waits for them, and re-layouts  12 us (4%)
  other arithmetic  5.33 us (2%)
    all_to_all x1, waiting for transfers between devices, body(): lax.all_to_all(send_a, 'expert', 0, 0, tiled=True)  61.6 us
    all_to_all x1, waiting for transfers between devices, body(): lax.all_to_all(send_b, 'expert', 0, 0, tiled=True)  55.3 us
    all_to_all x1, waiting for transfers between devices, body(): returned_b = lax.all_to_all(back_b, 'expert', 0, 0, tiled=True)  31.6 us
    all_to_all x1, waiting for transfers between devices, body(): lax.all_to_all(back_a.reshape(peer_count, chunk, model_width), 'expert',...  17.4 us
    dot_general x2, matrix products, expert_rows(): lax.dot_general(grad_rows, down_matrix, (((1,), (1,)), ((), ())), preferr...  11.6 us
    dot_general x2, matrix products, expert_rows(): up_pre = jnp.dot(input_rows, up_matrix, preferred_element_type=jnp.float32)  11.3 us
    dot_general x2, matrix products, expert_rows(): jnp.dot(input_rows, gate_matrix, preferred_element_type=jnp.float32)  10.6 us
    dot_general x2, matrix products, expert_rows(): lax.dot_general(gate_part, gate_matrix, (((1,), (1,)), ((), ())), preferr...  9.02 us
  transfers between devices with their start and end apart: 5, of which 5 were waited for; matrix products, arithmetic and copies ran while one was open for 16% of the time, Pallas kernels for 0%

profile of v1, /device:TPU:0, one launch (start us, length us, event | category | flops | bytes accessed | tf_op | source)
XLA Modules:
  0.0 279.2 jit_solution(7852684278306788572)
XLA Ops:
  0.6 0.0 copy-start.2
  0.6 0.0 copy-start.1
  0.6 0.9 copy.28
  1.5 0.1 eq.51
  1.7 0.1 eq.55
  1.8 1.7 reduce-window.6
  3.6 0.3 slice_reduce_fusion
  3.9 0.1 fusion.36
  4.0 0.1 sub.22
  4.1 0.1 sub.26
  4.3 0.1 copy.32
  4.4 0.3 fusion.26
  4.6 0.0 copy-done.2
  4.7 0.0 copy-done.1
  4.7 3.9 %convolution_convert_fusion.1 = bf16[512,5120]{1,0:T(8,128)(2,1)} fusion(pred[128,512]{1,0:T(8,128)(4,1)S(1)} %fusion.26, bf16[128,2560]{1,0:T(8,128)(2,1)S(1)} %bitcast.80, bf16[128,2560]{1,0:T(8,128)(2,1)S(1)} %bitcast.78), kind=kOutput, calls=%fused_computation.2 | convolution fusion | flops 676331520 | bytes 6619136 | tf_op jit(solution)/shard_map/dot_general | solution.py:67
  8.6 8.6 %all-to-all-start = ((bf16[32,16,5120]{2,1,0:T(8,128)(2,1)}), bf16[32,16,5120]{2,1,0:T(8,128)(2,1)}, u32[]{:S(2)}, u32[]{:S(2)}) async-start(bf16[32,16,5120]{2,1,0:T(8,128)(2,1)} %bitcast.75), calls=%async_computation | async-start | bytes 10485760 | tf_op jit(solution)/shard_map/all_to_all | solution.py:75
  17.1 0.1 copy.33
  17.2 0.3 fusion.25
  17.5 3.9 %convolution_convert_fusion = bf16[512,5120]{1,0:T(8,128)(2,1)} fusion(pred[128,512]{1,0:T(8,128)(4,1)S(1)} %fusion.25, bf16[128,2560]{1,0:T(8,128)(2,1)S(1)} %bitcast.81, bf16[128,2560]{1,0:T(8,128)(2,1)S(1)} %bitcast.79), kind=kOutput, calls=%fused_computation.1 | convolution fusion | flops 676331520 | bytes 6619136 | tf_op jit(solution)/shard_map/dot_general | solution.py:67
  21.4 61.6 %all-to-all-done = bf16[32,16,5120]{2,1,0:T(8,128)(2,1)} async-done(((bf16[32,16,5120]{2,1,0:T(8,128)(2,1)}), bf16[32,16,5120]{2,1,0:T(8,128)(2,1)}, u32[]{:S(2)}, u32[]{:S(2)}) %all-to-all-start) | async-done | bytes 5242912 | tf_op jit(solution)/shard_map/all_to_all | solution.py:75
  83.0 5.0 %all-to-all-start.2 = ((bf16[32,16,5120]{2,1,0:T(8,128)(2,1)}), bf16[32,16,5120]{2,1,0:T(8,128)(2,1)}, u32[]{:S(2)}, u32[]{:S(2)}) async-start(bf16[32,16,5120]{2,1,0:T(8,128)(2,1)} %bitcast.74), calls=%async_computation.2 | async-start | bytes 10485760 | tf_op jit(solution)/shard_map/all_to_all | solution.py:76
  88.1 0.0 copy-start.5
  88.1 5.2 %fusion.6 = f32[512,768]{1,0:T(8,128)S(1)} fusion(bf16[1,1,2560,768]{3,2,1,0:T(8,128)(2,1)} %param.11, bf16[512,5120]{1,0:T(8,128)(2,1)} %bitcast.5), kind=kOutput, calls=%fused_computation.11 | convolution fusion | flops 2013265920 | bytes 8126464 | tf_op jit(solution)/shard_map/dot_general | solution.py:14
  93.3 0.0 copy-done.5
  93.3 5.1 %fusion.16 = f32[512,768]{1,0:T(8,128)} fusion(bf16[1,1,768,2560]{3,2,1,0:T(8,128)(2,1)S(1)} %copy-done.5, bf16[512,5120]{1,0:T(8,128)(2,1)} %bitcast.5), kind=kOutput, calls=%fused_computation.21 | convolution fusion | flops 2013265920 | bytes 8126464 | tf_op jit(solution)/shard_map/dot_general | solution.py:16
  98.5 55.3 %all-to-all-done.2 = bf16[32,16,5120]{2,1,0:T(8,128)(2,1)} async-done(((bf16[32,16,5120]{2,1,0:T(8,128)(2,1)}), bf16[32,16,5120]{2,1,0:T(8,128)(2,1)}, u32[]{:S(2)}, u32[]{:S(2)}) %all-to-all-start.2) | async-done | bytes 5242912 | tf_op jit(solution)/shard_map/all_to_all | solution.py:76
  153.8 6.4 %fusion.14 = f32[512,768]{1,0:T(8,128)} fusion(bf16[1,1,768,2560]{3,2,1,0:T(8,128)(2,1)} %param.13, bf16[512,5120]{1,0:T(8,128)(2,1)} %bitcast.12), kind=kOutput, calls=%fused_computation.19 | convolution fusion | flops 2013265920 | bytes 8126464 | tf_op jit(solution)/shard_map/dot_general | solution.py:16
  160.2 0.0 copy-done.6
  160.2 5.3 %fusion.2 = f32[512,768]{1,0:T(8,128)} fusion(bf16[1,1,2560,768]{3,2,1,0:T(8,128)(2,1)S(1)} %copy-done.6, bf16[512,5120]{1,0:T(8,128)(2,1)} %bitcast.12), kind=kOutput, calls=%fused_computation.7 | convolution fusion | flops 2013265920 | bytes 8126464 | tf_op jit(solution)/shard_map/dot_general | solution.py:14
  165.5 0.0 copy-done.7
  165.5 0.0 copy-done.11
  165.5 4.1 %multiply_reduce_fusion.1 = (bf16[512]{0:T(512)(128)(2,1)S(1)}, f32[512,768]{1,0:T(8,128)S(1)}) fusion(f32[512,768]{1,0:T(8,128)S(1)} %copy-done.11, f32[512,768]{1,0:T(8,128)S(1)} %fusion.6, bf16[1,1,2560,768]{3,2,1,0:T(8,128)(2,1)S(1)} %copy-done.7, bf16[512,5120]{1,0:T(8,128)(2,1)} %bitcast.5), kind=kOutput, calls=%fused_computation.34 | convolution fusion | flops 2016017920 | bytes 11273216 | tf_op jit(solution)/shard_map/dot_general | solution.py:15
  169.7 2.7 fusion.4
  172.4 3.8 %add_convert_fusion.1 = bf16[512,2560]{1,0:T(8,128)(2,1)} fusion(f32[512,2560]{1,0:T(8,128)S(1)} %fusion.4, bf16[1,1,2560,768]{3,2,1,0:T(8,128)(2,1)S(1)} %copy-done.7, f32[512,768]{1,0:T(8,128)S(1)} %copy-done.11, f32[512,768]{1,0:T(8,128)S(1)} %fusion.6), kind=kOutput, calls=%fused_computation.4 | convolution fusion | flops 2018246656 | bytes 14942208 | tf_op jit(solution)/shard_map/dot_general | solution.py:28
  176.1 4.3 %all-to-all-start.1 = ((bf16[32,16,2560]{2,1,0:T(8,128)(2,1)}), bf16[32,16,2560]{2,1,0:T(8,128)(2,1)S(1)}, u32[]{:S(2)}, u32[]{:S(2)}) async-start(bf16[32,16,2560]{2,1,0:T(8,128)(2,1)} %bitcast.82), calls=%async_computation.1 | async-start | bytes 5242880 | tf_op jit(solution)/shard_map/all_to_all | solution.py:80
  180.4 7.2 %multiply_reduce_fusion = (bf16[512]{0:T(512)(128)(2,1)S(1)}, f32[512,768]{1,0:T(8,128)}) fusion(f32[512,768]{1,0:T(8,128)} %fusion.14, f32[512,768]{1,0:T(8,128)} %fusion.2, bf16[1,1,2560,768]{3,2,1,0:T(8,128)(2,1)} %param.12, bf16[512,5120]{1,0:T(8,128)(2,1)} %bitcast.12), kind=kOutput, calls=%fused_computation.33 | convolution fusion | flops 2016017920 | bytes 11273216 | tf_op jit(solution)/shard_map/dot_general | solution.py:15
  187.6 0.1 convert_element_type.68
  187.7 0.1 convert_element_type.66
  187.8 0.1 fusion.34
  187.8 0.3 copy.34
  188.1 0.0 copy-start.8
  188.1 6.3 %fusion = f32[512,2560]{1,0:T(8,128)S(1)} fusion(bf16[1,1,2560,768]{3,2,1,0:T(8,128)(2,1)} %param.11, f32[512,768]{1,0:T(8,128)} %fusion.2, f32[512,768]{1,0:T(8,128)} %fusion.14, f32[512,768]{1,0:T(8,128)} %get-tuple-element.15), kind=kOutput, calls=%fused_computation.5 | convolution fusion | flops 2017198080 | bytes 13893632 | tf_op jit(solution)/shard_map/dot_general | solution.py:26
  194.5 0.0 copy-done.8
  194.5 0.0 copy-done.9
  194.5 0.0 copy-done.10
  194.5 2.2 add_convert_fusion
  196.8 2.2 pad_maximum_fusion
  199.0 17.4 %all-to-all-done.1 = bf16[32,16,2560]{2,1,0:T(8,128)(2,1)S(1)} async-done(((bf16[32,16,2560]{2,1,0:T(8,128)(2,1)}), bf16[32,16,2560]{2,1,0:T(8,128)(2,1)S(1)}, u32[]{:S(2)}, u32[]{:S(2)}) %all-to-all-start.1) | async-done | bytes 2621472 | tf_op jit(solution)/shard_map/all_to_all | solution.py:80
  216.4 1.5 copy-done
  217.9 4.1 %all-to-all-start.3 = ((bf16[32,16,2560]{2,1,0:T(8,128)(2,1)}), bf16[32,16,2560]{2,1,0:T(8,128)(2,1)S(1)}, u32[]{:S(2)}, u32[]{:S(2)}) async-start(bf16[32,16,2560]{2,1,0:T(8,128)(2,1)} %pad_maximum_fusion), calls=%async_computation.3 | async-start | bytes 5242880 | tf_op jit(solution)/shard_map/all_to_all | solution.py:93
  222.0 0.5 select_reduce_fusion
  222.5 4.0 %convolution_add_fusion.1 = f32[128,2560]{1,0:T(8,128)} fusion(f32[128,512]{1,0:T(8,128)S(1)} %get-tuple-element.9, bf16[512,2560]{1,0:T(8,128)(2,1)} %bitcast.77, bf16[1,128,2560]{2,1,0:T(8,128)(2,1)S(1)} %copy-done.1), kind=kOutput, calls=%fused_computation.24 | convolution fusion | flops 2013921280 | bytes 4849664 | tf_op jit(solution)/shard_map/dot_general | solution.py:98
  226.5 31.6 %all-to-all-done.3 = bf16[32,16,2560]{2,1,0:T(8,128)(2,1)S(1)} async-done(((bf16[32,16,2560]{2,1,0:T(8,128)(2,1)}), bf16[32,16,2560]{2,1,0:T(8,128)(2,1)S(1)}, u32[]{:S(2)}, u32[]{:S(2)}) %all-to-all-start.3) | async-done | bytes 2621472 | tf_op jit(solution)/shard_map/all_to_all | solution.py:93
  258.1 2.5 fusion.18
  260.7 1.3 collective-permute-start
  262.0 0.1 copy.35
  262.1 0.1 mul.98
  262.3 0.1 slice_reduce_fusion.1
  262.3 0.1 reshape_squeeze.3
  262.4 5.0 %gather_fusion = bf16[768]{0:T(1024)(128)(2,1)S(1)} fusion(bf16[1024]{0:T(1024)(128)(2,1)S(1)} %reshape_squeeze.3, s32[1024]{0:T(1024)S(1)} %pad_clamp_fusion), kind=kCustom, calls=%fused_computation | custom fusion | bytes 6144 | tf_op jit(solution)/shard_map/gather | solution.py:107
  267.4 0.1 broadcast_in_dim_reshape.3
  267.6 0.7 copy.36
  268.3 9.0 %collective-permute-done = bf16[128,2560]{1,0:T(8,128)(2,1)} collective-permute-done((bf16[128,2560]{1,0:T(8,128)(2,1)S(1)}, bf16[128,2560]{1,0:T(8,128)(2,1)}, u32[]{:S(2)}, u32[]{:S(2)}) %collective-permute-start) | collective-permute-done | bytes 655392 | tf_op jit(solution)/shard_map/ppermute | solution.py:10
  277.3 2.0 copy.43
  (18 shorter events, 0.1 us)
Async XLA Ops:
  0.6 4.0 %copy-start.2 = (bf16[1,128,2560]{2,1,0:T(8,128)(2,1)S(1)}, bf16[1,128,2560]{2,1,0:T(8,128)(2,1)}, u32[]{:S(2)}) copy-start(bf16[1,128,2560]{2,1,0:T(8,128)(2,1)} %param.8) | copy-start | bytes 1966084
  0.6 4.0 %copy-start.1 = (bf16[1,128,2560]{2,1,0:T(8,128)(2,1)S(1)}, bf16[1,128,2560]{2,1,0:T(8,128)(2,1)}, u32[]{:S(2)}) copy-start(bf16[1,128,2560]{2,1,0:T(8,128)(2,1)} %param.7) | copy-start | bytes 1966084
  8.6 74.4 %all-to-all-start = ((bf16[32,16,5120]{2,1,0:T(8,128)(2,1)}), bf16[32,16,5120]{2,1,0:T(8,128)(2,1)}, u32[]{:S(2)}, u32[]{:S(2)}) async-start(bf16[32,16,5120]{2,1,0:T(8,128)(2,1)} %bitcast.75), calls=%async_computation | async-start | bytes 10485760 | tf_op jit(solution)/shard_map/all_to_all | solution.py:75
  83.0 70.7 %all-to-all-start.2 = ((bf16[32,16,5120]{2,1,0:T(8,128)(2,1)}), bf16[32,16,5120]{2,1,0:T(8,128)(2,1)}, u32[]{:S(2)}, u32[]{:S(2)}) async-start(bf16[32,16,5120]{2,1,0:T(8,128)(2,1)} %bitcast.74), calls=%async_computation.2 | async-start | bytes 10485760 | tf_op jit(solution)/shard_map/all_to_all | solution.py:76
  88.1 5.3 %copy-start.5 = (bf16[1,1,768,2560]{3,2,1,0:T(8,128)(2,1)S(1)}, bf16[1,1,768,2560]{3,2,1,0:T(8,128)(2,1)}, u32[]{:S(2)}) copy-start(bf16[1,1,768,2560]{3,2,1,0:T(8,128)(2,1)} %param.13) | copy-start | bytes 11796484
  153.8 6.4 %copy-start.6 = (bf16[1,1,2560,768]{3,2,1,0:T(8,128)(2,1)S(1)}, bf16[1,1,2560,768]{3,2,1,0:T(8,128)(2,1)}, u32[]{:S(2)}) copy-start(bf16[1,1,2560,768]{3,2,1,0:T(8,128)(2,1)} %param.11) | copy-start | bytes 11796484
  160.2 5.3 %copy-start.7 = (bf16[1,1,2560,768]{3,2,1,0:T(8,128)(2,1)S(1)}, bf16[1,1,2560,768]{3,2,1,0:T(8,128)(2,1)}, u32[]{:S(2)}) copy-start(bf16[1,1,2560,768]{3,2,1,0:T(8,128)(2,1)} %param.12) | copy-start | bytes 11796484
  160.2 5.3 %copy-start.11 = (f32[512,768]{1,0:T(8,128)S(1)}, f32[512,768]{1,0:T(8,128)}, u32[]{:S(2)}) copy-start(f32[512,768]{1,0:T(8,128)} %fusion.16) | copy-start | bytes 4718596
  176.1 40.2 %all-to-all-start.1 = ((bf16[32,16,2560]{2,1,0:T(8,128)(2,1)}), bf16[32,16,2560]{2,1,0:T(8,128)(2,1)S(1)}, u32[]{:S(2)}, u32[]{:S(2)}) async-start(bf16[32,16,2560]{2,1,0:T(8,128)(2,1)} %bitcast.82), calls=%async_computation.1 | async-start | bytes 5242880 | tf_op jit(solution)/shard_map/all_to_all | solution.py:80
  188.1 6.4 %copy-start.8 = (bf16[1,1,2560,768]{3,2,1,0:T(8,128)(2,1)S(1)}, bf16[1,1,2560,768]{3,2,1,0:T(8,128)(2,1)}, u32[]{:S(2)}) copy-start(bf16[1,1,2560,768]{3,2,1,0:T(8,128)(2,1)} %param.12) | copy-start | bytes 11796484
  188.1 6.4 %copy-start.9 = (f32[512,768]{1,0:T(8,128)S(1)}, f32[512,768]{1,0:T(8,128)}, u32[]{:S(2)}) copy-start(f32[512,768]{1,0:T(8,128)} %fusion.14) | copy-start | bytes 4718596
  188.1 6.4 %copy-start.10 = (f32[512,768]{1,0:T(8,128)S(1)}, f32[512,768]{1,0:T(8,128)}, u32[]{:S(2)}) copy-start(f32[512,768]{1,0:T(8,128)} %fusion.2) | copy-start | bytes 4718596
  199.0 23.0 %copy-start.4 = (f32[1,128,6]{1,0,2:T(1,128)S(1)}, f32[1,128,6]{1,0,2:T(1,128)}, u32[]{:S(2)}) copy-start(f32[1,128,6]{1,0,2:T(1,128)} %param.10) | copy-start | bytes 9220
  216.4 1.5 copy-start
  217.9 40.2 %all-to-all-start.3 = ((bf16[32,16,2560]{2,1,0:T(8,128)(2,1)}), bf16[32,16,2560]{2,1,0:T(8,128)(2,1)S(1)}, u32[]{:S(2)}, u32[]{:S(2)}) async-start(bf16[32,16,2560]{2,1,0:T(8,128)(2,1)} %pad_maximum_fusion), calls=%async_computation.3 | async-start | bytes 5242880 | tf_op jit(solution)/shard_map/all_to_all | solution.py:93
  258.1 3.8 %copy-start.3 = (s32[1,128,6]{1,0,2:T(1,128)S(1)}, s32[1,128,6]{1,0,2:T(1,128)}, u32[]{:S(2)}) copy-start(s32[1,128,6]{1,0,2:T(1,128)} %param.9) | copy-start | bytes 9220
  260.7 16.6 %collective-permute-start = (bf16[128,2560]{1,0:T(8,128)(2,1)S(1)}, bf16[128,2560]{1,0:T(8,128)(2,1)}, u32[]{:S(2)}, u32[]{:S(2)}) collective-permute-start(bf16[128,2560]{1,0:T(8,128)(2,1)S(1)} %fusion.18), channel_id=1, source_target_pairs={{32,0},{64,32},{96,64},{33,1},{65,33},{97,65},{34,2},{66,34},{98,6... | collective-permute-start | bytes 1966088 | tf_op jit(solution)/shard_map/ppermute | solution.py:10

commit v2 on v1

--- a/solution.py
+++ b/solution.py
@@ -77,6 +77,7 @@
     back_a, gate_a = expert_rows(
         arrived_a[:, :model_width], arrived_a[:, model_width:], gate_matrix, up_matrix, down_matrix
     )
+    back_a, gate_a, arrived_b = lax.optimization_barrier((back_a, gate_a, arrived_b))
     returned_a = lax.all_to_all(
         back_a.reshape(peer_count, chunk, model_width), "expert", 0, 0, tiled=True
     ).reshape(rows, model_width)
@@ -104,7 +105,11 @@
 
     combined = grad_tokens.astype(jnp.float32) + weighted(weights_a, returned_a)
     combined = combined + weighted(weights_b, returned_b)
-    gate_slot = gate_table[(ids * 2 * chunk + places).reshape(-1)].reshape(token_count, top_count)
+    gate_index = ids * 2 * chunk + places
+    gate_hits = gate_index[:, :, None] == jnp.arange(gate_table.shape[0], dtype=jnp.int32)
+    gate_slot = jnp.sum(
+        jnp.where(gate_hits, gate_table.astype(jnp.float32), 0.0), axis=2
+    ).astype(jnp.bfloat16)
     passed = passed_along(combined.astype(jnp.bfloat16), "pipe", -1)
     return (passed[None], gate_slot[None])
 

time: 280 us -> 270 us (0.964)
  waiting for transfers between devices: 175 us -> 169 us
  local copies, waits for them, and re-layouts: 12 us -> 6.74 us
    all_to_all x1, waiting for transfers between devices: 55.3 us -> 45.5 us  [body(): lax.all_to_all(send_b, 'expert', 0, 0, tiled=True)]
    gather x1 -> x0, local copies, waits for them, and re-layouts: 4.99 us -> none  [body(): gate_table[(ids * 2 * chunk + places).reshape(-1)]]
    ppermute x1, waiting for transfers between devices: 9.01 us -> 13.1 us  [passed_along(): lax.ppermute(value, axis, [(source, source + steps) for source in range(f...]
  transfers between devices with their start and end apart: 5 -> 5, of which waited for: 5 -> 5; matrix products, arithmetic and copies ran while one was open for 16% -> 18% of each run, Pallas kernels for 0% -> 0%
where the time goes in v2:
time: 270 us; the launch traced here: 269 us
  waiting for transfers between devices  169 us (63%)
  matrix products  61.8 us (23%)
  starting transfers between devices  23.2 us (9%)
  other arithmetic  7.08 us (3%)
  local copies, waits for them, and re-layouts  6.74 us (2%)
    all_to_all x1, waiting for transfers between devices, body(): lax.all_to_all(send_a, 'expert', 0, 0, tiled=True)  61.6 us
    all_to_all x1, waiting for transfers between devices, body(): lax.all_to_all(send_b, 'expert', 0, 0, tiled=True)  45.5 us
    all_to_all x1, waiting for transfers between devices, body(): returned_b = lax.all_to_all(back_b, 'expert', 0, 0, tiled=True)  31.6 us
    all_to_all x1, waiting for transfers between devices, body(): lax.all_to_all(back_a.reshape(peer_count, chunk, model_width), 'expert',...  17.3 us
    ppermute x1, waiting for transfers between devices, passed_along(): lax.ppermute(value, axis, [(source, source + steps) for source in range(f...  13.1 us
    dot_general x2, matrix products, expert_rows(): up_pre = jnp.dot(input_rows, up_matrix, preferred_element_type=jnp.float32)  11.6 us
    dot_general x2, matrix products, expert_rows(): lax.dot_general(grad_rows, down_matrix, (((1,), (1,)), ((), ())), preferr...  10.6 us
    dot_general x2, matrix products, expert_rows(): jnp.dot(input_rows, gate_matrix, preferred_element_type=jnp.float32)  10.3 us
  transfers between devices with their start and end apart: 5, of which 5 were waited for; matrix products, arithmetic and copies ran while one was open for 18% of the time, Pallas kernels for 0%

profile of v2, /device:TPU:0, one launch (start us, length us, event | category | flops | bytes accessed | tf_op | source)
XLA Modules:
  0.0 269.0 jit_solution(3784469545812159849)
XLA Ops:
  0.6 0.0 copy-start.2
  0.6 0.0 copy-start.1
  0.6 0.9 copy.21
  1.5 0.1 eq.64
  1.7 0.1 eq.68
  1.8 1.7 reduce-window.6
  3.6 0.3 slice_reduce_fusion
  3.9 0.1 fusion.36
  4.0 0.1 sub.20
  4.1 0.1 sub.24
  4.3 0.7 bitcast_add_fusion
  4.9 0.1 copy.25
  5.0 0.3 fusion.26
  5.3 0.0 copy-done.2
  5.3 0.0 copy-done.1
  5.3 3.9 %convolution_convert_fusion.1 = bf16[512,5120]{1,0:T(8,128)(2,1)} fusion(pred[128,512]{1,0:T(8,128)(4,1)S(1)} %fusion.26, bf16[128,2560]{1,0:T(8,128)(2,1)S(1)} %bitcast.85, bf16[128,2560]{1,0:T(8,128)(2,1)S(1)} %bitcast.83), kind=kOutput, calls=%fused_computation.1 | convolution fusion | flops 676331520 | bytes 6619136 | tf_op jit(solution)/shard_map/dot_general | solution.py:67
  9.2 8.6 %all-to-all-start = ((bf16[32,16,5120]{2,1,0:T(8,128)(2,1)}), bf16[32,16,5120]{2,1,0:T(8,128)(2,1)}, u32[]{:S(2)}, u32[]{:S(2)}) async-start(bf16[32,16,5120]{2,1,0:T(8,128)(2,1)} %bitcast.80), calls=%async_computation | async-start | bytes 10485760 | tf_op jit(solution)/shard_map/all_to_all | solution.py:75
  17.7 0.1 copy.26
  17.8 0.3 fusion.25
  18.1 3.9 %convolution_convert_fusion = bf16[512,5120]{1,0:T(8,128)(2,1)} fusion(pred[128,512]{1,0:T(8,128)(4,1)S(1)} %fusion.25, bf16[128,2560]{1,0:T(8,128)(2,1)S(1)} %bitcast.86, bf16[128,2560]{1,0:T(8,128)(2,1)S(1)} %bitcast.84), kind=kOutput, calls=%fused_computation | convolution fusion | flops 676331520 | bytes 6619136 | tf_op jit(solution)/shard_map/dot_general | solution.py:67
  22.0 61.6 %all-to-all-done = bf16[32,16,5120]{2,1,0:T(8,128)(2,1)} async-done(((bf16[32,16,5120]{2,1,0:T(8,128)(2,1)}), bf16[32,16,5120]{2,1,0:T(8,128)(2,1)}, u32[]{:S(2)}, u32[]{:S(2)}) %all-to-all-start) | async-done | bytes 5242912 | tf_op jit(solution)/shard_map/all_to_all | solution.py:75
  83.6 5.0 %all-to-all-start.1 = ((bf16[32,16,5120]{2,1,0:T(8,128)(2,1)}), bf16[32,16,5120]{2,1,0:T(8,128)(2,1)}, u32[]{:S(2)}, u32[]{:S(2)}) async-start(bf16[32,16,5120]{2,1,0:T(8,128)(2,1)} %bitcast.79), calls=%async_computation.1 | async-start | bytes 10485760 | tf_op jit(solution)/shard_map/all_to_all | solution.py:76
  88.7 0.0 copy-start.4
  88.7 5.2 %fusion.6 = f32[512,768]{1,0:T(8,128)S(1)} fusion(bf16[1,1,2560,768]{3,2,1,0:T(8,128)(2,1)} %param.11, bf16[512,5120]{1,0:T(8,128)(2,1)} %bitcast.5), kind=kOutput, calls=%fused_computation.10 | convolution fusion | flops 2013265920 | bytes 8126464 | tf_op jit(solution)/shard_map/dot_general | solution.py:14
  93.9 0.0 copy-done.4
  93.9 0.0 copy-start.7
  93.9 4.1 %fusion.16 = f32[512,768]{1,0:T(8,128)S(1)} fusion(bf16[1,1,768,2560]{3,2,1,0:T(8,128)(2,1)S(1)} %copy-done.4, bf16[512,5120]{1,0:T(8,128)(2,1)} %bitcast.5), kind=kOutput, calls=%fused_computation.20 | convolution fusion | flops 2013265920 | bytes 8126464 | tf_op jit(solution)/shard_map/dot_general | solution.py:16
  98.1 0.0 copy-done.7
  98.1 0.0 copy-start.5
  98.1 4.3 %multiply_reduce_fusion.1 = (bf16[512]{0:T(512)(128)(2,1)S(1)}, f32[512,768]{1,0:T(8,128)S(1)}) fusion(f32[512,768]{1,0:T(8,128)S(1)} %fusion.16, f32[512,768]{1,0:T(8,128)S(1)} %fusion.6, bf16[1,1,2560,768]{3,2,1,0:T(8,128)(2,1)S(1)} %copy-done.7, bf16[512,5120]{1,0:T(8,128)(2,1)} %bitcast.5), kind=kOutput, calls=%fused_computation.41 | convolution fusion | flops 2016017920 | bytes 11273216 | tf_op jit(solution)/shard_map/dot_general | solution.py:15
  102.4 0.0 copy-done.5
  102.4 2.7 fusion.4
  105.1 3.8 %add_convert_fusion.1 = bf16[512,2560]{1,0:T(8,128)(2,1)} fusion(f32[512,2560]{1,0:T(8,128)S(1)} %fusion.4, bf16[1,1,2560,768]{3,2,1,0:T(8,128)(2,1)S(1)} %copy-done.7, f32[512,768]{1,0:T(8,128)S(1)} %fusion.16, f32[512,768]{1,0:T(8,128)S(1)} %fusion.6), kind=kOutput, calls=%fused_computation.3 | convolution fusion | flops 2018246656 | bytes 14942208 | tf_op jit(solution)/shard_map/dot_general | solution.py:28
  108.8 45.5 %all-to-all-done.1 = bf16[32,16,5120]{2,1,0:T(8,128)(2,1)} async-done(((bf16[32,16,5120]{2,1,0:T(8,128)(2,1)}), bf16[32,16,5120]{2,1,0:T(8,128)(2,1)}, u32[]{:S(2)}, u32[]{:S(2)}) %all-to-all-start.1) | async-done | bytes 5242912 | tf_op jit(solution)/shard_map/all_to_all | solution.py:76
  154.4 6.5 %fusion.14 = f32[512,768]{1,0:T(8,128)} fusion(bf16[1,1,768,2560]{3,2,1,0:T(8,128)(2,1)} %param.13, bf16[512,5120]{1,0:T(8,128)(2,1)} %bitcast.10), kind=kOutput, calls=%fused_computation.18 | convolution fusion | flops 2013265920 | bytes 8126464 | tf_op jit(solution)/shard_map/dot_general | solution.py:16
  160.8 0.0 copy-done.6
  160.8 5.1 %fusion.2 = f32[512,768]{1,0:T(8,128)} fusion(bf16[1,1,2560,768]{3,2,1,0:T(8,128)(2,1)S(1)} %copy-done.6, bf16[512,5120]{1,0:T(8,128)(2,1)} %bitcast.10), kind=kOutput, calls=%fused_computation.6 | convolution fusion | flops 2013265920 | bytes 8126464 | tf_op jit(solution)/shard_map/dot_general | solution.py:14
  165.9 4.3 %all-to-all-start.2 = ((bf16[32,16,2560]{2,1,0:T(8,128)(2,1)}), bf16[32,16,2560]{2,1,0:T(8,128)(2,1)S(1)}, u32[]{:S(2)}, u32[]{:S(2)}) async-start(bf16[32,16,2560]{2,1,0:T(8,128)(2,1)} %bitcast.87), calls=%async_computation.2 | async-start | bytes 5242880 | tf_op jit(solution)/shard_map/all_to_all | solution.py:81
  170.2 7.3 %multiply_reduce_fusion = (bf16[512]{0:T(512)(128)(2,1)S(1)}, f32[512,768]{1,0:T(8,128)}) fusion(f32[512,768]{1,0:T(8,128)} %fusion.14, f32[512,768]{1,0:T(8,128)} %fusion.2, bf16[1,1,2560,768]{3,2,1,0:T(8,128)(2,1)} %param.12, bf16[512,5120]{1,0:T(8,128)(2,1)} %bitcast.10), kind=kOutput, calls=%fused_computation.34 | convolution fusion | flops 2016017920 | bytes 11273216 | tf_op jit(solution)/shard_map/dot_general | solution.py:15
  177.5 0.1 convert_element_type.82
  177.6 0.1 reshape.117
  177.7 0.1 fusion.34
  177.7 0.3 copy.27
  178.0 0.0 copy-start.8
  178.0 0.0 copy-start.9
  178.0 0.0 copy-start.10
  178.0 6.3 %fusion = f32[512,2560]{1,0:T(8,128)S(1)} fusion(bf16[1,1,2560,768]{3,2,1,0:T(8,128)(2,1)} %param.11, f32[512,768]{1,0:T(8,128)} %fusion.2, f32[512,768]{1,0:T(8,128)} %fusion.14, f32[512,768]{1,0:T(8,128)} %get-tuple-element.18), kind=kOutput, calls=%fused_computation.4 | convolution fusion | flops 2017198080 | bytes 13893632 | tf_op jit(solution)/shard_map/dot_general | solution.py:26
  184.4 2.2 add_convert_fusion
  186.7 2.2 pad_maximum_fusion
  188.8 17.3 %all-to-all-done.2 = bf16[32,16,2560]{2,1,0:T(8,128)(2,1)S(1)} async-done(((bf16[32,16,2560]{2,1,0:T(8,128)(2,1)}), bf16[32,16,2560]{2,1,0:T(8,128)(2,1)S(1)}, u32[]{:S(2)}, u32[]{:S(2)}) %all-to-all-start.2) | async-done | bytes 2621472 | tf_op jit(solution)/shard_map/all_to_all | solution.py:81
  206.2 1.5 copy-done
  207.7 4.1 %all-to-all-start.3 = ((bf16[32,16,2560]{2,1,0:T(8,128)(2,1)}), bf16[32,16,2560]{2,1,0:T(8,128)(2,1)S(1)}, u32[]{:S(2)}, u32[]{:S(2)}) async-start(bf16[32,16,2560]{2,1,0:T(8,128)(2,1)} %pad_maximum_fusion), calls=%async_computation.3 | async-start | bytes 5242880 | tf_op jit(solution)/shard_map/all_to_all | solution.py:94
  211.8 0.0 copy-done.3
  211.8 0.5 select_reduce_fusion.1
  212.3 4.0 %convolution_add_fusion.1 = f32[128,2560]{1,0:T(8,128)} fusion(f32[128,512]{1,0:T(8,128)S(1)} %get-tuple-element.9, bf16[512,2560]{1,0:T(8,128)(2,1)} %bitcast.82, bf16[1,128,2560]{2,1,0:T(8,128)(2,1)S(1)} %copy-done.1), kind=kOutput, calls=%fused_computation.23 | convolution fusion | flops 2013921280 | bytes 4849664 | tf_op jit(solution)/shard_map/dot_general | solution.py:99
  216.3 31.6 %all-to-all-done.3 = bf16[32,16,2560]{2,1,0:T(8,128)(2,1)S(1)} async-done(((bf16[32,16,2560]{2,1,0:T(8,128)(2,1)}), bf16[32,16,2560]{2,1,0:T(8,128)(2,1)S(1)}, u32[]{:S(2)}, u32[]{:S(2)}) %all-to-all-start.3) | async-done | bytes 2621472 | tf_op jit(solution)/shard_map/all_to_all | solution.py:94
  247.9 2.5 fusion.18
  250.5 1.3 collective-permute-start
  251.8 0.9 copy.29
  252.7 0.1 fusion.40
  252.7 0.1 reshape.119
  252.8 1.1 select_reduce_fusion
  253.9 13.1 %collective-permute-done = bf16[128,2560]{1,0:T(8,128)(2,1)} collective-permute-done((bf16[128,2560]{1,0:T(8,128)(2,1)S(1)}, bf16[128,2560]{1,0:T(8,128)(2,1)}, u32[]{:S(2)}, u32[]{:S(2)}) %collective-permute-start) | collective-permute-done | bytes 655392 | tf_op jit(solution)/shard_map/ppermute | solution.py:10
  267.1 2.0 copy.36
  (10 shorter events, 0.1 us)
Async XLA Ops:
  0.6 4.6 %copy-start.2 = (bf16[1,128,2560]{2,1,0:T(8,128)(2,1)S(1)}, bf16[1,128,2560]{2,1,0:T(8,128)(2,1)}, u32[]{:S(2)}) copy-start(bf16[1,128,2560]{2,1,0:T(8,128)(2,1)} %param.8) | copy-start | bytes 1966084
  0.6 4.6 %copy-start.1 = (bf16[1,128,2560]{2,1,0:T(8,128)(2,1)S(1)}, bf16[1,128,2560]{2,1,0:T(8,128)(2,1)}, u32[]{:S(2)}) copy-start(bf16[1,128,2560]{2,1,0:T(8,128)(2,1)} %param.7) | copy-start | bytes 1966084
  9.2 74.4 %all-to-all-start = ((bf16[32,16,5120]{2,1,0:T(8,128)(2,1)}), bf16[32,16,5120]{2,1,0:T(8,128)(2,1)}, u32[]{:S(2)}, u32[]{:S(2)}) async-start(bf16[32,16,5120]{2,1,0:T(8,128)(2,1)} %bitcast.80), calls=%async_computation | async-start | bytes 10485760 | tf_op jit(solution)/shard_map/all_to_all | solution.py:75
  83.6 70.7 %all-to-all-start.1 = ((bf16[32,16,5120]{2,1,0:T(8,128)(2,1)}), bf16[32,16,5120]{2,1,0:T(8,128)(2,1)}, u32[]{:S(2)}, u32[]{:S(2)}) async-start(bf16[32,16,5120]{2,1,0:T(8,128)(2,1)} %bitcast.79), calls=%async_computation.1 | async-start | bytes 10485760 | tf_op jit(solution)/shard_map/all_to_all | solution.py:76
  88.7 5.3 %copy-start.4 = (bf16[1,1,768,2560]{3,2,1,0:T(8,128)(2,1)S(1)}, bf16[1,1,768,2560]{3,2,1,0:T(8,128)(2,1)}, u32[]{:S(2)}) copy-start(bf16[1,1,768,2560]{3,2,1,0:T(8,128)(2,1)} %param.13) | copy-start | bytes 11796484
  93.9 4.1 %copy-start.7 = (bf16[1,1,2560,768]{3,2,1,0:T(8,128)(2,1)S(1)}, bf16[1,1,2560,768]{3,2,1,0:T(8,128)(2,1)}, u32[]{:S(2)}) copy-start(bf16[1,1,2560,768]{3,2,1,0:T(8,128)(2,1)} %param.12) | copy-start | bytes 11796484
  98.1 4.3 %copy-start.5 = (bf16[1,1,2560,768]{3,2,1,0:T(8,128)(2,1)S(1)}, bf16[1,1,2560,768]{3,2,1,0:T(8,128)(2,1)}, u32[]{:S(2)}) copy-start(bf16[1,1,2560,768]{3,2,1,0:T(8,128)(2,1)} %param.11) | copy-start | bytes 11796484
  154.4 6.5 %copy-start.6 = (bf16[1,1,2560,768]{3,2,1,0:T(8,128)(2,1)S(1)}, bf16[1,1,2560,768]{3,2,1,0:T(8,128)(2,1)}, u32[]{:S(2)}) copy-start(bf16[1,1,2560,768]{3,2,1,0:T(8,128)(2,1)} %param.11) | copy-start | bytes 11796484
  165.9 40.2 %all-to-all-start.2 = ((bf16[32,16,2560]{2,1,0:T(8,128)(2,1)}), bf16[32,16,2560]{2,1,0:T(8,128)(2,1)S(1)}, u32[]{:S(2)}, u32[]{:S(2)}) async-start(bf16[32,16,2560]{2,1,0:T(8,128)(2,1)} %bitcast.87), calls=%async_computation.2 | async-start | bytes 5242880 | tf_op jit(solution)/shard_map/all_to_all | solution.py:81
  178.0 6.4 %copy-start.8 = (bf16[1,1,2560,768]{3,2,1,0:T(8,128)(2,1)S(1)}, bf16[1,1,2560,768]{3,2,1,0:T(8,128)(2,1)}, u32[]{:S(2)}) copy-start(bf16[1,1,2560,768]{3,2,1,0:T(8,128)(2,1)} %param.12) | copy-start | bytes 11796484
  178.0 6.4 %copy-start.9 = (f32[512,768]{1,0:T(8,128)S(1)}, f32[512,768]{1,0:T(8,128)}, u32[]{:S(2)}) copy-start(f32[512,768]{1,0:T(8,128)} %fusion.14) | copy-start | bytes 4718596
  178.0 6.4 %copy-start.10 = (f32[512,768]{1,0:T(8,128)S(1)}, f32[512,768]{1,0:T(8,128)}, u32[]{:S(2)}) copy-start(f32[512,768]{1,0:T(8,128)} %fusion.2) | copy-start | bytes 4718596
  188.8 22.9 %copy-start.3 = (f32[1,128,6]{1,0,2:T(1,128)S(1)}, f32[1,128,6]{1,0,2:T(1,128)}, u32[]{:S(2)}) copy-start(f32[1,128,6]{1,0,2:T(1,128)} %param.10) | copy-start | bytes 9220
  206.2 1.5 copy-start
  207.7 40.2 %all-to-all-start.3 = ((bf16[32,16,2560]{2,1,0:T(8,128)(2,1)}), bf16[32,16,2560]{2,1,0:T(8,128)(2,1)S(1)}, u32[]{:S(2)}, u32[]{:S(2)}) async-start(bf16[32,16,2560]{2,1,0:T(8,128)(2,1)} %pad_maximum_fusion), calls=%async_computation.3 | async-start | bytes 5242880 | tf_op jit(solution)/shard_map/all_to_all | solution.py:94
  250.5 16.6 %collective-permute-start = (bf16[128,2560]{1,0:T(8,128)(2,1)S(1)}, bf16[128,2560]{1,0:T(8,128)(2,1)}, u32[]{:S(2)}, u32[]{:S(2)}) collective-permute-start(bf16[128,2560]{1,0:T(8,128)(2,1)S(1)} %fusion.18), channel_id=1, source_target_pairs={{32,0},{64,32},{96,64},{33,1},{65,33},{97,65},{34,2},{66,34},{98,6... | collective-permute-start | bytes 1966088 | tf_op jit(solution)/shard_map/ppermute | solution.py:10

commit v3 on v2

--- a/solution.py
+++ b/solution.py
@@ -1,6 +1,7 @@
 import jax
 import jax.numpy as jnp
 from jax import lax
+from jax.experimental import pallas as pl
 from jax.sharding import PartitionSpec as P
 
 
@@ -29,6 +30,58 @@
         up_part, up_matrix, (((1,), (1,)), ((), ())), preferred_element_type=jnp.float32
     )
     return input_back.astype(jnp.bfloat16), gate_value
+
+
+def expert_kernel(grad_ref, input_ref, gate_ref, up_ref, down_ref, back_ref, value_ref):
+    grad_rows = grad_ref[...]
+    input_rows = input_ref[...]
+    gate_matrix = gate_ref[...]
+    up_matrix = up_ref[...]
+    gate_pre = jnp.dot(input_rows, gate_matrix, preferred_element_type=jnp.float32)
+    up_pre = jnp.dot(input_rows, up_matrix, preferred_element_type=jnp.float32)
+    hidden_grad = lax.dot_general(
+        grad_rows, down_ref[...], (((1,), (1,)), ((), ())), preferred_element_type=jnp.float32
+    )
+    sigmoid = jax.nn.sigmoid(gate_pre)
+    active = gate_pre * sigmoid
+    value = jnp.sum(hidden_grad * active * up_pre, axis=-1, keepdims=True)
+    value_ref[...] = jnp.broadcast_to(value, value_ref.shape)
+    gate_part = (hidden_grad * up_pre * sigmoid * (1.0 + gate_pre * (1.0 - sigmoid))).astype(jnp.bfloat16)
+    up_part = (hidden_grad * active).astype(jnp.bfloat16)
+    back = lax.dot_general(
+        gate_part, gate_matrix, (((1,), (1,)), ((), ())), preferred_element_type=jnp.float32
+    ) + lax.dot_general(up_part, up_matrix, (((1,), (1,)), ((), ())), preferred_element_type=jnp.float32)
+    back_ref[...] = back.astype(back_ref.dtype)
+
+def expert_call(arrived, gate_matrix, up_matrix, down_matrix, tile=256):
+    rows, both = arrived.shape
+    width = both // 2
+    hidden = gate_matrix.shape[1]
+    steps = rows // tile
+    flops = 2 * rows * width * hidden * 5
+    cost = pl.CostEstimate(flops=flops, transcendentals=rows * hidden,
+                           bytes_accessed=rows * both * 2 + 3 * width * hidden * 2 + rows * width * 2)
+    back, value = pl.pallas_call(
+        expert_kernel,
+        grid=(steps,),
+        in_specs=[
+            pl.BlockSpec((tile, width), lambda i: (i, 0)),
+            pl.BlockSpec((tile, width), lambda i: (i, 1)),
+            pl.BlockSpec((width, hidden), lambda i: (0, 0)),
+            pl.BlockSpec((width, hidden), lambda i: (0, 0)),
+            pl.BlockSpec((hidden, width), lambda i: (0, 0)),
+        ],
+        out_specs=[
+            pl.BlockSpec((tile, width), lambda i: (i, 0)),
+            pl.BlockSpec((tile, 128), lambda i: (i, 0)),
+        ],
+        out_shape=[
+            jax.ShapeDtypeStruct((rows, width), jnp.bfloat16),
+            jax.ShapeDtypeStruct((rows, 128), jnp.float32),
+        ],
+        cost_estimate=cost,
+    )(arrived, arrived, gate_matrix, up_matrix, down_matrix)
+    return back, value[:, 0].astype(jnp.bfloat16)
 
 
 def body(out_grad, layer_input, route_ids, route_probs, gate_weight, up_weight, down_weight):
@@ -74,16 +127,12 @@
     send_b, weights_b = dispatch(1)
     arrived_a = lax.all_to_all(send_a, "expert", 0, 0, tiled=True).reshape(rows, 2 * model_width)
     arrived_b = lax.all_to_all(send_b, "expert", 0, 0, tiled=True).reshape(rows, 2 * model_width)
-    back_a, gate_a = expert_rows(
-        arrived_a[:, :model_width], arrived_a[:, model_width:], gate_matrix, up_matrix, down_matrix
-    )
+    back_a, gate_a = expert_call(arrived_a, gate_matrix, up_matrix, down_matrix)
     back_a, gate_a, arrived_b = lax.optimization_barrier((back_a, gate_a, arrived_b))
     returned_a = lax.all_to_all(
         back_a.reshape(peer_count, chunk, model_width), "expert", 0, 0, tiled=True
     ).reshape(rows, model_width)
-    back_b, gate_b = expert_rows(
-        arrived_b[:, :model_width], arrived_b[:, model_width:], gate_matrix, up_matrix, down_matrix
-    )
+    back_b, gate_b = expert_call(arrived_b, gate_matrix, up_matrix, down_matrix)
     gates = jnp.concatenate(
         [gate_a.reshape(peer_count, chunk), gate_b.reshape(peer_count, chunk)], axis=1
     )
@@ -110,8 +159,8 @@
     gate_slot = jnp.sum(
         jnp.where(gate_hits, gate_table.astype(jnp.float32), 0.0), axis=2
     ).astype(jnp.bfloat16)
-    passed = passed_along(combined.astype(jnp.bfloat16), "pipe", -1)
-    return (passed[None], gate_slot[None])
+    passed = passed_along(combined.astype(jnp.bfloat16)[None], "pipe", -1)
+    return (passed, gate_slot[None])
 
 
 def solution(mesh):

time: 270 us -> 259 us (0.959)
  matrix products: 61.8 us -> 15.7 us
  Pallas kernels: 0 us -> 40 us
  waiting for transfers between devices: 169 us -> 162 us
    dot_general x10 -> x0, matrix products: 47.5 us -> none  [the longest x2 11.6 us: expert_rows(): up_pre = jnp.dot(input_rows, up_matrix, preferred_element_type=jnp.float32)]
    pallas_call x0 -> x2, Pallas kernels: none -> 40 us  [expert_call(): pl.pallas_call(expert_kernel, grid=(steps,), in_specs=[pl.BlockSpec((tile...]
    all_to_all x1, waiting for transfers between devices: 17.3 us -> 10.4 us  [body(): lax.all_to_all(back_a.reshape(peer_count, chunk, model_width), 'expert',...]
  transfers between devices with their start and end apart: 5 -> 5, of which waited for: 5 -> 5; matrix products, arithmetic and copies ran while one was open for 18% -> 7% of each run, Pallas kernels for 0% -> 15%
where the time goes in v3:
time: 259 us
  waiting for transfers between devices  162 us (63%)
  Pallas kernels  40 us (15%)
  starting transfers between devices  23.1 us (9%)
  matrix products  15.7 us (6%)
  other arithmetic  8.81 us (3%)
  local copies, waits for them, and re-layouts  8.78 us (3%)
    all_to_all x1, waiting for transfers between devices, body(): lax.all_to_all(send_a, 'expert', 0, 0, tiled=True)  61.6 us
    all_to_all x1, waiting for transfers between devices, body(): lax.all_to_all(send_b, 'expert', 0, 0, tiled=True)  44.8 us
    pallas_call x2, Pallas kernels, expert_call(): pl.pallas_call(expert_kernel, grid=(steps,), in_specs=[pl.BlockSpec((tile...  40 us
    all_to_all x1, waiting for transfers between devices, body(): returned_b = lax.all_to_all(back_b, 'expert', 0, 0, tiled=True)  31.6 us
    ppermute x1, waiting for transfers between devices, passed_along(): lax.ppermute(value, axis, [(source, source + steps) for source in range(f...  13.2 us
    all_to_all x1, waiting for transfers between devices, body(): lax.all_to_all(back_a.reshape(peer_count, chunk, model_width), 'expert',...  10.4 us
    dot_general x2, matrix products, dispatch(): lax.dot_general(pick, both, (((0,), (0,)), ((), ())), preferred_element_t...  9.14 us
    all_to_all x1, starting transfers between devices, body(): lax.all_to_all(send_a, 'expert', 0, 0, tiled=True)  8.69 us
  transfers between devices with their start and end apart: 5, of which 5 were waited for; matrix products, arithmetic and copies ran while one was open for 7% of the time, Pallas kernels for 15%

profile of v3, /device:TPU:0, one launch (start us, length us, event | category | flops | bytes accessed | tf_op | source)
XLA Modules:
  0.0 258.8 jit_solution(2865658386169144716)
XLA Ops:
  0.6 0.8 copy.22
  1.4 0.1 eq.68
  1.6 0.1 eq.64
  1.7 1.7 reduce-window.6
  3.5 0.3 slice_reduce_fusion
  3.7 0.1 fusion.11
  3.9 0.1 sub.14
  4.0 0.1 sub.17
  4.1 0.6 bitcast_add_fusion
  4.8 0.1 copy.26
  4.8 0.3 fusion.3
  5.1 5.2 %convolution_convert_fusion.1 = bf16[512,5120]{1,0:T(8,128)(2,1)} fusion(pred[128,512]{1,0:T(8,128)(4,1)S(1)} %fusion.3, bf16[128,2560]{1,0:T(8,128)(2,1)} %bitcast.62, bf16[128,2560]{1,0:T(8,128)(2,1)} %bitcast.60), kind=kOutput, calls=%fused_computation.1 | convolution fusion | flops 676331520 | bytes 6619136 | tf_op jit(solution)/shard_map/dot_general | solution.py:120
  10.3 0.0 copy-start.1
  10.3 0.0 copy-start.2
  10.3 8.7 %all-to-all-start = ((bf16[32,16,5120]{2,1,0:T(8,128)(2,1)}), bf16[32,16,5120]{2,1,0:T(8,128)(2,1)}, u32[]{:S(2)}, u32[]{:S(2)}) async-start(bf16[32,16,5120]{2,1,0:T(8,128)(2,1)} %bitcast.57), calls=%async_computation | async-start | bytes 10485760 | tf_op jit(solution)/shard_map/all_to_all | solution.py:128
  19.0 0.1 copy.27
  19.1 0.3 fusion.2
  19.4 0.0 copy-done.1
  19.4 0.0 copy-done.2
  19.4 3.9 %convolution_convert_fusion = bf16[512,5120]{1,0:T(8,128)(2,1)} fusion(pred[128,512]{1,0:T(8,128)(4,1)S(1)} %fusion.2, bf16[128,2560]{1,0:T(8,128)(2,1)S(1)} %bitcast.63, bf16[128,2560]{1,0:T(8,128)(2,1)S(1)} %bitcast.61), kind=kOutput, calls=%fused_computation | convolution fusion | flops 676331520 | bytes 6619136 | tf_op jit(solution)/shard_map/dot_general | solution.py:120
  23.3 61.6 %all-to-all-done = bf16[32,16,5120]{2,1,0:T(8,128)(2,1)} async-done(((bf16[32,16,5120]{2,1,0:T(8,128)(2,1)}), bf16[32,16,5120]{2,1,0:T(8,128)(2,1)}, u32[]{:S(2)}, u32[]{:S(2)}) %all-to-all-start) | async-done | bytes 5242912 | tf_op jit(solution)/shard_map/all_to_all | solution.py:128
  84.9 4.9 %all-to-all-start.1 = ((bf16[32,16,5120]{2,1,0:T(8,128)(2,1)}), bf16[32,16,5120]{2,1,0:T(8,128)(2,1)}, u32[]{:S(2)}, u32[]{:S(2)}) async-start(bf16[32,16,5120]{2,1,0:T(8,128)(2,1)} %bitcast.56), calls=%async_computation.1 | async-start | bytes 10485760 | tf_op jit(solution)/shard_map/all_to_all | solution.py:129
  89.8 20.0 %shard_map.86 = (bf16[512,2560]{1,0:T(8,128)(2,1)}, f32[512,128]{1,0:T(8,128)}) custom-call(bf16[512,5120]{1,0:T(8,128)(2,1)} %bitcast.5.grad_ref.input_ref, bf16[512,5120]{1,0:T(8,128)(2,1)} %bitcast.5.grad_ref.input_ref, bf16[2560,768]{1,0:T(8,128)(2,1)} %bitcast.69, bf16[2560,768]{1,0:T(8,128)(2,1)} %bitcast.71, bf16[768,2560]{1,0:T(8,128)(2,1)} %bitcast.73), custom_call_target="tpu_custom_call" | custom-call | flops 10066329600 | bytes 19660800 | tf_op jit(solution)/shard_map/pallas_call | solution.py:64
  109.8 1.1 fusion.8
  110.9 44.8 %all-to-all-done.1 = bf16[32,16,5120]{2,1,0:T(8,128)(2,1)} async-done(((bf16[32,16,5120]{2,1,0:T(8,128)(2,1)}), bf16[32,16,5120]{2,1,0:T(8,128)(2,1)}, u32[]{:S(2)}, u32[]{:S(2)}) %all-to-all-start.1) | async-done | bytes 5242912 | tf_op jit(solution)/shard_map/all_to_all | solution.py:129
  155.7 4.2 %all-to-all-start.2 = ((bf16[32,16,2560]{2,1,0:T(8,128)(2,1)}), bf16[32,16,2560]{2,1,0:T(8,128)(2,1)S(1)}, u32[]{:S(2)}, u32[]{:S(2)}) async-start(bf16[32,16,2560]{2,1,0:T(8,128)(2,1)} %bitcast.64), calls=%async_computation.2 | async-start | bytes 5242880 | tf_op jit(solution)/shard_map/all_to_all | solution.py:132
  159.9 20.0 %shard_map.87 = (bf16[512,2560]{1,0:T(8,128)(2,1)}, f32[512,128]{1,0:T(8,128)}) custom-call(bf16[512,5120]{1,0:T(8,128)(2,1)} %bitcast.10.grad_ref.input_ref, bf16[512,5120]{1,0:T(8,128)(2,1)} %bitcast.10.grad_ref.input_ref, bf16[2560,768]{1,0:T(8,128)(2,1)} %bitcast.70, bf16[2560,768]{1,0:T(8,128)(2,1)} %bitcast.72, bf16[768,2560]{1,0:T(8,128)(2,1)} %bitcast.74), custom_call_target="tpu_custom_call" | custom-call | flops 10066329600 | bytes 19660800 | tf_op jit(solution)/shard_map/pallas_call | solution.py:64
  179.9 1.1 fusion.9
  181.0 0.1 convert_element_type.56
  181.1 0.1 reshape.118
  181.2 0.1 fusion.7
  181.3 0.3 copy.28
  181.6 3.9 %pad_maximum_fusion = bf16[32,16,2560]{2,1,0:T(8,128)(2,1)} fusion(bf16[32,1,2560]{2,1,0:T(2,128)(2,1)S(1)} %copy.28, bf16[32,15,2560]{2,1,0:T(8,128)(2,1)} %bitcast.65), kind=kLoop, calls=%fused_computation.8 | loop fusion | flops 5242880 | bytes 5242880 | tf_op jit(solution)/shard_map/concatenate | solution.py:140
  185.5 0.0 copy-start.3
  185.5 10.4 %all-to-all-done.2 = bf16[32,16,2560]{2,1,0:T(8,128)(2,1)S(1)} async-done(((bf16[32,16,2560]{2,1,0:T(8,128)(2,1)}), bf16[32,16,2560]{2,1,0:T(8,128)(2,1)S(1)}, u32[]{:S(2)}, u32[]{:S(2)}) %all-to-all-start.2) | async-done | bytes 2621472 | tf_op jit(solution)/shard_map/all_to_all | solution.py:132
  195.9 0.0 copy-start
  195.9 1.5 copy-done
  197.4 4.1 %all-to-all-start.3 = ((bf16[32,16,2560]{2,1,0:T(8,128)(2,1)}), bf16[32,16,2560]{2,1,0:T(8,128)(2,1)S(1)}, u32[]{:S(2)}, u32[]{:S(2)}) async-start(bf16[32,16,2560]{2,1,0:T(8,128)(2,1)} %pad_maximum_fusion), calls=%async_computation.3 | async-start | bytes 5242880 | tf_op jit(solution)/shard_map/all_to_all | solution.py:143
  201.5 0.0 copy-done.3
  201.5 0.5 select_reduce_fusion.1
  202.1 4.0 %convolution_add_fusion.1 = f32[128,2560]{1,0:T(8,128)} fusion(f32[128,512]{1,0:T(8,128)S(1)} %get-tuple-element.17, bf16[512,2560]{1,0:T(8,128)(2,1)} %bitcast.59, bf16[1,128,2560]{2,1,0:T(8,128)(2,1)S(1)} %copy-done.1), kind=kOutput, calls=%fused_computation.3 | convolution fusion | flops 2013921280 | bytes 4849664 | tf_op jit(solution)/shard_map/dot_general | solution.py:148
  206.1 31.6 %all-to-all-done.3 = bf16[32,16,2560]{2,1,0:T(8,128)(2,1)S(1)} async-done(((bf16[32,16,2560]{2,1,0:T(8,128)(2,1)}), bf16[32,16,2560]{2,1,0:T(8,128)(2,1)S(1)}, u32[]{:S(2)}, u32[]{:S(2)}) %all-to-all-start.3) | async-done | bytes 2621472 | tf_op jit(solution)/shard_map/all_to_all | solution.py:143
  237.7 2.5 fusion.1
  240.2 1.3 collective-permute-start
  241.5 0.9 copy.30
  242.4 0.1 fusion.15
  242.5 0.1 reshape.120
  242.6 1.1 select_reduce_fusion
  243.7 13.2 %collective-permute-done = bf16[1,128,2560]{2,1,0:T(8,128)(2,1)} collective-permute-done((bf16[1,128,2560]{2,1,0:T(8,128)(2,1)S(1)}, bf16[1,128,2560]{2,1,0:T(8,128)(2,1)}, u32[]{:S(2)}, u32[]{:S(2)}) %collective-permute-start) | collective-permute-done | bytes 655392 | tf_op jit(solution)/shard_map/ppermute | solution.py:11
  256.8 2.0 copy.37
  (4 shorter events, 0.0 us)
Async XLA Ops:
  10.3 9.0 %copy-start.1 = (bf16[1,128,2560]{2,1,0:T(8,128)(2,1)S(1)}, bf16[1,128,2560]{2,1,0:T(8,128)(2,1)}, u32[]{:S(2)}) copy-start(bf16[1,128,2560]{2,1,0:T(8,128)(2,1)} %param.7) | copy-start | bytes 1966084
  10.3 9.1 %copy-start.2 = (bf16[1,128,2560]{2,1,0:T(8,128)(2,1)S(1)}, bf16[1,128,2560]{2,1,0:T(8,128)(2,1)}, u32[]{:S(2)}) copy-start(bf16[1,128,2560]{2,1,0:T(8,128)(2,1)} %param.8) | copy-start | bytes 1966084
  10.3 74.6 %all-to-all-start = ((bf16[32,16,5120]{2,1,0:T(8,128)(2,1)}), bf16[32,16,5120]{2,1,0:T(8,128)(2,1)}, u32[]{:S(2)}, u32[]{:S(2)}) async-start(bf16[32,16,5120]{2,1,0:T(8,128)(2,1)} %bitcast.57), calls=%async_computation | async-start | bytes 10485760 | tf_op jit(solution)/shard_map/all_to_all | solution.py:128
  84.9 70.7 %all-to-all-start.1 = ((bf16[32,16,5120]{2,1,0:T(8,128)(2,1)}), bf16[32,16,5120]{2,1,0:T(8,128)(2,1)}, u32[]{:S(2)}, u32[]{:S(2)}) async-start(bf16[32,16,5120]{2,1,0:T(8,128)(2,1)} %bitcast.56), calls=%async_computation.1 | async-start | bytes 10485760 | tf_op jit(solution)/shard_map/all_to_all | solution.py:129
  155.7 40.2 %all-to-all-start.2 = ((bf16[32,16,2560]{2,1,0:T(8,128)(2,1)}), bf16[32,16,2560]{2,1,0:T(8,128)(2,1)S(1)}, u32[]{:S(2)}, u32[]{:S(2)}) async-start(bf16[32,16,2560]{2,1,0:T(8,128)(2,1)} %bitcast.64), calls=%async_computation.2 | async-start | bytes 5242880 | tf_op jit(solution)/shard_map/all_to_all | solution.py:132
  185.5 16.0 %copy-start.3 = (f32[1,128,6]{1,0,2:T(1,128)S(1)}, f32[1,128,6]{1,0,2:T(1,128)}, u32[]{:S(2)}) copy-start(f32[1,128,6]{1,0,2:T(1,128)} %param.10) | copy-start | bytes 9220
  195.9 1.5 copy-start
  197.4 40.2 %all-to-all-start.3 = ((bf16[32,16,2560]{2,1,0:T(8,128)(2,1)}), bf16[32,16,2560]{2,1,0:T(8,128)(2,1)S(1)}, u32[]{:S(2)}, u32[]{:S(2)}) async-start(bf16[32,16,2560]{2,1,0:T(8,128)(2,1)} %pad_maximum_fusion), calls=%async_computation.3 | async-start | bytes 5242880 | tf_op jit(solution)/shard_map/all_to_all | solution.py:143
  240.2 16.6 %collective-permute-start = (bf16[1,128,2560]{2,1,0:T(8,128)(2,1)S(1)}, bf16[1,128,2560]{2,1,0:T(8,128)(2,1)}, u32[]{:S(2)}, u32[]{:S(2)}) collective-permute-start(bf16[1,128,2560]{2,1,0:T(8,128)(2,1)S(1)} %fusion.1), channel_id=1, source_target_pairs={{32,0},{64,32},{96,64},{33,1},{65,33},{97,65},{34,2},{66,34},{98,6... | collective-permute-start | bytes 1966088 | tf_op jit(solution)/shard_map/ppermute | solution.py:11

commit v4 on v3

--- a/solution.py
+++ b/solution.py
@@ -116,9 +116,9 @@
         inside = (local >= 0) & (local < chunk)
         target = jnp.where(inside, ids * chunk + local, -1)
         hits = target[:, :, None] == lanes
-        pick = jnp.any(hits, axis=1).astype(jnp.bfloat16)
-        send = lax.dot_general(
-            pick, both, (((0,), (0,)), ((), ())), preferred_element_type=jnp.float32
+        pick = jnp.any(target[None, :, :] == lanes.reshape(rows, 1, 1), axis=2)
+        send = jnp.dot(
+            pick.astype(jnp.bfloat16), both, preferred_element_type=jnp.float32
         ).astype(jnp.bfloat16)
         weights = jnp.sum(jnp.where(hits, slot_probs[:, :, None], 0.0), axis=1)
         return send.reshape(peer_count, chunk, 2 * model_width), weights

time: 259 us -> 259 us (level)
  transfers between devices with their start and end apart: 5 -> 5, of which waited for: 5 -> 5; matrix products, arithmetic and copies ran while one was open for 7% -> 8% of each run, Pallas kernels for 15% -> 16%
where the time goes in v4:
time: 259 us; the launch traced here: 258 us
  waiting for transfers between devices  160 us (62%)
  Pallas kernels  40 us (15%)
  starting transfers between devices  23.1 us (9%)
  matrix products  15.6 us (6%)
  local copies, waits for them, and re-layouts  10 us (4%)
  other arithmetic  8.82 us (3%)
    all_to_all x1, waiting for transfers between devices, body(): lax.all_to_all(send_a, 'expert', 0, 0, tiled=True)  61.7 us
    all_to_all x1, waiting for transfers between devices, body(): lax.all_to_all(send_b, 'expert', 0, 0, tiled=True)  44.8 us
    pallas_call x2, Pallas kernels, expert_call(): pl.pallas_call(expert_kernel, grid=(steps,), in_specs=[pl.BlockSpec((tile...  40 us
    all_to_all x1, waiting for transfers between devices, body(): returned_b = lax.all_to_all(back_b, 'expert', 0, 0, tiled=True)  29.7 us
    ppermute x1, waiting for transfers between devices, passed_along(): lax.ppermute(value, axis, [(source, source + steps) for source in range(f...  13.1 us
    all_to_all x1, waiting for transfers between devices, body(): lax.all_to_all(back_a.reshape(peer_count, chunk, model_width), 'expert',...  10.4 us
    dot_general x2, matrix products, dispatch(): jnp.dot(pick.astype(jnp.bfloat16), both, preferred_element_type=jnp.float32)  9.02 us
    all_to_all x1, starting transfers between devices, body(): lax.all_to_all(send_a, 'expert', 0, 0, tiled=True)  8.69 us
  transfers between devices with their start and end apart: 5, of which 5 were waited for; matrix products, arithmetic and copies ran while one was open for 8% of the time, Pallas kernels for 16%

profile of v4, /device:TPU:0, one launch (start us, length us, event | category | flops | bytes accessed | tf_op | source)
XLA Modules:
  0.0 258.1 jit_solution(7652026112905875523)
XLA Ops:
  0.6 0.8 copy.24
  1.4 0.1 eq.98
  1.6 0.1 eq.94
  1.7 1.7 reduce-window.6
  3.5 0.3 slice_reduce_fusion
  3.7 0.1 fusion.11
  3.9 0.1 sub.19
  4.0 0.1 sub.22
  4.2 0.1 copy.29
  4.2 0.2 fusion.2
  4.5 5.1 %convolution_convert_fusion.1 = bf16[512,5120]{1,0:T(8,128)(2,1)} fusion(pred[512,128]{1,0:T(8,128)(4,1)S(1)} %fusion.2, bf16[128,2560]{1,0:T(8,128)(2,1)} %bitcast.66, bf16[128,2560]{1,0:T(8,128)(2,1)} %bitcast.64), kind=kOutput, calls=%fused_computation.1 | convolution fusion | flops 676331520 | bytes 6619136 | tf_op jit(solution)/shard_map/dot_general | solution.py:120
  9.6 0.0 copy-start.1
  9.6 0.0 copy-start.2
  9.6 8.7 %all-to-all-start = ((bf16[32,16,5120]{2,1,0:T(8,128)(2,1)}), bf16[32,16,5120]{2,1,0:T(8,128)(2,1)}, u32[]{:S(2)}, u32[]{:S(2)}) async-start(bf16[32,16,5120]{2,1,0:T(8,128)(2,1)} %bitcast.61), calls=%async_computation | async-start | bytes 10485760 | tf_op jit(solution)/shard_map/all_to_all | solution.py:128
  18.3 0.1 copy.30
  18.4 0.2 fusion.3
  18.6 0.0 copy-done.1
  18.7 0.0 copy-done.2
  18.7 3.9 %convolution_convert_fusion = bf16[512,5120]{1,0:T(8,128)(2,1)} fusion(pred[512,128]{1,0:T(8,128)(4,1)S(1)} %fusion.3, bf16[128,2560]{1,0:T(8,128)(2,1)S(1)} %bitcast.67, bf16[128,2560]{1,0:T(8,128)(2,1)S(1)} %bitcast.65), kind=kOutput, calls=%fused_computation | convolution fusion | flops 676331520 | bytes 6619136 | tf_op jit(solution)/shard_map/dot_general | solution.py:120
  22.5 61.7 %all-to-all-done = bf16[32,16,5120]{2,1,0:T(8,128)(2,1)} async-done(((bf16[32,16,5120]{2,1,0:T(8,128)(2,1)}), bf16[32,16,5120]{2,1,0:T(8,128)(2,1)}, u32[]{:S(2)}, u32[]{:S(2)}) %all-to-all-start) | async-done | bytes 5242912 | tf_op jit(solution)/shard_map/all_to_all | solution.py:128
  84.2 4.9 %all-to-all-start.1 = ((bf16[32,16,5120]{2,1,0:T(8,128)(2,1)}), bf16[32,16,5120]{2,1,0:T(8,128)(2,1)}, u32[]{:S(2)}, u32[]{:S(2)}) async-start(bf16[32,16,5120]{2,1,0:T(8,128)(2,1)} %bitcast.60), calls=%async_computation.1 | async-start | bytes 10485760 | tf_op jit(solution)/shard_map/all_to_all | solution.py:129
  89.1 20.0 %shard_map.86 = (bf16[512,2560]{1,0:T(8,128)(2,1)}, f32[512,128]{1,0:T(8,128)}) custom-call(bf16[512,5120]{1,0:T(8,128)(2,1)} %bitcast.6.grad_ref.input_ref, bf16[512,5120]{1,0:T(8,128)(2,1)} %bitcast.6.grad_ref.input_ref, bf16[2560,768]{1,0:T(8,128)(2,1)} %bitcast.73, bf16[2560,768]{1,0:T(8,128)(2,1)} %bitcast.75, bf16[768,2560]{1,0:T(8,128)(2,1)} %bitcast.77), custom_call_target="tpu_custom_call" | custom-call | flops 10066329600 | bytes 19660800 | tf_op jit(solution)/shard_map/pallas_call | solution.py:64
  109.1 1.1 fusion.8
  110.2 44.8 %all-to-all-done.1 = bf16[32,16,5120]{2,1,0:T(8,128)(2,1)} async-done(((bf16[32,16,5120]{2,1,0:T(8,128)(2,1)}), bf16[32,16,5120]{2,1,0:T(8,128)(2,1)}, u32[]{:S(2)}, u32[]{:S(2)}) %all-to-all-start.1) | async-done | bytes 5242912 | tf_op jit(solution)/shard_map/all_to_all | solution.py:129
  155.0 4.2 %all-to-all-start.2 = ((bf16[32,16,2560]{2,1,0:T(8,128)(2,1)}), bf16[32,16,2560]{2,1,0:T(8,128)(2,1)S(1)}, u32[]{:S(2)}, u32[]{:S(2)}) async-start(bf16[32,16,2560]{2,1,0:T(8,128)(2,1)} %bitcast.68), calls=%async_computation.2 | async-start | bytes 5242880 | tf_op jit(solution)/shard_map/all_to_all | solution.py:132
  159.2 20.0 %shard_map.87 = (bf16[512,2560]{1,0:T(8,128)(2,1)}, f32[512,128]{1,0:T(8,128)}) custom-call(bf16[512,5120]{1,0:T(8,128)(2,1)} %bitcast.12.grad_ref.input_ref, bf16[512,5120]{1,0:T(8,128)(2,1)} %bitcast.12.grad_ref.input_ref, bf16[2560,768]{1,0:T(8,128)(2,1)} %bitcast.74, bf16[2560,768]{1,0:T(8,128)(2,1)} %bitcast.76, bf16[768,2560]{1,0:T(8,128)(2,1)} %bitcast.78), custom_call_target="tpu_custom_call" | custom-call | flops 10066329600 | bytes 19660800 | tf_op jit(solution)/shard_map/pallas_call | solution.py:64
  179.2 1.1 fusion.9
  180.3 0.1 convert_element_type.56
  180.4 0.1 reshape.166
  180.5 0.1 fusion.7
  180.6 0.3 copy.32
  180.8 3.9 %pad_maximum_fusion = bf16[32,16,2560]{2,1,0:T(8,128)(2,1)} fusion(bf16[32,1,2560]{2,1,0:T(2,128)(2,1)S(1)} %copy.32, bf16[32,15,2560]{2,1,0:T(8,128)(2,1)} %bitcast.69), kind=kLoop, calls=%fused_computation.8 | loop fusion | flops 5242880 | bytes 5242880 | tf_op jit(solution)/shard_map/concatenate | solution.py:140
  184.8 0.0 copy-start.3
  184.8 10.4 %all-to-all-done.2 = bf16[32,16,2560]{2,1,0:T(8,128)(2,1)S(1)} async-done(((bf16[32,16,2560]{2,1,0:T(8,128)(2,1)}), bf16[32,16,2560]{2,1,0:T(8,128)(2,1)S(1)}, u32[]{:S(2)}, u32[]{:S(2)}) %all-to-all-start.2) | async-done | bytes 2621472 | tf_op jit(solution)/shard_map/all_to_all | solution.py:132
  195.2 0.0 copy-start
  195.2 1.5 copy-done
  196.7 4.1 %all-to-all-start.3 = ((bf16[32,16,2560]{2,1,0:T(8,128)(2,1)}), bf16[32,16,2560]{2,1,0:T(8,128)(2,1)S(1)}, u32[]{:S(2)}, u32[]{:S(2)}) async-start(bf16[32,16,2560]{2,1,0:T(8,128)(2,1)} %pad_maximum_fusion), calls=%async_computation.3 | async-start | bytes 5242880 | tf_op jit(solution)/shard_map/all_to_all | solution.py:143
  200.8 0.1 sub.18
  200.9 0.1 sub.23
  201.1 0.7 bitcast_add_fusion
  201.7 0.9 copy.28
  202.6 0.1 copy.31
  202.7 0.0 copy-done.3
  202.7 0.5 select_reduce_fusion.1
  203.3 4.0 %convolution_add_fusion.1 = f32[128,2560]{1,0:T(8,128)} fusion(f32[128,512]{1,0:T(8,128)S(1)} %get-tuple-element.17, bf16[512,2560]{1,0:T(8,128)(2,1)} %bitcast.63, bf16[1,128,2560]{2,1,0:T(8,128)(2,1)S(1)} %copy-done.1), kind=kOutput, calls=%fused_computation.3 | convolution fusion | flops 2013921280 | bytes 4849664 | tf_op jit(solution)/shard_map/dot_general | solution.py:148
  207.3 29.7 %all-to-all-done.3 = bf16[32,16,2560]{2,1,0:T(8,128)(2,1)S(1)} async-done(((bf16[32,16,2560]{2,1,0:T(8,128)(2,1)}), bf16[32,16,2560]{2,1,0:T(8,128)(2,1)S(1)}, u32[]{:S(2)}, u32[]{:S(2)}) %all-to-all-start.3) | async-done | bytes 2621472 | tf_op jit(solution)/shard_map/all_to_all | solution.py:143
  237.0 2.5 fusion.1
  239.5 1.3 collective-permute-start
  240.8 0.9 copy.34
  241.7 0.1 fusion.15
  241.8 0.1 reshape.168
  241.9 1.1 select_reduce_fusion
  243.0 13.1 %collective-permute-done = bf16[1,128,2560]{2,1,0:T(8,128)(2,1)} collective-permute-done((bf16[1,128,2560]{2,1,0:T(8,128)(2,1)S(1)}, bf16[1,128,2560]{2,1,0:T(8,128)(2,1)}, u32[]{:S(2)}, u32[]{:S(2)}) %collective-permute-start) | collective-permute-done | bytes 655392 | tf_op jit(solution)/shard_map/ppermute | solution.py:11
  256.1 2.0 copy.41
  (5 shorter events, 0.1 us)
Async XLA Ops:
  9.6 9.0 %copy-start.1 = (bf16[1,128,2560]{2,1,0:T(8,128)(2,1)S(1)}, bf16[1,128,2560]{2,1,0:T(8,128)(2,1)}, u32[]{:S(2)}) copy-start(bf16[1,128,2560]{2,1,0:T(8,128)(2,1)} %param.7) | copy-start | bytes 1966084
  9.6 9.0 %copy-start.2 = (bf16[1,128,2560]{2,1,0:T(8,128)(2,1)S(1)}, bf16[1,128,2560]{2,1,0:T(8,128)(2,1)}, u32[]{:S(2)}) copy-start(bf16[1,128,2560]{2,1,0:T(8,128)(2,1)} %param.8) | copy-start | bytes 1966084
  9.6 74.6 %all-to-all-start = ((bf16[32,16,5120]{2,1,0:T(8,128)(2,1)}), bf16[32,16,5120]{2,1,0:T(8,128)(2,1)}, u32[]{:S(2)}, u32[]{:S(2)}) async-start(bf16[32,16,5120]{2,1,0:T(8,128)(2,1)} %bitcast.61), calls=%async_computation | async-start | bytes 10485760 | tf_op jit(solution)/shard_map/all_to_all | solution.py:128
  84.2 70.7 %all-to-all-start.1 = ((bf16[32,16,5120]{2,1,0:T(8,128)(2,1)}), bf16[32,16,5120]{2,1,0:T(8,128)(2,1)}, u32[]{:S(2)}, u32[]{:S(2)}) async-start(bf16[32,16,5120]{2,1,0:T(8,128)(2,1)} %bitcast.60), calls=%async_computation.1 | async-start | bytes 10485760 | tf_op jit(solution)/shard_map/all_to_all | solution.py:129
  155.0 40.2 %all-to-all-start.2 = ((bf16[32,16,2560]{2,1,0:T(8,128)(2,1)}), bf16[32,16,2560]{2,1,0:T(8,128)(2,1)S(1)}, u32[]{:S(2)}, u32[]{:S(2)}) async-start(bf16[32,16,2560]{2,1,0:T(8,128)(2,1)} %bitcast.68), calls=%async_computation.2 | async-start | bytes 5242880 | tf_op jit(solution)/shard_map/all_to_all | solution.py:132
  184.8 17.9 %copy-start.3 = (f32[1,128,6]{1,0,2:T(1,128)S(1)}, f32[1,128,6]{1,0,2:T(1,128)}, u32[]{:S(2)}) copy-start(f32[1,128,6]{1,0,2:T(1,128)} %param.10) | copy-start | bytes 9220
  195.2 1.5 copy-start
  196.7 40.2 %all-to-all-start.3 = ((bf16[32,16,2560]{2,1,0:T(8,128)(2,1)}), bf16[32,16,2560]{2,1,0:T(8,128)(2,1)S(1)}, u32[]{:S(2)}, u32[]{:S(2)}) async-start(bf16[32,16,2560]{2,1,0:T(8,128)(2,1)} %pad_maximum_fusion), calls=%async_computation.3 | async-start | bytes 5242880 | tf_op jit(solution)/shard_map/all_to_all | solution.py:143
  239.5 16.6 %collective-permute-start = (bf16[1,128,2560]{2,1,0:T(8,128)(2,1)S(1)}, bf16[1,128,2560]{2,1,0:T(8,128)(2,1)}, u32[]{:S(2)}, u32[]{:S(2)}) collective-permute-start(bf16[1,128,2560]{2,1,0:T(8,128)(2,1)S(1)} %fusion.1), channel_id=1, source_target_pairs={{32,0},{64,32},{96,64},{33,1},{65,33},{97,65},{34,2},{66,34},{98,6... | collective-permute-start | bytes 1966088 | tf_op jit(solution)/shard_map/ppermute | solution.py:11

commit v5 on v4

--- a/solution.py
+++ b/solution.py
@@ -109,7 +109,6 @@
     ids = chosen
     lanes = jnp.arange(rows, dtype=jnp.int32)[None, None, :]
     both = jnp.concatenate([grad_tokens, input_tokens], axis=1)
-    gate_row = chunk - 1
 
     def dispatch(part):
         local = places - part * chunk
@@ -117,31 +116,54 @@
         target = jnp.where(inside, ids * chunk + local, -1)
         hits = target[:, :, None] == lanes
         pick = jnp.any(target[None, :, :] == lanes.reshape(rows, 1, 1), axis=2)
-        send = jnp.dot(
-            pick.astype(jnp.bfloat16), both, preferred_element_type=jnp.float32
-        ).astype(jnp.bfloat16)
         weights = jnp.sum(jnp.where(hits, slot_probs[:, :, None], 0.0), axis=1)
-        return send.reshape(peer_count, chunk, 2 * model_width), weights
-
-    send_a, weights_a = dispatch(0)
-    send_b, weights_b = dispatch(1)
+        return pick, weights
+
+    pick_a, weights_a = dispatch(0)
+    send_a = jnp.dot(pick_a.astype(jnp.bfloat16), both, preferred_element_type=jnp.float32)
+    send_a = send_a.astype(jnp.bfloat16).reshape(peer_count, chunk, 2 * model_width)
+    unused, weights_b = dispatch(1)
+    rest = capacity - chunk
+    local = places - chunk
+    grad_row = jnp.where(local >= 0, ids * 2 * rest + local, -1)
+    input_row = jnp.where(local >= 0, grad_row + rest, -1)
+    send_lanes = jnp.arange(peer_count * 2 * rest, dtype=jnp.int32).reshape(-1, 1, 1)
+    pick_grad = jnp.any(grad_row[None, :, :] == send_lanes, axis=2).astype(jnp.bfloat16)
+    pick_input = jnp.any(input_row[None, :, :] == send_lanes, axis=2).astype(jnp.bfloat16)
+    send_b = jnp.dot(pick_grad, grad_tokens, preferred_element_type=jnp.float32) + jnp.dot(
+        pick_input, input_tokens, preferred_element_type=jnp.float32
+    )
+    send_b = send_b.astype(jnp.bfloat16).reshape(peer_count, 2 * rest, model_width)
+
     arrived_a = lax.all_to_all(send_a, "expert", 0, 0, tiled=True).reshape(rows, 2 * model_width)
-    arrived_b = lax.all_to_all(send_b, "expert", 0, 0, tiled=True).reshape(rows, 2 * model_width)
+    arrived_b = lax.all_to_all(send_b, "expert", 0, 0, tiled=True)
     back_a, gate_a = expert_call(arrived_a, gate_matrix, up_matrix, down_matrix)
     back_a, gate_a, arrived_b = lax.optimization_barrier((back_a, gate_a, arrived_b))
     returned_a = lax.all_to_all(
         back_a.reshape(peer_count, chunk, model_width), "expert", 0, 0, tiled=True
     ).reshape(rows, model_width)
-    back_b, gate_b = expert_call(arrived_b, gate_matrix, up_matrix, down_matrix)
+    arrived_b = jnp.concatenate(
+        [
+            arrived_b[:, :rest].reshape(peer_count * rest, model_width),
+            arrived_b[:, rest:].reshape(peer_count * rest, model_width),
+        ],
+        axis=1,
+    )
+    back_b, gate_b = expert_call(arrived_b, gate_matrix, up_matrix, down_matrix, tile=128)
     gates = jnp.concatenate(
-        [gate_a.reshape(peer_count, chunk), gate_b.reshape(peer_count, chunk)], axis=1
-    )
-    gates = jnp.pad(gates, ((0, 0), (0, model_width - 2 * chunk)))
+        [gate_a.reshape(peer_count, chunk), gate_b.reshape(peer_count, rest)], axis=1
+    )
+    gates = jnp.pad(gates, ((0, 0), (0, model_width - capacity)))
     back_b = jnp.concatenate(
-        [back_b.reshape(peer_count, chunk, model_width)[:, :gate_row], gates[:, None, :]], axis=1
+        [
+            back_b.reshape(peer_count, rest, model_width),
+            gates[:, None, :],
+            jnp.zeros((peer_count, chunk - rest - 1, model_width), back_b.dtype),
+        ],
+        axis=1,
     )
     returned_b = lax.all_to_all(back_b, "expert", 0, 0, tiled=True)
-    gate_table = returned_b[:, gate_row, : 2 * chunk].reshape(-1)
+    gate_table = returned_b[:, rest, :capacity].reshape(-1)
     returned_b = returned_b.reshape(rows, model_width)
 
     def weighted(weights, returned):
@@ -154,7 +176,7 @@
 
     combined = grad_tokens.astype(jnp.float32) + weighted(weights_a, returned_a)
     combined = combined + weighted(weights_b, returned_b)
-    gate_index = ids * 2 * chunk + places
+    gate_index = ids * capacity + places
     gate_hits = gate_index[:, :, None] == jnp.arange(gate_table.shape[0], dtype=jnp.int32)
     gate_slot = jnp.sum(
         jnp.where(gate_hits, gate_table.astype(jnp.float32), 0.0), axis=2

time: 259 us -> 260 us (level)
  waiting for transfers between devices: 160 us -> 135 us
  local copies, waits for them, and re-layouts: 10 us -> 21.6 us
  other arithmetic: 8.82 us -> 14.1 us
  Pallas kernels: 40 us -> 43.5 us
  starting transfers between devices: 23.1 us -> 26.4 us
    all_to_all x1, waiting for transfers between devices: 44.8 us -> 29.8 us  [body(): arrived_b = lax.all_to_all(send_b, 'expert', 0, 0, tiled=True)]
    all_to_all x1, waiting for transfers between devices: 10.4 us -> 0.01 us  [body(): lax.all_to_all(back_a.reshape(peer_count, chunk, model_width), 'expert',...]
    reshape x0 -> x3, local copies, waits for them, and re-layouts: none -> 10.1 us  [the longest x1 4.06 us: body(): back_b.reshape(peer_count, rest, model_width)]
    slice x1 -> x2, local copies, waits for them, and re-layouts: 0.26 us -> 5.04 us  [the longest x1 4.78 us: body(): arrived_b[:, :rest].reshape(peer_count * rest, model_width)]
    concatenate x1 -> x2, other arithmetic: 3.93 us -> 8.7 us  [the longest x1 4.42 us: body(): jnp.concatenate([arrived_b[:, :rest].reshape(peer_count * rest, model_wid...]
    pallas_call x2, Pallas kernels: 40 us -> 43.5 us  [expert_call(): pl.pallas_call(expert_kernel, grid=(steps,), in_specs=[pl.BlockSpec((tile...]
    all_to_all x1, starting transfers between devices: 4.06 us -> 7.38 us  [body(): returned_b = lax.all_to_all(back_b, 'expert', 0, 0, tiled=True)]
    dot_general x2 -> x3, matrix products: 9.02 us -> 9.5 us  [the longest x1 5.14 us: body(): jnp.dot(pick_a.astype(jnp.bfloat16), both, preferred_element_type=jnp.flo...]
  transfers between devices with their start and end apart: 5 -> 5, of which waited for: 5 -> 4; matrix products, arithmetic and copies ran while one was open for 8% -> 10% of each run, Pallas kernels for 16% -> 17%
where the time goes in v5:
time: 260 us; the launch traced here: 259 us
  waiting for transfers between devices  135 us (52%)
  Pallas kernels  43.5 us (17%)
  starting transfers between devices  26.4 us (10%)
  local copies, waits for them, and re-layouts  21.6 us (8%)
  matrix products  16.9 us (6%)
  other arithmetic  14.1 us (5%)
    all_to_all x1, waiting for transfers between devices, body(): lax.all_to_all(send_a, 'expert', 0, 0, tiled=True)  60.7 us
    pallas_call x2, Pallas kernels, expert_call(): pl.pallas_call(expert_kernel, grid=(steps,), in_specs=[pl.BlockSpec((tile...  43.5 us
    all_to_all x1, waiting for transfers between devices, body(): returned_b = lax.all_to_all(back_b, 'expert', 0, 0, tiled=True)  30.9 us
    all_to_all x1, waiting for transfers between devices, body(): arrived_b = lax.all_to_all(send_b, 'expert', 0, 0, tiled=True)  29.8 us
    ppermute x1, waiting for transfers between devices, passed_along(): lax.ppermute(value, axis, [(source, source + steps) for source in range(f...  14.1 us
    all_to_all x1, starting transfers between devices, body(): lax.all_to_all(send_a, 'expert', 0, 0, tiled=True)  8.69 us
    dot_general x2, matrix products, weighted(): jnp.dot(weights, returned.astype(jnp.float32), precision=lax.Precision.HI...  7.41 us
    all_to_all x1, starting transfers between devices, body(): returned_b = lax.all_to_all(back_b, 'expert', 0, 0, tiled=True)  7.38 us
  transfers between devices with their start and end apart: 5, of which 4 were waited for; matrix products, arithmetic and copies ran while one was open for 10% of the time, Pallas kernels for 17%

profile of v5, /device:TPU:0, one launch (start us, length us, event | category | flops | bytes accessed | tf_op | source)
XLA Modules:
  0.0 258.9 jit_solution(7874038442339760541)
XLA Ops:
  0.6 0.8 copy.40
  1.4 0.1 eq.113
  1.6 0.1 eq.109
  1.7 1.7 reduce-window.6
  3.5 0.3 slice_reduce_fusion
  3.8 0.1 fusion.15
  3.9 0.1 sub.20
  4.0 0.1 copy.46
  4.1 0.2 sub.23
  4.2 0.1 copy.49
  4.3 0.7 compare_select_fusion
  5.0 0.2 fusion.4
  5.3 5.1 %convolution_convert_fusion = bf16[512,5120]{1,0:T(8,128)(2,1)} fusion(pred[512,128]{1,0:T(8,128)(4,1)S(1)} %fusion.4, bf16[128,2560]{1,0:T(8,128)(2,1)} %bitcast.70, bf16[128,2560]{1,0:T(8,128)(2,1)} %bitcast.69), kind=kOutput, calls=%fused_computation.1 | convolution fusion | flops 676331520 | bytes 6619136 | tf_op jit(solution)/shard_map/dot_general | solution.py:123
  10.4 0.0 copy-done.3
  10.4 8.7 %all-to-all-start = ((bf16[32,16,5120]{2,1,0:T(8,128)(2,1)}), bf16[32,16,5120]{2,1,0:T(8,128)(2,1)}, u32[]{:S(2)}, u32[]{:S(2)}) async-start(bf16[32,16,5120]{2,1,0:T(8,128)(2,1)} %bitcast.65), calls=%async_computation | async-start | bytes 10485760 | tf_op jit(solution)/shard_map/all_to_all | solution.py:138
  19.1 0.4 fusion.2
  19.5 0.4 fusion.3
  19.9 0.0 copy-done.1
  19.9 0.0 copy-start.2
  19.9 1.2 fusion.22
  21.1 0.0 copy-done.2
  21.1 3.2 %add_convert_fusion = bf16[768,2560]{1,0:T(8,128)(2,1)} fusion(f32[768,2560]{1,0:T(8,128)S(1)} %fusion.22, pred[768,128]{1,0:T(8,128)(4,1)S(1)} %fusion.3, bf16[1,128,2560]{2,1,0:T(8,128)(2,1)S(1)} %copy-done.2), kind=kOutput, calls=%fused_computation | convolution fusion | flops 507248640 | bytes 12550144 | tf_op jit(solution)/shard_map/dot_general | solution.py:133
  24.3 60.7 %all-to-all-done = bf16[32,16,5120]{2,1,0:T(8,128)(2,1)} async-done(((bf16[32,16,5120]{2,1,0:T(8,128)(2,1)}), bf16[32,16,5120]{2,1,0:T(8,128)(2,1)}, u32[]{:S(2)}, u32[]{:S(2)}) %all-to-all-start) | async-done | bytes 5242912 | tf_op jit(solution)/shard_map/all_to_all | solution.py:138
  85.0 4.8 %all-to-all-start.1 = ((bf16[32,24,2560]{2,1,0:T(8,128)(2,1)}), bf16[32,24,2560]{2,1,0:T(8,128)(2,1)}, u32[]{:S(2)}, u32[]{:S(2)}) async-start(bf16[32,24,2560]{2,1,0:T(8,128)(2,1)} %bitcast.66), calls=%async_computation.1 | async-start | bytes 7864320 | tf_op jit(solution)/shard_map/all_to_all | solution.py:139
  89.8 0.1 pad.7.clone
  89.9 20.0 %shard_map.86 = (bf16[512,2560]{1,0:T(8,128)(2,1)}, f32[512,128]{1,0:T(8,128)}) custom-call(bf16[512,5120]{1,0:T(8,128)(2,1)} %bitcast.4.grad_ref.input_ref, bf16[512,5120]{1,0:T(8,128)(2,1)} %bitcast.4.grad_ref.input_ref, bf16[2560,768]{1,0:T(8,128)(2,1)} %bitcast.76, bf16[2560,768]{1,0:T(8,128)(2,1)} %bitcast.78, bf16[768,2560]{1,0:T(8,128)(2,1)} %bitcast.80), custom_call_target="tpu_custom_call" | custom-call | flops 10066329600 | bytes 19660800 | tf_op jit(solution)/shard_map/pallas_call | solution.py:64
  109.9 1.1 fusion.12
  111.0 29.8 %all-to-all-done.1 = bf16[32,24,2560]{2,1,0:T(8,128)(2,1)} async-done(((bf16[32,24,2560]{2,1,0:T(8,128)(2,1)}), bf16[32,24,2560]{2,1,0:T(8,128)(2,1)}, u32[]{:S(2)}, u32[]{:S(2)}) %all-to-all-start.1) | async-done | bytes 3932192 | tf_op jit(solution)/shard_map/all_to_all | solution.py:139
  140.8 4.8 %fusion.24 = (bf16[32,12,2560]{2,1,0:T(8,128)(2,1)}, bf16[32,12,2560]{2,1,0:T(8,128)(2,1)S(1)}) fusion(bf16[32,24,2560]{2,1,0:T(8,128)(2,1)} %all-to-all-done.1), kind=kLoop, calls=%fused_computation.62 | loop fusion | bytes 7864320 | tf_op jit(solution)/shard_map/slice | solution.py:147
  145.5 4.0 %reshape.163 = bf16[384,2560]{1,0:T(8,128)(2,1)} reshape(bf16[32,12,2560]{2,1,0:T(8,128)(2,1)} %get-tuple-element.20) | data formatting | bytes 3932160 | tf_op jit(solution)/shard_map/reshape | solution.py:147
  149.6 2.0 reshape.164
  151.5 4.2 %all-to-all-start.2 = ((bf16[32,16,2560]{2,1,0:T(8,128)(2,1)}), bf16[32,16,2560]{2,1,0:T(8,128)(2,1)S(1)}, u32[]{:S(2)}, u32[]{:S(2)}) async-start(bf16[32,16,2560]{2,1,0:T(8,128)(2,1)} %bitcast.71), calls=%async_computation.2 | async-start | bytes 5242880 | tf_op jit(solution)/shard_map/all_to_all | solution.py:142
  155.8 4.4 %pad_maximum_fusion.grad_ref.input_ref = bf16[384,5120]{1,0:T(8,128)(2,1)} fusion(bf16[384,2560]{1,0:T(8,128)(2,1)} %reshape.164, bf16[384,2560]{1,0:T(8,128)(2,1)} %reshape.163), kind=kLoop, calls=%fused_computation.2 | loop fusion | flops 7864320 | bytes 7864320 | tf_op jit(solution)/shard_map/concatenate | solution.py:145
  160.2 23.6 %shard_map.87 = (bf16[384,2560]{1,0:T(8,128)(2,1)}, f32[384,128]{1,0:T(8,128)}) custom-call(bf16[384,5120]{1,0:T(8,128)(2,1)} %pad_maximum_fusion.grad_ref.input_ref, bf16[384,5120]{1,0:T(8,128)(2,1)} %pad_maximum_fusion.grad_ref.input_ref, bf16[2560,768]{1,0:T(8,128)(2,1)} %bitcast.77, bf16[2560,768]{1,0:T(8,128)(2,1)} %bitcast.79, bf16[768,2560]{1,0:T(8,128)(2,1)} %bitcast.81), custom_call_target="tpu_custom_call" | custom-call | flops 7549747200 | bytes 17694720 | tf_op jit(solution)/shard_map/pallas_call | solution.py:64
  183.8 4.1 %reshape.165 = bf16[32,12,2560]{2,1,0:T(8,128)(2,1)} reshape(bf16[384,2560]{1,0:T(8,128)(2,1)} %get-tuple-element.13) | data formatting | bytes 3932160 | tf_op jit(solution)/shard_map/reshape | solution.py:159
  187.8 0.0 copy-done.7
  187.8 0.1 fusion.13
  188.0 0.1 convert_element_type.57
  188.1 0.1 reshape.166
  188.2 0.1 fusion.11
  188.3 0.3 copy.54
  188.5 4.3 %maximum_maximum_fusion = bf16[32,16,2560]{2,1,0:T(8,128)(2,1)} fusion(bf16[32,1,2560]{2,1,0:T(2,128)(2,1)S(1)} %copy.54, bf16[32,12,2560]{2,1,0:T(8,128)(2,1)} %reshape.165, bf16[16]{0:T(256)(128)(2,1)S(1)} %pad.7.clone), kind=kLoop, calls=%fused_computation.9 | loop fusion | flops 7864320 | bytes 4751392 | tf_op jit(solution)/shard_map/concatenate | solution.py:157
  192.8 0.0 all-to-all-done.2
  192.8 1.5 copy-done
  194.3 7.4 %all-to-all-start.3 = ((bf16[32,16,2560]{2,1,0:T(8,128)(2,1)}), bf16[32,16,2560]{2,1,0:T(8,128)(2,1)S(1)}, u32[]{:S(2)}, u32[]{:S(2)}) async-start(bf16[32,16,2560]{2,1,0:T(8,128)(2,1)} %maximum_maximum_fusion), calls=%async_computation.3 | async-start | bytes 5242880 | tf_op jit(solution)/shard_map/all_to_all | solution.py:165
  201.7 0.1 sub.19
  201.9 0.0 copy-start.5
  201.9 0.1 sub.24
  202.0 0.1 copy.43
  202.1 0.1 copy.51
  202.2 0.3 copy-done.5
  202.5 0.5 select_reduce_fusion.1
  203.0 4.0 %convolution_add_fusion.1 = f32[128,2560]{1,0:T(8,128)} fusion(f32[128,512]{1,0:T(8,128)S(1)} %get-tuple-element.17, bf16[512,2560]{1,0:T(8,128)(2,1)} %bitcast.68, bf16[1,128,2560]{2,1,0:T(8,128)(2,1)S(1)} %copy-done.1), kind=kOutput, calls=%fused_computation.4 | convolution fusion | flops 2013921280 | bytes 4849664 | tf_op jit(solution)/shard_map/dot_general | solution.py:170
  207.0 30.9 %all-to-all-done.3 = bf16[32,16,2560]{2,1,0:T(8,128)(2,1)S(1)} async-done(((bf16[32,16,2560]{2,1,0:T(8,128)(2,1)}), bf16[32,16,2560]{2,1,0:T(8,128)(2,1)S(1)}, u32[]{:S(2)}, u32[]{:S(2)}) %all-to-all-start.3) | async-done | bytes 2621472 | tf_op jit(solution)/shard_map/all_to_all | solution.py:165
  237.9 3.4 %fusion.1 = bf16[1,128,2560]{2,1,0:T(8,128)(2,1)} fusion(f32[128,2560]{1,0:T(8,128)} %convolution_add_fusion.1, f32[128,512]{1,0:T(8,128)S(1)} %get-tuple-element.16, bf16[512,2560]{1,0:T(8,128)(2,1)S(1)} %bitcast.67), kind=kOutput, calls=%fused_computation.6 | convolution fusion | flops 2013921280 | bytes 4849664 | tf_op jit(solution)/shard_map/dot_general | solution.py:170
  241.3 1.3 collective-permute-start
  242.6 0.0 copy-done.4
  242.6 0.0 copy-done.6
  242.6 0.1 copy.56
  242.7 0.1 fusion.17
  242.8 0.1 reshape.168
  242.9 1.1 select_reduce_fusion
  243.9 14.1 %collective-permute-done = bf16[1,128,2560]{2,1,0:T(8,128)(2,1)S(1)} collective-permute-done((bf16[1,128,2560]{2,1,0:T(8,128)(2,1)}, bf16[1,128,2560]{2,1,0:T(8,128)(2,1)S(1)}, u32[]{:S(2)}, u32[]{:S(2)}) %collective-permute-start) | collective-permute-done | bytes 655392 | tf_op jit(solution)/shard_map/ppermute | solution.py:11
  258.1 0.8 copy.77
  (17 shorter events, 0.1 us)
Async XLA Ops:
  1.4 9.0 %copy-start.3 = (s32[1,128,6]{2,1,0:T(8,128)}, s32[1,128,6]{2,1,0:T(8,128)S(1)}, u32[]{:S(2)}) copy-start(s32[1,128,6]{2,1,0:T(8,128)S(1)} %copy.40) | copy-start | bytes 9220
  10.4 9.5 %copy-start.1 = (bf16[1,128,2560]{2,1,0:T(8,128)(2,1)S(1)}, bf16[1,128,2560]{2,1,0:T(8,128)(2,1)}, u32[]{:S(2)}) copy-start(bf16[1,128,2560]{2,1,0:T(8,128)(2,1)} %param.7) | copy-start | bytes 1966084
  10.4 74.6 %all-to-all-start = ((bf16[32,16,5120]{2,1,0:T(8,128)(2,1)}), bf16[32,16,5120]{2,1,0:T(8,128)(2,1)}, u32[]{:S(2)}, u32[]{:S(2)}) async-start(bf16[32,16,5120]{2,1,0:T(8,128)(2,1)} %bitcast.65), calls=%async_computation | async-start | bytes 10485760 | tf_op jit(solution)/shard_map/all_to_all | solution.py:138
  19.9 1.2 copy-start.2
  85.0 55.8 %all-to-all-start.1 = ((bf16[32,24,2560]{2,1,0:T(8,128)(2,1)}), bf16[32,24,2560]{2,1,0:T(8,128)(2,1)}, u32[]{:S(2)}, u32[]{:S(2)}) async-start(bf16[32,24,2560]{2,1,0:T(8,128)(2,1)} %bitcast.66), calls=%async_computation.1 | async-start | bytes 7864320 | tf_op jit(solution)/shard_map/all_to_all | solution.py:139
  151.5 41.3 %all-to-all-start.2 = ((bf16[32,16,2560]{2,1,0:T(8,128)(2,1)}), bf16[32,16,2560]{2,1,0:T(8,128)(2,1)S(1)}, u32[]{:S(2)}, u32[]{:S(2)}) async-start(bf16[32,16,2560]{2,1,0:T(8,128)(2,1)} %bitcast.71), calls=%async_computation.2 | async-start | bytes 5242880 | tf_op jit(solution)/shard_map/all_to_all | solution.py:142
  183.8 4.1 %copy-start.7 = (f32[384,128]{1,0:T(8,128)S(1)}, f32[384,128]{1,0:T(8,128)}, u32[]{:S(2)}) copy-start(f32[384,128]{1,0:T(8,128)} %get-tuple-element.15) | copy-start | bytes 589828
  192.8 9.3 %copy-start.8 = (f32[1,128,6]{1,0,2:T(1,128)S(1)}, f32[1,128,6]{1,0,2:T(1,128)}, u32[]{:S(2)}) copy-start(f32[1,128,6]{1,0,2:T(1,128)} %param.10) | copy-start | bytes 9220
  192.8 1.5 copy-start
  194.3 43.6 %all-to-all-start.3 = ((bf16[32,16,2560]{2,1,0:T(8,128)(2,1)}), bf16[32,16,2560]{2,1,0:T(8,128)(2,1)S(1)}, u32[]{:S(2)}, u32[]{:S(2)}) async-start(bf16[32,16,2560]{2,1,0:T(8,128)(2,1)} %maximum_maximum_fusion), calls=%async_computation.3 | async-start | bytes 5242880 | tf_op jit(solution)/shard_map/all_to_all | solution.py:165
  201.9 0.6 copy-start.5
  207.0 35.5 %copy-start.4 = (s32[1,128,6]{2,1,0:T(8,128)S(1)}, s32[1,128,6]{2,1,0:T(8,128)}, u32[]{:S(2)}) copy-start(s32[1,128,6]{2,1,0:T(8,128)} %copy-done.3) | copy-start | bytes 9220
  237.9 4.7 %copy-start.6 = (s32[128,6]{1,0:T(8,128)S(1)}, s32[128,6]{1,0:T(8,128)}, u32[]{:S(2)}) copy-start(s32[128,6]{1,0:T(8,128)} %copy-done.5) | copy-start | bytes 9220
  241.3 16.8 %collective-permute-start = (bf16[1,128,2560]{2,1,0:T(8,128)(2,1)}, bf16[1,128,2560]{2,1,0:T(8,128)(2,1)S(1)}, u32[]{:S(2)}, u32[]{:S(2)}) collective-permute-start(bf16[1,128,2560]{2,1,0:T(8,128)(2,1)} %fusion.1), channel_id=1, source_target_pairs={{32,0},{64,32},{96,64},{33,1},{65,33},{97,65},{34,2},{66,34},{98,6... | collective-permute-start | bytes 1966088 | tf_op jit(solution)/shard_map/ppermute | solution.py:11

commit v6 on v5

--- a/solution.py
+++ b/solution.py
@@ -142,12 +142,10 @@
     returned_a = lax.all_to_all(
         back_a.reshape(peer_count, chunk, model_width), "expert", 0, 0, tiled=True
     ).reshape(rows, model_width)
-    arrived_b = jnp.concatenate(
-        [
-            arrived_b[:, :rest].reshape(peer_count * rest, model_width),
-            arrived_b[:, rest:].reshape(peer_count * rest, model_width),
-        ],
-        axis=1,
+    arrived_b = (
+        arrived_b.reshape(peer_count, 2, rest, model_width)
+        .transpose(0, 2, 1, 3)
+        .reshape(peer_count * rest, 2 * model_width)
     )
     back_b, gate_b = expert_call(arrived_b, gate_matrix, up_matrix, down_matrix, tile=128)
     gates = jnp.concatenate(

time: 260 us -> 250 us (0.962)
  other arithmetic: 14.1 us -> 8.02 us
  local copies, waits for them, and re-layouts: 21.6 us -> 17.6 us
    reshape x2 -> x0, local copies, waits for them, and re-layouts: 5.99 us -> none  [the longest x1 4.02 us: body(): arrived_b[:, :rest].reshape(peer_count * rest, model_width)]
    slice x2 -> x1, local copies, waits for them, and re-layouts: 5.04 us -> 0.26 us  [the longest x1 4.78 us: body(): arrived_b[:, :rest].reshape(peer_count * rest, model_width)]
    concatenate x1 -> x0, other arithmetic: 4.42 us -> none  [body(): jnp.concatenate([arrived_b[:, :rest].reshape(peer_count * rest, model_wid...]
    transpose x0 -> x1, local copies, waits for them, and re-layouts: none -> 4.04 us  [body(): arrived_b = arrived_b.reshape(peer_count, 2, rest, model_width).transpose...]
    optimization_barrier x0 -> x1, local copies, waits for them, and re-layouts: none -> 3.26 us  [body(): lax.optimization_barrier((back_a, gate_a, arrived_b))]
  transfers between devices with their start and end apart: 5 -> 5, of which waited for: 4 -> 4; matrix products, arithmetic and copies ran while one was open for 10% -> 11% of each run, Pallas kernels for 17% -> 17%
where the time goes in v6:
time: 250 us
  waiting for transfers between devices  135 us (54%)
  Pallas kernels  43.6 us (17%)
  starting transfers between devices  27.3 us (11%)
  local copies, waits for them, and re-layouts  17.6 us (7%)
  matrix products  16.9 us (7%)
  other arithmetic  8.02 us (3%)
    all_to_all x1, waiting for transfers between devices, body(): lax.all_to_all(send_a, 'expert', 0, 0, tiled=True)  60.7 us
    pallas_call x2, Pallas kernels, expert_call(): pl.pallas_call(expert_kernel, grid=(steps,), in_specs=[pl.BlockSpec((tile...  43.6 us
    all_to_all x1, waiting for transfers between devices, body(): returned_b = lax.all_to_all(back_b, 'expert', 0, 0, tiled=True)  30.7 us
    all_to_all x1, waiting for transfers between devices, body(): arrived_b = lax.all_to_all(send_b, 'expert', 0, 0, tiled=True)  29.8 us
    ppermute x1, waiting for transfers between devices, passed_along(): lax.ppermute(value, axis, [(source, source + steps) for source in range(f...  14.2 us
    all_to_all x1, starting transfers between devices, body(): lax.all_to_all(send_a, 'expert', 0, 0, tiled=True)  8.69 us
    all_to_all x1, starting transfers between devices, body(): returned_b = lax.all_to_all(back_b, 'expert', 0, 0, tiled=True)  7.5 us
    dot_general x2, matrix products, weighted(): jnp.dot(weights, returned.astype(jnp.float32), precision=lax.Precision.HI...  7.37 us
  transfers between devices with their start and end apart: 5, of which 4 were waited for; matrix products, arithmetic and copies ran while one was open for 11% of the time, Pallas kernels for 17%

profile of v6, /device:TPU:0, one launch (start us, length us, event | category | flops | bytes accessed | tf_op | source)
XLA Modules:
  0.0 249.7 jit_solution(15234072027732798982)
XLA Ops:
  0.6 0.8 copy.55
  1.4 0.0 copy-start.2
  1.4 0.1 eq.113
  1.6 0.1 eq.109
  1.7 1.7 reduce-window.6
  3.5 0.3 slice_reduce_fusion
  3.8 0.1 fusion.15
  3.9 0.1 sub.20
  4.0 0.1 copy.61
  4.1 0.2 sub.23
  4.2 0.1 copy.64
  4.3 0.7 compare_select_fusion
  5.0 0.2 fusion.4
  5.3 5.1 %convolution_convert_fusion = bf16[512,5120]{1,0:T(8,128)(2,1)} fusion(pred[512,128]{1,0:T(8,128)(4,1)S(1)} %fusion.4, bf16[128,2560]{1,0:T(8,128)(2,1)} %bitcast.79, bf16[128,2560]{1,0:T(8,128)(2,1)} %bitcast.76), kind=kOutput, calls=%fused_computation.1 | convolution fusion | flops 676331520 | bytes 6619136 | tf_op jit(solution)/shard_map/dot_general | solution.py:123
  10.4 0.0 copy-done.2
  10.4 8.7 %all-to-all-start = ((bf16[32,16,5120]{2,1,0:T(8,128)(2,1)}), bf16[32,16,5120]{2,1,0:T(8,128)(2,1)}, u32[]{:S(2)}, u32[]{:S(2)}) async-start(bf16[32,16,5120]{2,1,0:T(8,128)(2,1)} %bitcast.71), calls=%async_computation | async-start | bytes 10485760 | tf_op jit(solution)/shard_map/all_to_all | solution.py:138
  19.1 0.4 fusion.2
  19.5 0.4 fusion.3
  19.9 0.0 copy-done
  19.9 0.0 copy-start.1
  19.9 1.2 fusion.22
  21.1 0.0 copy-done.1
  21.1 3.2 %add_convert_fusion = bf16[768,2560]{1,0:T(8,128)(2,1)} fusion(f32[768,2560]{1,0:T(8,128)S(1)} %fusion.22, pred[768,128]{1,0:T(8,128)(4,1)S(1)} %fusion.3, bf16[1,128,2560]{2,1,0:T(8,128)(2,1)S(1)} %copy-done.1), kind=kOutput, calls=%fused_computation | convolution fusion | flops 507248640 | bytes 12550144 | tf_op jit(solution)/shard_map/dot_general | solution.py:133
  24.3 60.7 %all-to-all-done = bf16[32,16,5120]{2,1,0:T(8,128)(2,1)} async-done(((bf16[32,16,5120]{2,1,0:T(8,128)(2,1)}), bf16[32,16,5120]{2,1,0:T(8,128)(2,1)}, u32[]{:S(2)}, u32[]{:S(2)}) %all-to-all-start) | async-done | bytes 5242912 | tf_op jit(solution)/shard_map/all_to_all | solution.py:138
  85.0 4.8 %all-to-all-start.1 = ((bf16[32,24,2560]{2,1,0:T(8,128)(2,1)}), bf16[32,24,2560]{2,1,0:T(8,128)(2,1)}, u32[]{:S(2)}, u32[]{:S(2)}) async-start(bf16[32,24,2560]{2,1,0:T(8,128)(2,1)} %bitcast.72), calls=%async_computation.1 | async-start | bytes 7864320 | tf_op jit(solution)/shard_map/all_to_all | solution.py:139
  89.8 20.0 %shard_map.86 = (bf16[512,2560]{1,0:T(8,128)(2,1)}, f32[512,128]{1,0:T(8,128)}) custom-call(bf16[512,5120]{1,0:T(8,128)(2,1)} %bitcast.4.grad_ref.input_ref, bf16[512,5120]{1,0:T(8,128)(2,1)} %bitcast.4.grad_ref.input_ref, bf16[2560,768]{1,0:T(8,128)(2,1)} %bitcast.85, bf16[2560,768]{1,0:T(8,128)(2,1)} %bitcast.87, bf16[768,2560]{1,0:T(8,128)(2,1)} %bitcast.89), custom_call_target="tpu_custom_call" | custom-call | flops 10066329600 | bytes 19660800 | tf_op jit(solution)/shard_map/pallas_call | solution.py:64
  109.8 1.1 fusion.12
  110.9 29.8 %all-to-all-done.1 = bf16[32,24,2560]{2,1,0:T(8,128)(2,1)} async-done(((bf16[32,24,2560]{2,1,0:T(8,128)(2,1)}), bf16[32,24,2560]{2,1,0:T(8,128)(2,1)}, u32[]{:S(2)}, u32[]{:S(2)}) %all-to-all-start.1) | async-done | bytes 3932192 | tf_op jit(solution)/shard_map/all_to_all | solution.py:139
  140.8 5.0 %all-to-all-start.2 = ((bf16[32,16,2560]{2,1,0:T(8,128)(2,1)}), bf16[32,16,2560]{2,1,0:T(8,128)(2,1)}, u32[]{:S(2)}, u32[]{:S(2)}) async-start(bf16[32,16,2560]{2,1,0:T(8,128)(2,1)} %bitcast.80), calls=%async_computation.2 | async-start | bytes 5242880 | tf_op jit(solution)/shard_map/all_to_all | solution.py:142
  145.8 0.1 pad.7.clone
  145.8 3.3 %copy.69 = bf16[32,24,2560]{2,0,1:T(8,128)(2,1)S(1)} copy(bf16[32,24,2560]{2,1,0:T(8,128)(2,1)} %all-to-all-done.1) | data formatting | bytes 7864320 | tf_op jit(solution)/shard_map/optimization_barrier | solution.py:141
  149.1 4.0 %copy.70 = bf16[32,12,2,2560]{3,2,1,0:T(2,128)(2,1)S(1)} copy(bf16[32,12,2,2560]{3,0,1,2:T(8,128)(2,1)S(1)} %bitcast.73) | data formatting | bytes 7864320 | tf_op jit(solution)/shard_map/transpose | solution.py:147
  153.2 2.6 %copy.80 = bf16[48,8,2,2560]{3,1,2,0:T(8,128)(2,1)} copy(bf16[48,8,2,2560]{3,2,1,0:T(2,128)(2,1)S(1)} %bitcast.74) | data formatting | bytes 7864320
  155.7 23.6 %shard_map.87 = (bf16[384,2560]{1,0:T(8,128)(2,1)}, f32[384,128]{1,0:T(8,128)}) custom-call(bf16[384,5120]{1,0:T(8,128)(2,1)} %bitcast.77, bf16[384,5120]{1,0:T(8,128)(2,1)} %bitcast.78, bf16[2560,768]{1,0:T(8,128)(2,1)} %bitcast.86, bf16[2560,768]{1,0:T(8,128)(2,1)} %bitcast.88, bf16[768,2560]{1,0:T(8,128)(2,1)} %bitcast.90), custom_call_target="tpu_custom_call" | custom-call | flops 7549747200 | bytes 17694720 | tf_op jit(solution)/shard_map/pallas_call | solution.py:64
  179.3 2.5 %reshape.165 = bf16[32,12,2560]{2,1,0:T(8,128)(2,1)S(1)} reshape(bf16[384,2560]{1,0:T(8,128)(2,1)} %get-tuple-element.13) | data formatting | bytes 3932160 | tf_op jit(solution)/shard_map/reshape | solution.py:157
  181.9 0.0 copy-done.6
  181.9 0.1 fusion.13
  182.0 0.1 convert_element_type.57
  182.1 0.1 reshape.166
  182.2 0.1 fusion.11
  182.3 0.3 copy.71
  182.6 2.6 %maximum_maximum_fusion = bf16[32,16,2560]{2,1,0:T(8,128)(2,1)} fusion(bf16[32,1,2560]{2,1,0:T(2,128)(2,1)S(1)} %copy.71, bf16[32,12,2560]{2,1,0:T(8,128)(2,1)S(1)} %reshape.165, bf16[16]{0:T(256)(128)(2,1)S(1)} %pad.7.clone), kind=kLoop, calls=%fused_computation.8 | loop fusion | flops 7864320 | bytes 4751392 | tf_op jit(solution)/shard_map/concatenate | solution.py:155
  185.2 0.0 all-to-all-done.2
  185.2 7.5 %all-to-all-start.3 = ((bf16[32,16,2560]{2,1,0:T(8,128)(2,1)}), bf16[32,16,2560]{2,1,0:T(8,128)(2,1)S(1)}, u32[]{:S(2)}, u32[]{:S(2)}) async-start(bf16[32,16,2560]{2,1,0:T(8,128)(2,1)} %maximum_maximum_fusion), calls=%async_computation.3 | async-start | bytes 5242880 | tf_op jit(solution)/shard_map/all_to_all | solution.py:163
  192.7 0.1 sub.19
  192.8 0.0 copy-start.4
  192.8 0.1 sub.24
  193.0 0.1 copy.58
  193.0 0.1 copy.66
  193.1 0.0 copy-done.7
  193.2 0.3 copy-done.4
  193.5 0.5 select_reduce_fusion.1
  194.0 4.0 %convolution_add_fusion.1 = f32[128,2560]{1,0:T(8,128)} fusion(f32[128,512]{1,0:T(8,128)S(1)} %get-tuple-element.17, bf16[512,2560]{1,0:T(8,128)(2,1)} %bitcast.10, bf16[1,128,2560]{2,1,0:T(8,128)(2,1)S(1)} %copy-done), kind=kOutput, calls=%fused_computation.3 | convolution fusion | flops 2013921280 | bytes 4849664 | tf_op jit(solution)/shard_map/dot_general | solution.py:168
  198.0 30.7 %all-to-all-done.3 = bf16[32,16,2560]{2,1,0:T(8,128)(2,1)S(1)} async-done(((bf16[32,16,2560]{2,1,0:T(8,128)(2,1)}), bf16[32,16,2560]{2,1,0:T(8,128)(2,1)S(1)}, u32[]{:S(2)}, u32[]{:S(2)}) %all-to-all-start.3) | async-done | bytes 2621472 | tf_op jit(solution)/shard_map/all_to_all | solution.py:163
  228.7 3.4 %fusion.1 = bf16[1,128,2560]{2,1,0:T(8,128)(2,1)} fusion(f32[128,2560]{1,0:T(8,128)} %convolution_add_fusion.1, f32[128,512]{1,0:T(8,128)S(1)} %get-tuple-element.16, bf16[512,2560]{1,0:T(8,128)(2,1)S(1)} %bitcast.75), kind=kOutput, calls=%fused_computation.5 | convolution fusion | flops 2013921280 | bytes 4849664 | tf_op jit(solution)/shard_map/dot_general | solution.py:168
  232.0 1.3 collective-permute-start
  233.3 0.0 copy-done.3
  233.3 0.0 copy-done.5
  233.4 0.1 copy.73
  233.4 0.1 fusion.17
  233.5 0.1 reshape.168
  233.6 1.1 select_reduce_fusion
  234.7 14.2 %collective-permute-done = bf16[1,128,2560]{2,1,0:T(8,128)(2,1)S(1)} collective-permute-done((bf16[1,128,2560]{2,1,0:T(8,128)(2,1)}, bf16[1,128,2560]{2,1,0:T(8,128)(2,1)S(1)}, u32[]{:S(2)}, u32[]{:S(2)}) %collective-permute-start) | collective-permute-done | bytes 655392 | tf_op jit(solution)/shard_map/ppermute | solution.py:11
  248.8 0.8 copy.95
  (14 shorter events, 0.1 us)
Async XLA Ops:
  1.4 9.0 %copy-start.2 = (s32[1,128,6]{2,1,0:T(8,128)}, s32[1,128,6]{2,1,0:T(8,128)S(1)}, u32[]{:S(2)}) copy-start(s32[1,128,6]{2,1,0:T(8,128)S(1)} %copy.55) | copy-start | bytes 9220
  10.4 9.5 %copy-start = (bf16[1,128,2560]{2,1,0:T(8,128)(2,1)S(1)}, bf16[1,128,2560]{2,1,0:T(8,128)(2,1)}, u32[]{:S(2)}) copy-start(bf16[1,128,2560]{2,1,0:T(8,128)(2,1)} %param.7) | copy-start | bytes 1966084
  10.4 74.6 %all-to-all-start = ((bf16[32,16,5120]{2,1,0:T(8,128)(2,1)}), bf16[32,16,5120]{2,1,0:T(8,128)(2,1)}, u32[]{:S(2)}, u32[]{:S(2)}) async-start(bf16[32,16,5120]{2,1,0:T(8,128)(2,1)} %bitcast.71), calls=%async_computation | async-start | bytes 10485760 | tf_op jit(solution)/shard_map/all_to_all | solution.py:138
  19.9 1.2 copy-start.1
  85.0 55.8 %all-to-all-start.1 = ((bf16[32,24,2560]{2,1,0:T(8,128)(2,1)}), bf16[32,24,2560]{2,1,0:T(8,128)(2,1)}, u32[]{:S(2)}, u32[]{:S(2)}) async-start(bf16[32,24,2560]{2,1,0:T(8,128)(2,1)} %bitcast.72), calls=%async_computation.1 | async-start | bytes 7864320 | tf_op jit(solution)/shard_map/all_to_all | solution.py:139
  140.8 44.4 %all-to-all-start.2 = ((bf16[32,16,2560]{2,1,0:T(8,128)(2,1)}), bf16[32,16,2560]{2,1,0:T(8,128)(2,1)}, u32[]{:S(2)}, u32[]{:S(2)}) async-start(bf16[32,16,2560]{2,1,0:T(8,128)(2,1)} %bitcast.80), calls=%async_computation.2 | async-start | bytes 5242880 | tf_op jit(solution)/shard_map/all_to_all | solution.py:142
  179.3 2.5 %copy-start.6 = (f32[384,128]{1,0:T(8,128)S(1)}, f32[384,128]{1,0:T(8,128)}, u32[]{:S(2)}) copy-start(f32[384,128]{1,0:T(8,128)} %get-tuple-element.15) | copy-start | bytes 589828
  185.2 7.9 %copy-start.7 = (f32[1,128,6]{1,0,2:T(1,128)S(1)}, f32[1,128,6]{1,0,2:T(1,128)}, u32[]{:S(2)}) copy-start(f32[1,128,6]{1,0,2:T(1,128)} %param.10) | copy-start | bytes 9220
  185.2 43.5 %all-to-all-start.3 = ((bf16[32,16,2560]{2,1,0:T(8,128)(2,1)}), bf16[32,16,2560]{2,1,0:T(8,128)(2,1)S(1)}, u32[]{:S(2)}, u32[]{:S(2)}) async-start(bf16[32,16,2560]{2,1,0:T(8,128)(2,1)} %maximum_maximum_fusion), calls=%async_computation.3 | async-start | bytes 5242880 | tf_op jit(solution)/shard_map/all_to_all | solution.py:163
  192.8 0.6 copy-start.4
  198.0 35.4 %copy-start.3 = (s32[1,128,6]{2,1,0:T(8,128)S(1)}, s32[1,128,6]{2,1,0:T(8,128)}, u32[]{:S(2)}) copy-start(s32[1,128,6]{2,1,0:T(8,128)} %copy-done.2) | copy-start | bytes 9220
  228.7 4.7 %copy-start.5 = (s32[128,6]{1,0:T(8,128)S(1)}, s32[128,6]{1,0:T(8,128)}, u32[]{:S(2)}) copy-start(s32[128,6]{1,0:T(8,128)} %copy-done.4) | copy-start | bytes 9220
  232.0 16.8 %collective-permute-start = (bf16[1,128,2560]{2,1,0:T(8,128)(2,1)}, bf16[1,128,2560]{2,1,0:T(8,128)(2,1)S(1)}, u32[]{:S(2)}, u32[]{:S(2)}) collective-permute-start(bf16[1,128,2560]{2,1,0:T(8,128)(2,1)} %fusion.1), channel_id=1, source_target_pairs={{32,0},{64,32},{96,64},{33,1},{65,33},{97,65},{34,2},{66,34},{98,6... | collective-permute-start | bytes 1966088 | tf_op jit(solution)/shard_map/ppermute | solution.py:11

commit v7 on v6

--- a/solution.py
+++ b/solution.py
@@ -147,7 +147,7 @@
         .transpose(0, 2, 1, 3)
         .reshape(peer_count * rest, 2 * model_width)
     )
-    back_b, gate_b = expert_call(arrived_b, gate_matrix, up_matrix, down_matrix, tile=128)
+    back_b, gate_b = expert_call(arrived_b, gate_matrix, up_matrix, down_matrix, tile=192)
     gates = jnp.concatenate(
         [gate_a.reshape(peer_count, chunk), gate_b.reshape(peer_count, rest)], axis=1
     )

time: 250 us -> 246 us (0.984)
  Pallas kernels: 43.6 us -> 39 us
    pallas_call x2, Pallas kernels: 43.6 us -> 39 us  [expert_call(): pl.pallas_call(expert_kernel, grid=(steps,), in_specs=[pl.BlockSpec((tile...]
  transfers between devices with their start and end apart: 5 -> 5, of which waited for: 4 -> 5; matrix products, arithmetic and copies ran while one was open for 11% -> 12% of each run, Pallas kernels for 17% -> 16%
where the time goes in v7:
time: 246 us; the launch traced here: 245 us
  waiting for transfers between devices  137 us (56%)
  Pallas kernels  39 us (16%)
  starting transfers between devices  25.9 us (11%)
  local copies, waits for them, and re-layouts  17.6 us (7%)
  matrix products  16.9 us (7%)
  other arithmetic  8.02 us (3%)
    all_to_all x1, waiting for transfers between devices, body(): lax.all_to_all(send_a, 'expert', 0, 0, tiled=True)  60.7 us
    pallas_call x2, Pallas kernels, expert_call(): pl.pallas_call(expert_kernel, grid=(steps,), in_specs=[pl.BlockSpec((tile...  39 us
    all_to_all x1, waiting for transfers between devices, body(): returned_b = lax.all_to_all(back_b, 'expert', 0, 0, tiled=True)  30.9 us
    all_to_all x1, waiting for transfers between devices, body(): arrived_b = lax.all_to_all(send_b, 'expert', 0, 0, tiled=True)  29.8 us
    ppermute x1, waiting for transfers between devices, passed_along(): lax.ppermute(value, axis, [(source, source + steps) for source in range(f...  14.1 us
    all_to_all x1, starting transfers between devices, body(): lax.all_to_all(send_a, 'expert', 0, 0, tiled=True)  8.69 us
    dot_general x2, matrix products, weighted(): jnp.dot(weights, returned.astype(jnp.float32), precision=lax.Precision.HI...  7.37 us
    all_to_all x1, starting transfers between devices, body(): returned_b = lax.all_to_all(back_b, 'expert', 0, 0, tiled=True)  6.12 us
  transfers between devices with their start and end apart: 5, of which 5 were waited for; matrix products, arithmetic and copies ran while one was open for 12% of the time, Pallas kernels for 16%

profile of v7, /device:TPU:0, one launch (start us, length us, event | category | flops | bytes accessed | tf_op | source)
XLA Modules:
  0.0 245.1 jit_solution(13404933769391807626)
XLA Ops:
  0.6 0.8 copy.55
  1.4 0.0 copy-start.2
  1.4 0.1 eq.113
  1.6 0.1 eq.109
  1.7 1.7 reduce-window.6
  3.5 0.3 slice_reduce_fusion
  3.8 0.1 fusion.15
  3.9 0.1 sub.20
  4.0 0.1 copy.61
  4.1 0.2 sub.23
  4.2 0.1 copy.64
  4.3 0.7 compare_select_fusion
  5.0 0.2 fusion.4
  5.3 5.1 %convolution_convert_fusion = bf16[512,5120]{1,0:T(8,128)(2,1)} fusion(pred[512,128]{1,0:T(8,128)(4,1)S(1)} %fusion.4, bf16[128,2560]{1,0:T(8,128)(2,1)} %bitcast.79, bf16[128,2560]{1,0:T(8,128)(2,1)} %bitcast.76), kind=kOutput, calls=%fused_computation.1 | convolution fusion | flops 676331520 | bytes 6619136 | tf_op jit(solution)/shard_map/dot_general | solution.py:123
  10.4 0.0 copy-done.2
  10.4 8.7 %all-to-all-start = ((bf16[32,16,5120]{2,1,0:T(8,128)(2,1)}), bf16[32,16,5120]{2,1,0:T(8,128)(2,1)}, u32[]{:S(2)}, u32[]{:S(2)}) async-start(bf16[32,16,5120]{2,1,0:T(8,128)(2,1)} %bitcast.71), calls=%async_computation | async-start | bytes 10485760 | tf_op jit(solution)/shard_map/all_to_all | solution.py:138
  19.1 0.4 fusion.2
  19.5 0.4 fusion.3
  19.9 0.0 copy-done
  19.9 0.0 copy-start.1
  19.9 1.2 fusion.22
  21.1 0.0 copy-done.1
  21.1 3.2 %add_convert_fusion = bf16[768,2560]{1,0:T(8,128)(2,1)} fusion(f32[768,2560]{1,0:T(8,128)S(1)} %fusion.22, pred[768,128]{1,0:T(8,128)(4,1)S(1)} %fusion.3, bf16[1,128,2560]{2,1,0:T(8,128)(2,1)S(1)} %copy-done.1), kind=kOutput, calls=%fused_computation | convolution fusion | flops 507248640 | bytes 12550144 | tf_op jit(solution)/shard_map/dot_general | solution.py:133
  24.3 60.7 %all-to-all-done = bf16[32,16,5120]{2,1,0:T(8,128)(2,1)} async-done(((bf16[32,16,5120]{2,1,0:T(8,128)(2,1)}), bf16[32,16,5120]{2,1,0:T(8,128)(2,1)}, u32[]{:S(2)}, u32[]{:S(2)}) %all-to-all-start) | async-done | bytes 5242912 | tf_op jit(solution)/shard_map/all_to_all | solution.py:138
  85.0 4.8 %all-to-all-start.1 = ((bf16[32,24,2560]{2,1,0:T(8,128)(2,1)}), bf16[32,24,2560]{2,1,0:T(8,128)(2,1)}, u32[]{:S(2)}, u32[]{:S(2)}) async-start(bf16[32,24,2560]{2,1,0:T(8,128)(2,1)} %bitcast.72), calls=%async_computation.1 | async-start | bytes 7864320 | tf_op jit(solution)/shard_map/all_to_all | solution.py:139
  89.8 20.0 %shard_map.86 = (bf16[512,2560]{1,0:T(8,128)(2,1)}, f32[512,128]{1,0:T(8,128)}) custom-call(bf16[512,5120]{1,0:T(8,128)(2,1)} %bitcast.4.grad_ref.input_ref, bf16[512,5120]{1,0:T(8,128)(2,1)} %bitcast.4.grad_ref.input_ref, bf16[2560,768]{1,0:T(8,128)(2,1)} %bitcast.85, bf16[2560,768]{1,0:T(8,128)(2,1)} %bitcast.87, bf16[768,2560]{1,0:T(8,128)(2,1)} %bitcast.89), custom_call_target="tpu_custom_call" | custom-call | flops 10066329600 | bytes 19660800 | tf_op jit(solution)/shard_map/pallas_call | solution.py:64
  109.8 1.1 fusion.12
  110.9 29.8 %all-to-all-done.1 = bf16[32,24,2560]{2,1,0:T(8,128)(2,1)} async-done(((bf16[32,24,2560]{2,1,0:T(8,128)(2,1)}), bf16[32,24,2560]{2,1,0:T(8,128)(2,1)}, u32[]{:S(2)}, u32[]{:S(2)}) %all-to-all-start.1) | async-done | bytes 3932192 | tf_op jit(solution)/shard_map/all_to_all | solution.py:139
  140.8 5.0 %all-to-all-start.2 = ((bf16[32,16,2560]{2,1,0:T(8,128)(2,1)}), bf16[32,16,2560]{2,1,0:T(8,128)(2,1)}, u32[]{:S(2)}, u32[]{:S(2)}) async-start(bf16[32,16,2560]{2,1,0:T(8,128)(2,1)} %bitcast.80), calls=%async_computation.2 | async-start | bytes 5242880 | tf_op jit(solution)/shard_map/all_to_all | solution.py:142
  145.8 0.1 pad.7.clone
  145.8 3.3 %copy.69 = bf16[32,24,2560]{2,0,1:T(8,128)(2,1)S(1)} copy(bf16[32,24,2560]{2,1,0:T(8,128)(2,1)} %all-to-all-done.1) | data formatting | bytes 7864320 | tf_op jit(solution)/shard_map/optimization_barrier | solution.py:141
  149.1 4.0 %copy.70 = bf16[32,12,2,2560]{3,2,1,0:T(2,128)(2,1)S(1)} copy(bf16[32,12,2,2560]{3,0,1,2:T(8,128)(2,1)S(1)} %bitcast.73) | data formatting | bytes 7864320 | tf_op jit(solution)/shard_map/transpose | solution.py:147
  153.2 2.6 %copy.80 = bf16[48,8,2,2560]{3,1,2,0:T(8,128)(2,1)} copy(bf16[48,8,2,2560]{3,2,1,0:T(2,128)(2,1)S(1)} %bitcast.74) | data formatting | bytes 7864320
  155.7 19.0 %shard_map.87 = (bf16[384,2560]{1,0:T(8,128)(2,1)}, f32[384,128]{1,0:T(8,128)}) custom-call(bf16[384,5120]{1,0:T(8,128)(2,1)} %bitcast.77, bf16[384,5120]{1,0:T(8,128)(2,1)} %bitcast.78, bf16[2560,768]{1,0:T(8,128)(2,1)} %bitcast.86, bf16[2560,768]{1,0:T(8,128)(2,1)} %bitcast.88, bf16[768,2560]{1,0:T(8,128)(2,1)} %bitcast.90), custom_call_target="tpu_custom_call" | custom-call | flops 7549747200 | bytes 17694720 | tf_op jit(solution)/shard_map/pallas_call | solution.py:64
  174.7 2.5 %reshape.165 = bf16[32,12,2560]{2,1,0:T(8,128)(2,1)S(1)} reshape(bf16[384,2560]{1,0:T(8,128)(2,1)} %get-tuple-element.13) | data formatting | bytes 3932160 | tf_op jit(solution)/shard_map/reshape | solution.py:157
  177.3 0.0 copy-done.6
  177.3 0.1 fusion.13
  177.4 0.1 convert_element_type.57
  177.5 0.1 reshape.166
  177.6 0.1 fusion.11
  177.7 0.3 copy.71
  178.0 2.6 %maximum_maximum_fusion = bf16[32,16,2560]{2,1,0:T(8,128)(2,1)} fusion(bf16[32,1,2560]{2,1,0:T(2,128)(2,1)S(1)} %copy.71, bf16[32,12,2560]{2,1,0:T(8,128)(2,1)S(1)} %reshape.165, bf16[16]{0:T(256)(128)(2,1)S(1)} %pad.7.clone), kind=kLoop, calls=%fused_computation.8 | loop fusion | flops 7864320 | bytes 4751392 | tf_op jit(solution)/shard_map/concatenate | solution.py:155
  180.6 1.2 all-to-all-done.2
  181.7 6.1 %all-to-all-start.3 = ((bf16[32,16,2560]{2,1,0:T(8,128)(2,1)}), bf16[32,16,2560]{2,1,0:T(8,128)(2,1)S(1)}, u32[]{:S(2)}, u32[]{:S(2)}) async-start(bf16[32,16,2560]{2,1,0:T(8,128)(2,1)} %maximum_maximum_fusion), calls=%async_computation.3 | async-start | bytes 5242880 | tf_op jit(solution)/shard_map/all_to_all | solution.py:163
  187.9 0.1 sub.19
  188.0 0.0 copy-start.4
  188.0 0.1 sub.24
  188.2 0.1 copy.58
  188.2 0.1 copy.66
  188.3 0.0 copy-done.7
  188.3 0.3 copy-done.4
  188.6 0.5 select_reduce_fusion.1
  189.2 4.0 %convolution_add_fusion.1 = f32[128,2560]{1,0:T(8,128)} fusion(f32[128,512]{1,0:T(8,128)S(1)} %get-tuple-element.17, bf16[512,2560]{1,0:T(8,128)(2,1)} %bitcast.10, bf16[1,128,2560]{2,1,0:T(8,128)(2,1)S(1)} %copy-done), kind=kOutput, calls=%fused_computation.3 | convolution fusion | flops 2013921280 | bytes 4849664 | tf_op jit(solution)/shard_map/dot_general | solution.py:168
  193.2 30.9 %all-to-all-done.3 = bf16[32,16,2560]{2,1,0:T(8,128)(2,1)S(1)} async-done(((bf16[32,16,2560]{2,1,0:T(8,128)(2,1)}), bf16[32,16,2560]{2,1,0:T(8,128)(2,1)S(1)}, u32[]{:S(2)}, u32[]{:S(2)}) %all-to-all-start.3) | async-done | bytes 2621472 | tf_op jit(solution)/shard_map/all_to_all | solution.py:163
  224.1 3.4 %fusion.1 = bf16[1,128,2560]{2,1,0:T(8,128)(2,1)} fusion(f32[128,2560]{1,0:T(8,128)} %convolution_add_fusion.1, f32[128,512]{1,0:T(8,128)S(1)} %get-tuple-element.16, bf16[512,2560]{1,0:T(8,128)(2,1)S(1)} %bitcast.75), kind=kOutput, calls=%fused_computation.5 | convolution fusion | flops 2013921280 | bytes 4849664 | tf_op jit(solution)/shard_map/dot_general | solution.py:168
  227.4 1.3 collective-permute-start
  228.7 0.0 copy-done.3
  228.7 0.0 copy-done.5
  228.8 0.1 copy.73
  228.8 0.1 fusion.17
  228.9 0.1 reshape.168
  229.0 1.1 select_reduce_fusion
  230.1 14.1 %collective-permute-done = bf16[1,128,2560]{2,1,0:T(8,128)(2,1)S(1)} collective-permute-done((bf16[1,128,2560]{2,1,0:T(8,128)(2,1)}, bf16[1,128,2560]{2,1,0:T(8,128)(2,1)S(1)}, u32[]{:S(2)}, u32[]{:S(2)}) %collective-permute-start) | collective-permute-done | bytes 655392 | tf_op jit(solution)/shard_map/ppermute | solution.py:11
  244.2 0.8 copy.95
  (14 shorter events, 0.1 us)
Async XLA Ops:
  1.4 9.0 %copy-start.2 = (s32[1,128,6]{2,1,0:T(8,128)}, s32[1,128,6]{2,1,0:T(8,128)S(1)}, u32[]{:S(2)}) copy-start(s32[1,128,6]{2,1,0:T(8,128)S(1)} %copy.55) | copy-start | bytes 9220
  10.4 9.5 %copy-start = (bf16[1,128,2560]{2,1,0:T(8,128)(2,1)S(1)}, bf16[1,128,2560]{2,1,0:T(8,128)(2,1)}, u32[]{:S(2)}) copy-start(bf16[1,128,2560]{2,1,0:T(8,128)(2,1)} %param.7) | copy-start | bytes 1966084
  10.4 74.6 %all-to-all-start = ((bf16[32,16,5120]{2,1,0:T(8,128)(2,1)}), bf16[32,16,5120]{2,1,0:T(8,128)(2,1)}, u32[]{:S(2)}, u32[]{:S(2)}) async-start(bf16[32,16,5120]{2,1,0:T(8,128)(2,1)} %bitcast.71), calls=%async_computation | async-start | bytes 10485760 | tf_op jit(solution)/shard_map/all_to_all | solution.py:138
  19.9 1.2 copy-start.1
  85.0 55.8 %all-to-all-start.1 = ((bf16[32,24,2560]{2,1,0:T(8,128)(2,1)}), bf16[32,24,2560]{2,1,0:T(8,128)(2,1)}, u32[]{:S(2)}, u32[]{:S(2)}) async-start(bf16[32,24,2560]{2,1,0:T(8,128)(2,1)} %bitcast.72), calls=%async_computation.1 | async-start | bytes 7864320 | tf_op jit(solution)/shard_map/all_to_all | solution.py:139
  140.8 41.0 %all-to-all-start.2 = ((bf16[32,16,2560]{2,1,0:T(8,128)(2,1)}), bf16[32,16,2560]{2,1,0:T(8,128)(2,1)}, u32[]{:S(2)}, u32[]{:S(2)}) async-start(bf16[32,16,2560]{2,1,0:T(8,128)(2,1)} %bitcast.80), calls=%async_computation.2 | async-start | bytes 5242880 | tf_op jit(solution)/shard_map/all_to_all | solution.py:142
  174.7 2.5 %copy-start.6 = (f32[384,128]{1,0:T(8,128)S(1)}, f32[384,128]{1,0:T(8,128)}, u32[]{:S(2)}) copy-start(f32[384,128]{1,0:T(8,128)} %get-tuple-element.15) | copy-start | bytes 589828
  180.6 7.7 %copy-start.7 = (f32[1,128,6]{1,0,2:T(1,128)S(1)}, f32[1,128,6]{1,0,2:T(1,128)}, u32[]{:S(2)}) copy-start(f32[1,128,6]{1,0,2:T(1,128)} %param.10) | copy-start | bytes 9220
  181.7 42.3 %all-to-all-start.3 = ((bf16[32,16,2560]{2,1,0:T(8,128)(2,1)}), bf16[32,16,2560]{2,1,0:T(8,128)(2,1)S(1)}, u32[]{:S(2)}, u32[]{:S(2)}) async-start(bf16[32,16,2560]{2,1,0:T(8,128)(2,1)} %maximum_maximum_fusion), calls=%async_computation.3 | async-start | bytes 5242880 | tf_op jit(solution)/shard_map/all_to_all | solution.py:163
  188.0 0.6 copy-start.4
  193.1 35.6 %copy-start.3 = (s32[1,128,6]{2,1,0:T(8,128)S(1)}, s32[1,128,6]{2,1,0:T(8,128)}, u32[]{:S(2)}) copy-start(s32[1,128,6]{2,1,0:T(8,128)} %copy-done.2) | copy-start | bytes 9220
  224.1 4.7 %copy-start.5 = (s32[128,6]{1,0:T(8,128)S(1)}, s32[128,6]{1,0:T(8,128)}, u32[]{:S(2)}) copy-start(s32[128,6]{1,0:T(8,128)} %copy-done.4) | copy-start | bytes 9220
  227.4 16.8 %collective-permute-start = (bf16[1,128,2560]{2,1,0:T(8,128)(2,1)}, bf16[1,128,2560]{2,1,0:T(8,128)(2,1)S(1)}, u32[]{:S(2)}, u32[]{:S(2)}) collective-permute-start(bf16[1,128,2560]{2,1,0:T(8,128)(2,1)} %fusion.1), channel_id=1, source_target_pairs={{32,0},{64,32},{96,64},{33,1},{65,33},{97,65},{34,2},{66,34},{98,6... | collective-permute-start | bytes 1966088 | tf_op jit(solution)/shard_map/ppermute | solution.py:11

commit v8 on v7

--- a/solution.py
+++ b/solution.py
@@ -84,6 +84,31 @@
     return back, value[:, 0].astype(jnp.bfloat16)
 
 
+def pick_kernel(pick_ref, rows_ref, out_ref):
+    out_ref[...] = jnp.dot(
+        pick_ref[...], rows_ref[...], preferred_element_type=jnp.float32
+    ).astype(out_ref.dtype)
+
+
+def pick_rows(pick, table, block=1280):
+    count, width = pick.shape[0], table.shape[1]
+    return pl.pallas_call(
+        pick_kernel,
+        grid=(width // block,),
+        in_specs=[
+            pl.BlockSpec(pick.shape, lambda j: (0, 0)),
+            pl.BlockSpec((table.shape[0], block), lambda j: (0, j)),
+        ],
+        out_specs=pl.BlockSpec((count, block), lambda j: (0, j)),
+        out_shape=jax.ShapeDtypeStruct((count, width), table.dtype),
+        cost_estimate=pl.CostEstimate(
+            flops=2 * count * table.shape[0] * width,
+            transcendentals=0,
+            bytes_accessed=2 * (count * table.shape[0] + table.size + count * width),
+        ),
+    )(pick, table)
+
+
 def body(out_grad, layer_input, route_ids, route_probs, gate_weight, up_weight, down_weight):
     grad_tokens = out_grad[0]
     input_tokens = layer_input[0]
@@ -120,8 +145,8 @@
         return pick, weights
 
     pick_a, weights_a = dispatch(0)
-    send_a = jnp.dot(pick_a.astype(jnp.bfloat16), both, preferred_element_type=jnp.float32)
-    send_a = send_a.astype(jnp.bfloat16).reshape(peer_count, chunk, 2 * model_width)
+    send_a = pick_rows(pick_a.astype(jnp.bfloat16), both)
+    send_a = send_a.reshape(peer_count, chunk, 2 * model_width)
     unused, weights_b = dispatch(1)
     rest = capacity - chunk
     local = places - chunk

time: 246 us -> 250 us (1.016)
  Pallas kernels: 39 us -> 44.3 us
  matrix products: 16.9 us -> 11.7 us
  other arithmetic: 8.02 us -> 11.2 us
    pallas_call x0 -> x1, Pallas kernels: none -> 5.29 us  [pick_rows(): pl.pallas_call(pick_kernel, grid=(width // block,), in_specs=[pl.BlockSpe...]
    dot_general x1 -> x0, matrix products: 5.14 us -> none  [body(): jnp.dot(pick_a.astype(jnp.bfloat16), both, preferred_element_type=jnp.flo...]
  transfers between devices with their start and end apart: 5 -> 5, of which waited for: 5 -> 5; matrix products, arithmetic and copies ran while one was open for 12% -> 11% of each run, Pallas kernels for 16% -> 16%
where the time goes in v8:
time: 250 us
  waiting for transfers between devices  137 us (55%)
  Pallas kernels  44.3 us (18%)
  starting transfers between devices  25.9 us (10%)
  local copies, waits for them, and re-layouts  18.7 us (7%)
  matrix products  11.7 us (5%)
  other arithmetic  11.2 us (4%)
    all_to_all x1, waiting for transfers between devices, body(): lax.all_to_all(send_a, 'expert', 0, 0, tiled=True)  60.7 us
    pallas_call x2, Pallas kernels, expert_call(): pl.pallas_call(expert_kernel, grid=(steps,), in_specs=[pl.BlockSpec((tile...  39 us
    all_to_all x1, waiting for transfers between devices, body(): returned_b = lax.all_to_all(back_b, 'expert', 0, 0, tiled=True)  30.9 us
    all_to_all x1, waiting for transfers between devices, body(): arrived_b = lax.all_to_all(send_b, 'expert', 0, 0, tiled=True)  29.8 us
    ppermute x1, waiting for transfers between devices, passed_along(): lax.ppermute(value, axis, [(source, source + steps) for source in range(f...  14.2 us
    all_to_all x1, starting transfers between devices, body(): lax.all_to_all(send_a, 'expert', 0, 0, tiled=True)  8.69 us
    dot_general x2, matrix products, weighted(): jnp.dot(weights, returned.astype(jnp.float32), precision=lax.Precision.HI...  7.34 us
    all_to_all x1, starting transfers between devices, body(): returned_b = lax.all_to_all(back_b, 'expert', 0, 0, tiled=True)  6.12 us
  transfers between devices with their start and end apart: 5, of which 5 were waited for; matrix products, arithmetic and copies ran while one was open for 11% of the time, Pallas kernels for 16%

profile of v8, /device:TPU:0, one launch (start us, length us, event | category | flops | bytes accessed | tf_op | source)
XLA Modules:
  0.0 249.6 jit_solution(5584715035847947656)
XLA Ops:
  0.6 0.8 copy.55
  1.4 0.1 eq.113
  1.6 0.1 eq.109
  1.7 1.7 reduce-window.6
  3.5 0.3 slice_reduce_fusion
  3.8 0.1 fusion.12
  3.9 0.1 sub.20
  4.0 0.1 copy.61
  4.1 0.2 sub.23
  4.2 0.1 copy.64
  4.3 0.7 compare_select_fusion
  5.0 0.2 fusion.4
  5.3 0.7 convert_element_type.53.pick_ref
  5.9 2.5 pad_maximum_fusion.rows_ref
  8.4 5.3 %shard_map.86 = bf16[512,5120]{1,0:T(8,128)(2,1)} custom-call(bf16[512,128]{1,0:T(8,128)(2,1)} %convert_element_type.53.pick_ref, bf16[128,5120]{1,0:T(8,128)(2,1)} %pad_maximum_fusion.rows_ref), custom_call_target="tpu_custom_call" | custom-call | flops 671088640 | bytes 6684672 | tf_op jit(solution)/shard_map/pallas_call | solution.py:95
  13.7 0.0 copy-done.2
  13.7 8.7 %all-to-all-start = ((bf16[32,16,5120]{2,1,0:T(8,128)(2,1)}), bf16[32,16,5120]{2,1,0:T(8,128)(2,1)}, u32[]{:S(2)}, u32[]{:S(2)}) async-start(bf16[32,16,5120]{2,1,0:T(8,128)(2,1)} %bitcast.70), calls=%async_computation | async-start | bytes 10485760 | tf_op jit(solution)/shard_map/all_to_all | solution.py:163
  22.4 0.4 fusion.2
  22.8 0.4 fusion.3
  23.2 0.0 copy-done
  23.2 0.0 copy-start.1
  23.2 1.2 fusion.18
  24.4 0.0 copy-done.1
  24.4 3.2 %add_convert_fusion = bf16[768,2560]{1,0:T(8,128)(2,1)} fusion(f32[768,2560]{1,0:T(8,128)S(1)} %fusion.18, pred[768,128]{1,0:T(8,128)(4,1)S(1)} %fusion.3, bf16[1,128,2560]{2,1,0:T(8,128)(2,1)S(1)} %copy-done.1), kind=kOutput, calls=%fused_computation | convolution fusion | flops 507248640 | bytes 12550144 | tf_op jit(solution)/shard_map/dot_general | solution.py:158
  27.6 60.7 %all-to-all-done = bf16[32,16,5120]{2,1,0:T(8,128)(2,1)} async-done(((bf16[32,16,5120]{2,1,0:T(8,128)(2,1)}), bf16[32,16,5120]{2,1,0:T(8,128)(2,1)}, u32[]{:S(2)}, u32[]{:S(2)}) %all-to-all-start) | async-done | bytes 5242912 | tf_op jit(solution)/shard_map/all_to_all | solution.py:163
  88.3 4.8 %all-to-all-start.1 = ((bf16[32,24,2560]{2,1,0:T(8,128)(2,1)}), bf16[32,24,2560]{2,1,0:T(8,128)(2,1)}, u32[]{:S(2)}, u32[]{:S(2)}) async-start(bf16[32,24,2560]{2,1,0:T(8,128)(2,1)} %bitcast.71), calls=%async_computation.1 | async-start | bytes 7864320 | tf_op jit(solution)/shard_map/all_to_all | solution.py:164
  93.1 20.0 %shard_map.87 = (bf16[512,2560]{1,0:T(8,128)(2,1)}, f32[512,128]{1,0:T(8,128)}) custom-call(bf16[512,5120]{1,0:T(8,128)(2,1)} %bitcast.4.grad_ref.input_ref, bf16[512,5120]{1,0:T(8,128)(2,1)} %bitcast.4.grad_ref.input_ref, bf16[2560,768]{1,0:T(8,128)(2,1)} %bitcast.84, bf16[2560,768]{1,0:T(8,128)(2,1)} %bitcast.86, bf16[768,2560]{1,0:T(8,128)(2,1)} %bitcast.88), custom_call_target="tpu_custom_call" | custom-call | flops 10066329600 | bytes 19660800 | tf_op jit(solution)/shard_map/pallas_call | solution.py:64
  113.1 1.1 fusion.9
  114.2 29.8 %all-to-all-done.1 = bf16[32,24,2560]{2,1,0:T(8,128)(2,1)} async-done(((bf16[32,24,2560]{2,1,0:T(8,128)(2,1)}), bf16[32,24,2560]{2,1,0:T(8,128)(2,1)}, u32[]{:S(2)}, u32[]{:S(2)}) %all-to-all-start.1) | async-done | bytes 3932192 | tf_op jit(solution)/shard_map/all_to_all | solution.py:164
  144.0 5.0 %all-to-all-start.2 = ((bf16[32,16,2560]{2,1,0:T(8,128)(2,1)}), bf16[32,16,2560]{2,1,0:T(8,128)(2,1)}, u32[]{:S(2)}, u32[]{:S(2)}) async-start(bf16[32,16,2560]{2,1,0:T(8,128)(2,1)} %bitcast.79), calls=%async_computation.2 | async-start | bytes 5242880 | tf_op jit(solution)/shard_map/all_to_all | solution.py:167
  149.1 0.1 pad.7.clone
  149.1 3.3 %copy.69 = bf16[32,24,2560]{2,0,1:T(8,128)(2,1)S(1)} copy(bf16[32,24,2560]{2,1,0:T(8,128)(2,1)} %all-to-all-done.1) | data formatting | bytes 7864320 | tf_op jit(solution)/shard_map/optimization_barrier | solution.py:166
  152.4 4.0 %copy.70 = bf16[32,12,2,2560]{3,2,1,0:T(2,128)(2,1)S(1)} copy(bf16[32,12,2,2560]{3,0,1,2:T(8,128)(2,1)S(1)} %bitcast.72) | data formatting | bytes 7864320 | tf_op jit(solution)/shard_map/transpose | solution.py:172
  156.5 2.6 %copy.80 = bf16[48,8,2,2560]{3,1,2,0:T(8,128)(2,1)} copy(bf16[48,8,2,2560]{3,2,1,0:T(2,128)(2,1)S(1)} %bitcast.73) | data formatting | bytes 7864320
  159.0 19.0 %shard_map.88 = (bf16[384,2560]{1,0:T(8,128)(2,1)}, f32[384,128]{1,0:T(8,128)}) custom-call(bf16[384,5120]{1,0:T(8,128)(2,1)} %bitcast.76, bf16[384,5120]{1,0:T(8,128)(2,1)} %bitcast.77, bf16[2560,768]{1,0:T(8,128)(2,1)} %bitcast.85, bf16[2560,768]{1,0:T(8,128)(2,1)} %bitcast.87, bf16[768,2560]{1,0:T(8,128)(2,1)} %bitcast.89), custom_call_target="tpu_custom_call" | custom-call | flops 7549747200 | bytes 17694720 | tf_op jit(solution)/shard_map/pallas_call | solution.py:64
  178.0 2.5 %reshape.165 = bf16[32,12,2560]{2,1,0:T(8,128)(2,1)S(1)} reshape(bf16[384,2560]{1,0:T(8,128)(2,1)} %get-tuple-element.13) | data formatting | bytes 3932160 | tf_op jit(solution)/shard_map/reshape | solution.py:182
  180.6 0.0 copy-done.6
  180.6 0.1 fusion.10
  180.7 0.1 convert_element_type.56
  180.8 0.1 reshape.166
  180.9 0.1 fusion.8
  181.0 0.3 copy.71
  181.3 2.6 %maximum_maximum_fusion = bf16[32,16,2560]{2,1,0:T(8,128)(2,1)} fusion(bf16[32,1,2560]{2,1,0:T(2,128)(2,1)S(1)} %copy.71, bf16[32,12,2560]{2,1,0:T(8,128)(2,1)S(1)} %reshape.165, bf16[16]{0:T(256)(128)(2,1)S(1)} %pad.7.clone), kind=kLoop, calls=%fused_computation.7 | loop fusion | flops 7864320 | bytes 4751392 | tf_op jit(solution)/shard_map/concatenate | solution.py:180
  183.9 1.2 all-to-all-done.2
  185.0 6.1 %all-to-all-start.3 = ((bf16[32,16,2560]{2,1,0:T(8,128)(2,1)}), bf16[32,16,2560]{2,1,0:T(8,128)(2,1)S(1)}, u32[]{:S(2)}, u32[]{:S(2)}) async-start(bf16[32,16,2560]{2,1,0:T(8,128)(2,1)} %maximum_maximum_fusion), calls=%async_computation.3 | async-start | bytes 5242880 | tf_op jit(solution)/shard_map/all_to_all | solution.py:188
  191.2 0.1 sub.19
  191.3 0.0 copy-start.4
  191.3 0.1 sub.24
  191.4 0.1 copy.58
  191.5 0.1 copy.66
  191.6 0.0 copy-done.7
  191.6 0.3 copy-done.4
  191.9 0.5 select_reduce_fusion.1
  192.4 4.0 %convolution_add_fusion.1 = f32[128,2560]{1,0:T(8,128)} fusion(f32[128,512]{1,0:T(8,128)S(1)} %get-tuple-element.17, bf16[512,2560]{1,0:T(8,128)(2,1)} %bitcast.10, bf16[1,128,2560]{2,1,0:T(8,128)(2,1)S(1)} %copy-done), kind=kOutput, calls=%fused_computation.2 | convolution fusion | flops 2013921280 | bytes 4849664 | tf_op jit(solution)/shard_map/dot_general | solution.py:193
  196.4 30.9 %all-to-all-done.3 = bf16[32,16,2560]{2,1,0:T(8,128)(2,1)S(1)} async-done(((bf16[32,16,2560]{2,1,0:T(8,128)(2,1)}), bf16[32,16,2560]{2,1,0:T(8,128)(2,1)S(1)}, u32[]{:S(2)}, u32[]{:S(2)}) %all-to-all-start.3) | async-done | bytes 2621472 | tf_op jit(solution)/shard_map/all_to_all | solution.py:188
  227.4 3.3 %fusion.1 = bf16[1,128,2560]{2,1,0:T(8,128)(2,1)} fusion(f32[128,2560]{1,0:T(8,128)} %convolution_add_fusion.1, f32[128,512]{1,0:T(8,128)S(1)} %get-tuple-element.16, bf16[512,2560]{1,0:T(8,128)(2,1)S(1)} %bitcast.74), kind=kOutput, calls=%fused_computation.4 | convolution fusion | flops 2013921280 | bytes 4849664 | tf_op jit(solution)/shard_map/dot_general | solution.py:193
  230.7 1.3 collective-permute-start
  232.0 0.0 copy-done.3
  232.0 0.1 copy.73
  232.1 0.1 fusion.14
  232.2 0.1 reshape.168
  232.3 1.1 select_reduce_fusion
  233.3 14.2 %collective-permute-done = bf16[1,128,2560]{2,1,0:T(8,128)(2,1)} collective-permute-done((bf16[1,128,2560]{2,1,0:T(8,128)(2,1)}, bf16[1,128,2560]{2,1,0:T(8,128)(2,1)}, u32[]{:S(2)}, u32[]{:S(2)}) %collective-permute-start) | collective-permute-done | bytes 655392 | tf_op jit(solution)/shard_map/ppermute | solution.py:11
  247.6 2.0 copy.95
  (16 shorter events, 0.1 us)
Async XLA Ops:
  1.4 12.3 %copy-start.2 = (s32[1,128,6]{2,1,0:T(8,128)}, s32[1,128,6]{2,1,0:T(8,128)S(1)}, u32[]{:S(2)}) copy-start(s32[1,128,6]{2,1,0:T(8,128)S(1)} %copy.55) | copy-start | bytes 9220
  13.7 9.5 %copy-start = (bf16[1,128,2560]{2,1,0:T(8,128)(2,1)S(1)}, bf16[1,128,2560]{2,1,0:T(8,128)(2,1)}, u32[]{:S(2)}) copy-start(bf16[1,128,2560]{2,1,0:T(8,128)(2,1)} %param.7) | copy-start | bytes 1966084
  13.7 74.6 %all-to-all-start = ((bf16[32,16,5120]{2,1,0:T(8,128)(2,1)}), bf16[32,16,5120]{2,1,0:T(8,128)(2,1)}, u32[]{:S(2)}, u32[]{:S(2)}) async-start(bf16[32,16,5120]{2,1,0:T(8,128)(2,1)} %bitcast.70), calls=%async_computation | async-start | bytes 10485760 | tf_op jit(solution)/shard_map/all_to_all | solution.py:163
  23.2 1.2 copy-start.1
  88.3 55.8 %all-to-all-start.1 = ((bf16[32,24,2560]{2,1,0:T(8,128)(2,1)}), bf16[32,24,2560]{2,1,0:T(8,128)(2,1)}, u32[]{:S(2)}, u32[]{:S(2)}) async-start(bf16[32,24,2560]{2,1,0:T(8,128)(2,1)} %bitcast.71), calls=%async_computation.1 | async-start | bytes 7864320 | tf_op jit(solution)/shard_map/all_to_all | solution.py:164
  144.0 41.0 %all-to-all-start.2 = ((bf16[32,16,2560]{2,1,0:T(8,128)(2,1)}), bf16[32,16,2560]{2,1,0:T(8,128)(2,1)}, u32[]{:S(2)}, u32[]{:S(2)}) async-start(bf16[32,16,2560]{2,1,0:T(8,128)(2,1)} %bitcast.79), calls=%async_computation.2 | async-start | bytes 5242880 | tf_op jit(solution)/shard_map/all_to_all | solution.py:167
  178.0 2.5 %copy-start.6 = (f32[384,128]{1,0:T(8,128)S(1)}, f32[384,128]{1,0:T(8,128)}, u32[]{:S(2)}) copy-start(f32[384,128]{1,0:T(8,128)} %get-tuple-element.15) | copy-start | bytes 589828
  183.9 7.7 %copy-start.7 = (f32[1,128,6]{1,0,2:T(1,128)S(1)}, f32[1,128,6]{1,0,2:T(1,128)}, u32[]{:S(2)}) copy-start(f32[1,128,6]{1,0,2:T(1,128)} %param.10) | copy-start | bytes 9220
  185.0 42.3 %all-to-all-start.3 = ((bf16[32,16,2560]{2,1,0:T(8,128)(2,1)}), bf16[32,16,2560]{2,1,0:T(8,128)(2,1)S(1)}, u32[]{:S(2)}, u32[]{:S(2)}) async-start(bf16[32,16,2560]{2,1,0:T(8,128)(2,1)} %maximum_maximum_fusion), calls=%async_computation.3 | async-start | bytes 5242880 | tf_op jit(solution)/shard_map/all_to_all | solution.py:188
  191.3 0.6 copy-start.4
  196.4 35.5 %copy-start.3 = (s32[1,128,6]{2,1,0:T(8,128)S(1)}, s32[1,128,6]{2,1,0:T(8,128)}, u32[]{:S(2)}) copy-start(s32[1,128,6]{2,1,0:T(8,128)} %copy-done.2) | copy-start | bytes 9220
  196.4 35.6 %copy-start.5 = (s32[128,6]{1,0:T(8,128)S(1)}, s32[128,6]{1,0:T(8,128)}, u32[]{:S(2)}) copy-start(s32[128,6]{1,0:T(8,128)} %copy-done.4) | copy-start | bytes 9220
  230.7 16.9 %collective-permute-start = (bf16[1,128,2560]{2,1,0:T(8,128)(2,1)}, bf16[1,128,2560]{2,1,0:T(8,128)(2,1)}, u32[]{:S(2)}, u32[]{:S(2)}) collective-permute-start(bf16[1,128,2560]{2,1,0:T(8,128)(2,1)} %fusion.1), channel_id=1, source_target_pairs={{32,0},{64,32},{96,64},{33,1},{65,33},{97,65},{34,2},{66,34},{98,6... | collective-permute-start | bytes 1966088 | tf_op jit(solution)/shard_map/ppermute | solution.py:11

commit v9 on v7

--- a/solution.py
+++ b/solution.py
@@ -99,13 +99,12 @@
     chunk = -(-(capacity + 1) // 16) * 8
     rows = peer_count * chunk
 
-    flat_ids = chosen.reshape(-1)
-    one_hot = (flat_ids[:, None] == jnp.arange(peer_count, dtype=jnp.int32)[None, :]).astype(
-        jnp.int32
-    )
-    places = (jnp.sum(one_hot * jnp.cumsum(one_hot, axis=0), axis=1) - 1).reshape(
-        token_count, top_count
-    )
+    named = chosen[:, :, None] == jnp.arange(peer_count, dtype=jnp.int32)[None, None, :]
+    incidence = jnp.any(named, axis=1).astype(jnp.bfloat16)
+    token_iota = jnp.arange(token_count, dtype=jnp.int32)
+    earlier = (token_iota[None, :] < token_iota[:, None]).astype(jnp.bfloat16)
+    before = jnp.dot(earlier, incidence, preferred_element_type=jnp.float32)
+    places = jnp.sum(jnp.where(named, before[:, None, :], 0.0), axis=2).astype(jnp.int32)
     ids = chosen
     lanes = jnp.arange(rows, dtype=jnp.int32)[None, None, :]
     both = jnp.concatenate([grad_tokens, input_tokens], axis=1)

time: 246 us -> 246 us (level)
    unnamed x22 -> x12, local copies, waits for them, and re-layouts: 4.55 us -> 5.26 us
  transfers between devices with their start and end apart: 5 -> 5, of which waited for: 5 -> 4; matrix products, arithmetic and copies ran while one was open for 12% -> 12% of each run, Pallas kernels for 16% -> 16%
where the time goes in v9:
time: 246 us; the launch traced here: 245 us
  waiting for transfers between devices  136 us (55%)
  Pallas kernels  39 us (16%)
  starting transfers between devices  27.1 us (11%)
  local copies, waits for them, and re-layouts  18.6 us (8%)
  matrix products  16.1 us (7%)
  other arithmetic  7.14 us (3%)
    all_to_all x1, waiting for transfers between devices, body(): lax.all_to_all(send_a, 'expert', 0, 0, tiled=True)  60.6 us
    pallas_call x2, Pallas kernels, expert_call(): pl.pallas_call(expert_kernel, grid=(steps,), in_specs=[pl.BlockSpec((tile...  39 us
    all_to_all x1, waiting for transfers between devices, body(): returned_b = lax.all_to_all(back_b, 'expert', 0, 0, tiled=True)  31.6 us
    all_to_all x1, waiting for transfers between devices, body(): arrived_b = lax.all_to_all(send_b, 'expert', 0, 0, tiled=True)  29.8 us
    ppermute x1, waiting for transfers between devices, passed_along(): lax.ppermute(value, axis, [(source, source + steps) for source in range(f...  14.2 us
    all_to_all x1, starting transfers between devices, body(): lax.all_to_all(send_a, 'expert', 0, 0, tiled=True)  8.69 us
    all_to_all x1, starting transfers between devices, body(): returned_b = lax.all_to_all(back_b, 'expert', 0, 0, tiled=True)  7.29 us
    dot_general x2, matrix products, weighted(): jnp.dot(weights, returned.astype(jnp.float32), precision=lax.Precision.HI...  6.5 us
  transfers between devices with their start and end apart: 5, of which 4 were waited for; matrix products, arithmetic and copies ran while one was open for 12% of the time, Pallas kernels for 16%

profile of v9, /device:TPU:0, one launch (start us, length us, event | category | flops | bytes accessed | tf_op | source)
XLA Modules:
  0.0 245.0 jit_solution(17558803978986026087)
XLA Ops:
  0.6 0.7 copy.80
  1.3 0.1 fusion.15
  1.5 0.7 select_bitcast_fusion
  2.2 0.2 fusion.4
  2.4 5.1 %convolution_convert_fusion = bf16[512,5120]{1,0:T(8,128)(2,1)} fusion(pred[512,128]{1,0:T(8,128)(4,1)S(1)} %fusion.4, bf16[128,2560]{1,0:T(8,128)(2,1)} %bitcast.86, bf16[128,2560]{1,0:T(8,128)(2,1)} %bitcast.83), kind=kOutput, calls=%fused_computation.1 | convolution fusion | flops 676331520 | bytes 6619136 | tf_op jit(solution)/shard_map/dot_general | solution.py:122
  7.6 0.0 copy-start
  7.6 8.7 %all-to-all-start = ((bf16[32,16,5120]{2,1,0:T(8,128)(2,1)}), bf16[32,16,5120]{2,1,0:T(8,128)(2,1)}, u32[]{:S(2)}, u32[]{:S(2)}) async-start(bf16[32,16,5120]{2,1,0:T(8,128)(2,1)} %bitcast.78), calls=%async_computation | async-start | bytes 10485760 | tf_op jit(solution)/shard_map/all_to_all | solution.py:137
  16.3 0.8 fusion.2
  17.1 0.0 copy-done
  17.1 0.0 copy-start.1
  17.1 1.2 fusion.28
  18.3 0.0 copy-done.1
  18.3 3.2 %add_convert_fusion = bf16[768,2560]{1,0:T(8,128)(2,1)} fusion(f32[768,2560]{1,0:T(8,128)S(1)} %fusion.28, pred[768,128]{1,0:T(8,128)(4,1)S(1)} %get-tuple-element.25, bf16[1,128,2560]{2,1,0:T(8,128)(2,1)S(1)} %copy-done.1), kind=kOutput, calls=%fused_computation | convolution fusion | flops 507248640 | bytes 12550144 | tf_op jit(solution)/shard_map/dot_general | solution.py:132
  21.5 60.6 %all-to-all-done = bf16[32,16,5120]{2,1,0:T(8,128)(2,1)} async-done(((bf16[32,16,5120]{2,1,0:T(8,128)(2,1)}), bf16[32,16,5120]{2,1,0:T(8,128)(2,1)}, u32[]{:S(2)}, u32[]{:S(2)}) %all-to-all-start) | async-done | bytes 5242912 | tf_op jit(solution)/shard_map/all_to_all | solution.py:137
  82.2 4.8 %all-to-all-start.1 = ((bf16[32,24,2560]{2,1,0:T(8,128)(2,1)}), bf16[32,24,2560]{2,1,0:T(8,128)(2,1)}, u32[]{:S(2)}, u32[]{:S(2)}) async-start(bf16[32,24,2560]{2,1,0:T(8,128)(2,1)} %bitcast.79), calls=%async_computation.1 | async-start | bytes 7864320 | tf_op jit(solution)/shard_map/all_to_all | solution.py:138
  87.0 20.0 %shard_map.86 = (bf16[512,2560]{1,0:T(8,128)(2,1)}, f32[512,128]{1,0:T(8,128)}) custom-call(bf16[512,5120]{1,0:T(8,128)(2,1)} %bitcast.5.grad_ref.input_ref, bf16[512,5120]{1,0:T(8,128)(2,1)} %bitcast.5.grad_ref.input_ref, bf16[2560,768]{1,0:T(8,128)(2,1)} %bitcast.92, bf16[2560,768]{1,0:T(8,128)(2,1)} %bitcast.94, bf16[768,2560]{1,0:T(8,128)(2,1)} %bitcast.96), custom_call_target="tpu_custom_call" | custom-call | flops 10066329600 | bytes 19660800 | tf_op jit(solution)/shard_map/pallas_call | solution.py:64
  107.0 1.1 fusion.12
  108.1 29.8 %all-to-all-done.1 = bf16[32,24,2560]{2,1,0:T(8,128)(2,1)} async-done(((bf16[32,24,2560]{2,1,0:T(8,128)(2,1)}), bf16[32,24,2560]{2,1,0:T(8,128)(2,1)}, u32[]{:S(2)}, u32[]{:S(2)}) %all-to-all-start.1) | async-done | bytes 3932192 | tf_op jit(solution)/shard_map/all_to_all | solution.py:138
  137.9 5.0 %all-to-all-start.2 = ((bf16[32,16,2560]{2,1,0:T(8,128)(2,1)}), bf16[32,16,2560]{2,1,0:T(8,128)(2,1)}, u32[]{:S(2)}, u32[]{:S(2)}) async-start(bf16[32,16,2560]{2,1,0:T(8,128)(2,1)} %bitcast.87), calls=%async_computation.2 | async-start | bytes 5242880 | tf_op jit(solution)/shard_map/all_to_all | solution.py:141
  142.9 0.1 pad.7.clone
  143.0 3.3 %copy.50 = bf16[32,24,2560]{2,0,1:T(8,128)(2,1)S(1)} copy(bf16[32,24,2560]{2,1,0:T(8,128)(2,1)} %all-to-all-done.1) | data formatting | bytes 7864320 | tf_op jit(solution)/shard_map/optimization_barrier | solution.py:140
  146.3 4.0 %copy.51 = bf16[32,12,2,2560]{3,2,1,0:T(2,128)(2,1)S(1)} copy(bf16[32,12,2,2560]{3,0,1,2:T(8,128)(2,1)S(1)} %bitcast.80) | data formatting | bytes 7864320 | tf_op jit(solution)/shard_map/transpose | solution.py:146
  150.3 2.6 %copy.55 = bf16[48,8,2,2560]{3,1,2,0:T(8,128)(2,1)} copy(bf16[48,8,2,2560]{3,2,1,0:T(2,128)(2,1)S(1)} %bitcast.81) | data formatting | bytes 7864320
  152.9 19.0 %shard_map.87 = (bf16[384,2560]{1,0:T(8,128)(2,1)}, f32[384,128]{1,0:T(8,128)}) custom-call(bf16[384,5120]{1,0:T(8,128)(2,1)} %bitcast.84, bf16[384,5120]{1,0:T(8,128)(2,1)} %bitcast.85, bf16[2560,768]{1,0:T(8,128)(2,1)} %bitcast.93, bf16[2560,768]{1,0:T(8,128)(2,1)} %bitcast.95, bf16[768,2560]{1,0:T(8,128)(2,1)} %bitcast.97), custom_call_target="tpu_custom_call" | custom-call | flops 7549747200 | bytes 17694720 | tf_op jit(solution)/shard_map/pallas_call | solution.py:64
  171.9 1.1 fusion.13
  173.0 0.1 convert_element_type.89
  173.1 0.1 reshape.126
  173.2 0.1 fusion.11
  173.3 1.0 copy.52
  174.3 2.5 %reshape.125 = bf16[32,12,2560]{2,1,0:T(8,128)(2,1)S(1)} reshape(bf16[384,2560]{1,0:T(8,128)(2,1)} %get-tuple-element.13) | data formatting | bytes 3932160 | tf_op jit(solution)/shard_map/reshape | solution.py:156
  176.8 3.6 %maximum_maximum_fusion = bf16[32,16,2560]{2,1,0:T(8,128)(2,1)} fusion(bf16[32,1,2560]{2,1,0:T(2,128)(2,1)} %copy.52, bf16[32,12,2560]{2,1,0:T(8,128)(2,1)S(1)} %reshape.125, bf16[16]{0:T(256)(128)(2,1)S(1)} %pad.7.clone), kind=kLoop, calls=%fused_computation.8 | loop fusion | flops 7864320 | bytes 4751392 | tf_op jit(solution)/shard_map/concatenate | solution.py:154
  180.3 0.0 copy-start.3
  180.3 0.0 copy-start.2
  180.3 0.0 all-to-all-done.2
  180.3 7.3 %all-to-all-start.3 = ((bf16[32,16,2560]{2,1,0:T(8,128)(2,1)}), bf16[32,16,2560]{2,1,0:T(8,128)(2,1)S(1)}, u32[]{:S(2)}, u32[]{:S(2)}) async-start(bf16[32,16,2560]{2,1,0:T(8,128)(2,1)} %maximum_maximum_fusion), calls=%async_computation.3 | async-start | bytes 5242880 | tf_op jit(solution)/shard_map/all_to_all | solution.py:162
  187.6 0.0 copy-done.3
  187.7 0.0 copy-done.2
  187.7 0.5 select_reduce_fusion.1
  188.2 4.0 %convolution_add_fusion.1 = f32[128,2560]{1,0:T(8,128)} fusion(f32[128,512]{1,0:T(8,128)S(1)} %get-tuple-element.17, bf16[512,2560]{1,0:T(8,128)(2,1)} %bitcast.13, bf16[1,128,2560]{2,1,0:T(8,128)(2,1)S(1)} %copy-done), kind=kOutput, calls=%fused_computation.3 | convolution fusion | flops 2013921280 | bytes 4849664 | tf_op jit(solution)/shard_map/dot_general | solution.py:167
  192.2 31.6 %all-to-all-done.3 = bf16[32,16,2560]{2,1,0:T(8,128)(2,1)S(1)} async-done(((bf16[32,16,2560]{2,1,0:T(8,128)(2,1)}), bf16[32,16,2560]{2,1,0:T(8,128)(2,1)S(1)}, u32[]{:S(2)}, u32[]{:S(2)}) %all-to-all-start.3) | async-done | bytes 2621472 | tf_op jit(solution)/shard_map/all_to_all | solution.py:162
  223.8 2.5 %fusion.1 = bf16[1,128,2560]{2,1,0:T(8,128)(2,1)S(1)} fusion(f32[128,2560]{1,0:T(8,128)} %convolution_add_fusion.1, f32[128,512]{1,0:T(8,128)S(1)} %get-tuple-element.16, bf16[512,2560]{1,0:T(8,128)(2,1)S(1)} %bitcast.82), kind=kOutput, calls=%fused_computation.5 | convolution fusion | flops 2013921280 | bytes 4849664 | tf_op jit(solution)/shard_map/dot_general | solution.py:167
  226.3 1.3 collective-permute-start
  227.6 0.1 fusion.16
  227.7 0.1 reshape.128
  227.8 1.1 select_reduce_fusion
  228.9 14.2 %collective-permute-done = bf16[1,128,2560]{2,1,0:T(8,128)(2,1)} collective-permute-done((bf16[1,128,2560]{2,1,0:T(8,128)(2,1)S(1)}, bf16[1,128,2560]{2,1,0:T(8,128)(2,1)}, u32[]{:S(2)}, u32[]{:S(2)}) %collective-permute-start) | collective-permute-done | bytes 655392 | tf_op jit(solution)/shard_map/ppermute | solution.py:11
  243.0 2.0 copy.83
  (5 shorter events, 0.1 us)
Async XLA Ops:
  7.6 9.5 %copy-start = (bf16[1,128,2560]{2,1,0:T(8,128)(2,1)S(1)}, bf16[1,128,2560]{2,1,0:T(8,128)(2,1)}, u32[]{:S(2)}) copy-start(bf16[1,128,2560]{2,1,0:T(8,128)(2,1)} %param.7) | copy-start | bytes 1966084
  7.6 74.6 %all-to-all-start = ((bf16[32,16,5120]{2,1,0:T(8,128)(2,1)}), bf16[32,16,5120]{2,1,0:T(8,128)(2,1)}, u32[]{:S(2)}, u32[]{:S(2)}) async-start(bf16[32,16,5120]{2,1,0:T(8,128)(2,1)} %bitcast.78), calls=%async_computation | async-start | bytes 10485760 | tf_op jit(solution)/shard_map/all_to_all | solution.py:137
  17.1 1.2 copy-start.1
  82.2 55.8 %all-to-all-start.1 = ((bf16[32,24,2560]{2,1,0:T(8,128)(2,1)}), bf16[32,24,2560]{2,1,0:T(8,128)(2,1)}, u32[]{:S(2)}, u32[]{:S(2)}) async-start(bf16[32,24,2560]{2,1,0:T(8,128)(2,1)} %bitcast.79), calls=%async_computation.1 | async-start | bytes 7864320 | tf_op jit(solution)/shard_map/all_to_all | solution.py:138
  137.9 42.4 %all-to-all-start.2 = ((bf16[32,16,2560]{2,1,0:T(8,128)(2,1)}), bf16[32,16,2560]{2,1,0:T(8,128)(2,1)}, u32[]{:S(2)}, u32[]{:S(2)}) async-start(bf16[32,16,2560]{2,1,0:T(8,128)(2,1)} %bitcast.87), calls=%async_computation.2 | async-start | bytes 5242880 | tf_op jit(solution)/shard_map/all_to_all | solution.py:141
  180.3 7.3 %copy-start.3 = (f32[1,128,6]{1,0,2:T(1,128)S(1)}, f32[1,128,6]{1,0,2:T(1,128)}, u32[]{:S(2)}) copy-start(f32[1,128,6]{1,0,2:T(1,128)} %param.10) | copy-start | bytes 9220
  180.3 7.3 %copy-start.2 = (s32[1,128,6]{1,0,2:T(1,128)S(1)}, s32[1,128,6]{1,0,2:T(1,128)}, u32[]{:S(2)}) copy-start(s32[1,128,6]{1,0,2:T(1,128)} %param.9) | copy-start | bytes 9220
  180.3 43.5 %all-to-all-start.3 = ((bf16[32,16,2560]{2,1,0:T(8,128)(2,1)}), bf16[32,16,2560]{2,1,0:T(8,128)(2,1)S(1)}, u32[]{:S(2)}, u32[]{:S(2)}) async-start(bf16[32,16,2560]{2,1,0:T(8,128)(2,1)} %maximum_maximum_fusion), calls=%async_computation.3 | async-start | bytes 5242880 | tf_op jit(solution)/shard_map/all_to_all | solution.py:162
  226.3 16.7 %collective-permute-start = (bf16[1,128,2560]{2,1,0:T(8,128)(2,1)S(1)}, bf16[1,128,2560]{2,1,0:T(8,128)(2,1)}, u32[]{:S(2)}, u32[]{:S(2)}) collective-permute-start(bf16[1,128,2560]{2,1,0:T(8,128)(2,1)S(1)} %fusion.1), channel_id=1, source_target_pairs={{32,0},{64,32},{96,64},{33,1},{65,33},{97,65},{34,2},{66,34},{98,6... | collective-permute-start | bytes 1966088 | tf_op jit(solution)/shard_map/ppermute | solution.py:11

commit v10 on v9

--- a/solution.py
+++ b/solution.py
@@ -172,7 +172,12 @@
         )
 
     combined = grad_tokens.astype(jnp.float32) + weighted(weights_a, returned_a)
-    combined = combined + weighted(weights_b, returned_b)
+    combined = combined + jnp.dot(
+        weights_b,
+        returned_b.astype(jnp.float32),
+        precision=lax.Precision.HIGH,
+        preferred_element_type=jnp.float32,
+    )
     gate_index = ids * capacity + places
     gate_hits = gate_index[:, :, None] == jnp.arange(gate_table.shape[0], dtype=jnp.int32)
     gate_slot = jnp.sum(

time: 246 us -> 245 us (level)
    dot_general x2 -> x1, matrix products: 6.5 us -> 3.99 us  [weighted(): jnp.dot(weights, returned.astype(jnp.float32), precision=lax.Precision.HI...]
where the time goes in v10:
time: 245 us
  waiting for transfers between devices  136 us (56%)
  Pallas kernels  39 us (16%)
  starting transfers between devices  27.1 us (11%)
  local copies, waits for them, and re-layouts  18.6 us (8%)
  matrix products  15.8 us (6%)
  other arithmetic  7.14 us (3%)
    all_to_all x1, waiting for transfers between devices, body(): lax.all_to_all(send_a, 'expert', 0, 0, tiled=True)  60.6 us
    pallas_call x2, Pallas kernels, expert_call(): pl.pallas_call(expert_kernel, grid=(steps,), in_specs=[pl.BlockSpec((tile...  39 us
    all_to_all x1, waiting for transfers between devices, body(): returned_b = lax.all_to_all(back_b, 'expert', 0, 0, tiled=True)  31.6 us
    all_to_all x1, waiting for transfers between devices, body(): arrived_b = lax.all_to_all(send_b, 'expert', 0, 0, tiled=True)  29.8 us
    ppermute x1, waiting for transfers between devices, passed_along(): lax.ppermute(value, axis, [(source, source + steps) for source in range(f...  14.2 us
    all_to_all x1, starting transfers between devices, body(): lax.all_to_all(send_a, 'expert', 0, 0, tiled=True)  8.69 us
    all_to_all x1, starting transfers between devices, body(): returned_b = lax.all_to_all(back_b, 'expert', 0, 0, tiled=True)  7.29 us
    unnamed x12, local copies, waits for them, and re-layouts  5.26 us
  transfers between devices with their start and end apart: 5, of which 4 were waited for; matrix products, arithmetic and copies ran while one was open for 12% of the time, Pallas kernels for 16%

profile of v10, /device:TPU:0, one launch (start us, length us, event | category | flops | bytes accessed | tf_op | source)
XLA Modules:
  0.0 244.7 jit_solution(5141588434109743745)
XLA Ops:
  0.6 0.7 copy.80
  1.3 0.1 fusion.15
  1.5 0.7 select_bitcast_fusion
  2.2 0.2 fusion.4
  2.4 5.1 %convolution_convert_fusion = bf16[512,5120]{1,0:T(8,128)(2,1)} fusion(pred[512,128]{1,0:T(8,128)(4,1)S(1)} %fusion.4, bf16[128,2560]{1,0:T(8,128)(2,1)} %bitcast.86, bf16[128,2560]{1,0:T(8,128)(2,1)} %bitcast.83), kind=kOutput, calls=%fused_computation.1 | convolution fusion | flops 676331520 | bytes 6619136 | tf_op jit(solution)/shard_map/dot_general | solution.py:122
  7.6 0.0 copy-start
  7.6 8.7 %all-to-all-start = ((bf16[32,16,5120]{2,1,0:T(8,128)(2,1)}), bf16[32,16,5120]{2,1,0:T(8,128)(2,1)}, u32[]{:S(2)}, u32[]{:S(2)}) async-start(bf16[32,16,5120]{2,1,0:T(8,128)(2,1)} %bitcast.78), calls=%async_computation | async-start | bytes 10485760 | tf_op jit(solution)/shard_map/all_to_all | solution.py:137
  16.3 0.8 fusion.2
  17.1 0.0 copy-done
  17.1 0.0 copy-start.1
  17.1 1.2 fusion.28
  18.3 0.0 copy-done.1
  18.3 3.2 %add_convert_fusion = bf16[768,2560]{1,0:T(8,128)(2,1)} fusion(f32[768,2560]{1,0:T(8,128)S(1)} %fusion.28, pred[768,128]{1,0:T(8,128)(4,1)S(1)} %get-tuple-element.25, bf16[1,128,2560]{2,1,0:T(8,128)(2,1)S(1)} %copy-done.1), kind=kOutput, calls=%fused_computation | convolution fusion | flops 507248640 | bytes 12550144 | tf_op jit(solution)/shard_map/dot_general | solution.py:132
  21.5 60.6 %all-to-all-done = bf16[32,16,5120]{2,1,0:T(8,128)(2,1)} async-done(((bf16[32,16,5120]{2,1,0:T(8,128)(2,1)}), bf16[32,16,5120]{2,1,0:T(8,128)(2,1)}, u32[]{:S(2)}, u32[]{:S(2)}) %all-to-all-start) | async-done | bytes 5242912 | tf_op jit(solution)/shard_map/all_to_all | solution.py:137
  82.2 4.8 %all-to-all-start.1 = ((bf16[32,24,2560]{2,1,0:T(8,128)(2,1)}), bf16[32,24,2560]{2,1,0:T(8,128)(2,1)}, u32[]{:S(2)}, u32[]{:S(2)}) async-start(bf16[32,24,2560]{2,1,0:T(8,128)(2,1)} %bitcast.79), calls=%async_computation.1 | async-start | bytes 7864320 | tf_op jit(solution)/shard_map/all_to_all | solution.py:138
  87.0 20.0 %shard_map.86 = (bf16[512,2560]{1,0:T(8,128)(2,1)}, f32[512,128]{1,0:T(8,128)}) custom-call(bf16[512,5120]{1,0:T(8,128)(2,1)} %bitcast.5.grad_ref.input_ref, bf16[512,5120]{1,0:T(8,128)(2,1)} %bitcast.5.grad_ref.input_ref, bf16[2560,768]{1,0:T(8,128)(2,1)} %bitcast.92, bf16[2560,768]{1,0:T(8,128)(2,1)} %bitcast.94, bf16[768,2560]{1,0:T(8,128)(2,1)} %bitcast.96), custom_call_target="tpu_custom_call" | custom-call | flops 10066329600 | bytes 19660800 | tf_op jit(solution)/shard_map/pallas_call | solution.py:64
  107.0 1.1 fusion.12
  108.1 29.8 %all-to-all-done.1 = bf16[32,24,2560]{2,1,0:T(8,128)(2,1)} async-done(((bf16[32,24,2560]{2,1,0:T(8,128)(2,1)}), bf16[32,24,2560]{2,1,0:T(8,128)(2,1)}, u32[]{:S(2)}, u32[]{:S(2)}) %all-to-all-start.1) | async-done | bytes 3932192 | tf_op jit(solution)/shard_map/all_to_all | solution.py:138
  137.9 5.0 %all-to-all-start.2 = ((bf16[32,16,2560]{2,1,0:T(8,128)(2,1)}), bf16[32,16,2560]{2,1,0:T(8,128)(2,1)}, u32[]{:S(2)}, u32[]{:S(2)}) async-start(bf16[32,16,2560]{2,1,0:T(8,128)(2,1)} %bitcast.87), calls=%async_computation.2 | async-start | bytes 5242880 | tf_op jit(solution)/shard_map/all_to_all | solution.py:141
  142.9 0.1 pad.7.clone
  143.0 3.3 %copy.50 = bf16[32,24,2560]{2,0,1:T(8,128)(2,1)S(1)} copy(bf16[32,24,2560]{2,1,0:T(8,128)(2,1)} %all-to-all-done.1) | data formatting | bytes 7864320 | tf_op jit(solution)/shard_map/optimization_barrier | solution.py:140
  146.3 4.0 %copy.51 = bf16[32,12,2,2560]{3,2,1,0:T(2,128)(2,1)S(1)} copy(bf16[32,12,2,2560]{3,0,1,2:T(8,128)(2,1)S(1)} %bitcast.80) | data formatting | bytes 7864320 | tf_op jit(solution)/shard_map/transpose | solution.py:146
  150.3 2.6 %copy.55 = bf16[48,8,2,2560]{3,1,2,0:T(8,128)(2,1)} copy(bf16[48,8,2,2560]{3,2,1,0:T(2,128)(2,1)S(1)} %bitcast.81) | data formatting | bytes 7864320
  152.9 19.0 %shard_map.87 = (bf16[384,2560]{1,0:T(8,128)(2,1)}, f32[384,128]{1,0:T(8,128)}) custom-call(bf16[384,5120]{1,0:T(8,128)(2,1)} %bitcast.84, bf16[384,5120]{1,0:T(8,128)(2,1)} %bitcast.85, bf16[2560,768]{1,0:T(8,128)(2,1)} %bitcast.93, bf16[2560,768]{1,0:T(8,128)(2,1)} %bitcast.95, bf16[768,2560]{1,0:T(8,128)(2,1)} %bitcast.97), custom_call_target="tpu_custom_call" | custom-call | flops 7549747200 | bytes 17694720 | tf_op jit(solution)/shard_map/pallas_call | solution.py:64
  171.9 1.1 fusion.13
  173.0 0.1 convert_element_type.89
  173.1 0.1 reshape.126
  173.2 0.1 fusion.11
  173.3 1.0 copy.52
  174.3 2.5 %reshape.125 = bf16[32,12,2560]{2,1,0:T(8,128)(2,1)S(1)} reshape(bf16[384,2560]{1,0:T(8,128)(2,1)} %get-tuple-element.13) | data formatting | bytes 3932160 | tf_op jit(solution)/shard_map/reshape | solution.py:156
  176.8 3.6 %maximum_maximum_fusion = bf16[32,16,2560]{2,1,0:T(8,128)(2,1)} fusion(bf16[32,1,2560]{2,1,0:T(2,128)(2,1)} %copy.52, bf16[32,12,2560]{2,1,0:T(8,128)(2,1)S(1)} %reshape.125, bf16[16]{0:T(256)(128)(2,1)S(1)} %pad.7.clone), kind=kLoop, calls=%fused_computation.8 | loop fusion | flops 7864320 | bytes 4751392 | tf_op jit(solution)/shard_map/concatenate | solution.py:154
  180.3 0.0 copy-start.3
  180.3 0.0 copy-start.2
  180.3 0.0 all-to-all-done.2
  180.3 7.3 %all-to-all-start.3 = ((bf16[32,16,2560]{2,1,0:T(8,128)(2,1)}), bf16[32,16,2560]{2,1,0:T(8,128)(2,1)S(1)}, u32[]{:S(2)}, u32[]{:S(2)}) async-start(bf16[32,16,2560]{2,1,0:T(8,128)(2,1)} %maximum_maximum_fusion), calls=%async_computation.3 | async-start | bytes 5242880 | tf_op jit(solution)/shard_map/all_to_all | solution.py:162
  187.6 0.0 copy-done.3
  187.7 0.0 copy-done.2
  187.7 0.5 select_reduce_fusion.1
  188.2 4.0 %convolution_add_fusion.1 = f32[128,2560]{1,0:T(8,128)} fusion(f32[128,512]{1,0:T(8,128)S(1)} %get-tuple-element.17, bf16[512,2560]{1,0:T(8,128)(2,1)} %bitcast.13, bf16[1,128,2560]{2,1,0:T(8,128)(2,1)S(1)} %copy-done), kind=kOutput, calls=%fused_computation.3 | convolution fusion | flops 2013921280 | bytes 4849664 | tf_op jit(solution)/shard_map/dot_general | solution.py:167
  192.2 31.6 %all-to-all-done.3 = bf16[32,16,2560]{2,1,0:T(8,128)(2,1)S(1)} async-done(((bf16[32,16,2560]{2,1,0:T(8,128)(2,1)}), bf16[32,16,2560]{2,1,0:T(8,128)(2,1)S(1)}, u32[]{:S(2)}, u32[]{:S(2)}) %all-to-all-start.3) | async-done | bytes 2621472 | tf_op jit(solution)/shard_map/all_to_all | solution.py:162
  223.8 2.2 fusion.1
  226.0 1.3 collective-permute-start
  227.3 0.1 fusion.16
  227.4 0.1 reshape.128
  227.5 1.1 select_reduce_fusion
  228.5 14.2 %collective-permute-done = bf16[1,128,2560]{2,1,0:T(8,128)(2,1)} collective-permute-done((bf16[1,128,2560]{2,1,0:T(8,128)(2,1)S(1)}, bf16[1,128,2560]{2,1,0:T(8,128)(2,1)}, u32[]{:S(2)}, u32[]{:S(2)}) %collective-permute-start) | collective-permute-done | bytes 655392 | tf_op jit(solution)/shard_map/ppermute | solution.py:11
  242.7 2.0 copy.83
  (5 shorter events, 0.1 us)
Async XLA Ops:
  7.6 9.5 %copy-start = (bf16[1,128,2560]{2,1,0:T(8,128)(2,1)S(1)}, bf16[1,128,2560]{2,1,0:T(8,128)(2,1)}, u32[]{:S(2)}) copy-start(bf16[1,128,2560]{2,1,0:T(8,128)(2,1)} %param.7) | copy-start | bytes 1966084
  7.6 74.6 %all-to-all-start = ((bf16[32,16,5120]{2,1,0:T(8,128)(2,1)}), bf16[32,16,5120]{2,1,0:T(8,128)(2,1)}, u32[]{:S(2)}, u32[]{:S(2)}) async-start(bf16[32,16,5120]{2,1,0:T(8,128)(2,1)} %bitcast.78), calls=%async_computation | async-start | bytes 10485760 | tf_op jit(solution)/shard_map/all_to_all | solution.py:137
  17.1 1.2 copy-start.1
  82.2 55.8 %all-to-all-start.1 = ((bf16[32,24,2560]{2,1,0:T(8,128)(2,1)}), bf16[32,24,2560]{2,1,0:T(8,128)(2,1)}, u32[]{:S(2)}, u32[]{:S(2)}) async-start(bf16[32,24,2560]{2,1,0:T(8,128)(2,1)} %bitcast.79), calls=%async_computation.1 | async-start | bytes 7864320 | tf_op jit(solution)/shard_map/all_to_all | solution.py:138
  137.9 42.4 %all-to-all-start.2 = ((bf16[32,16,2560]{2,1,0:T(8,128)(2,1)}), bf16[32,16,2560]{2,1,0:T(8,128)(2,1)}, u32[]{:S(2)}, u32[]{:S(2)}) async-start(bf16[32,16,2560]{2,1,0:T(8,128)(2,1)} %bitcast.87), calls=%async_computation.2 | async-start | bytes 5242880 | tf_op jit(solution)/shard_map/all_to_all | solution.py:141
  180.3 7.3 %copy-start.3 = (f32[1,128,6]{1,0,2:T(1,128)S(1)}, f32[1,128,6]{1,0,2:T(1,128)}, u32[]{:S(2)}) copy-start(f32[1,128,6]{1,0,2:T(1,128)} %param.10) | copy-start | bytes 9220
  180.3 7.3 %copy-start.2 = (s32[1,128,6]{1,0,2:T(1,128)S(1)}, s32[1,128,6]{1,0,2:T(1,128)}, u32[]{:S(2)}) copy-start(s32[1,128,6]{1,0,2:T(1,128)} %param.9) | copy-start | bytes 9220
  180.3 43.5 %all-to-all-start.3 = ((bf16[32,16,2560]{2,1,0:T(8,128)(2,1)}), bf16[32,16,2560]{2,1,0:T(8,128)(2,1)S(1)}, u32[]{:S(2)}, u32[]{:S(2)}) async-start(bf16[32,16,2560]{2,1,0:T(8,128)(2,1)} %maximum_maximum_fusion), calls=%async_computation.3 | async-start | bytes 5242880 | tf_op jit(solution)/shard_map/all_to_all | solution.py:162
  226.0 16.7 %collective-permute-start = (bf16[1,128,2560]{2,1,0:T(8,128)(2,1)S(1)}, bf16[1,128,2560]{2,1,0:T(8,128)(2,1)}, u32[]{:S(2)}, u32[]{:S(2)}) collective-permute-start(bf16[1,128,2560]{2,1,0:T(8,128)(2,1)S(1)} %fusion.1), channel_id=1, source_target_pairs={{32,0},{64,32},{96,64},{33,1},{65,33},{97,65},{34,2},{66,34},{98,6... | collective-permute-start | bytes 1966088 | tf_op jit(solution)/shard_map/ppermute | solution.py:11

commit v11 on v10

--- a/solution.py
+++ b/solution.py
@@ -96,7 +96,8 @@
     token_count, top_count = chosen.shape
     model_width = grad_tokens.shape[1]
     capacity = min(token_count, 7 * token_count * top_count // (6 * peer_count))
-    chunk = -(-(capacity + 1) // 16) * 8
+    chunk = (capacity - 1) // 8 * 8
+    tail = -(-(capacity - chunk + 1) // 8) * 8
     rows = peer_count * chunk
 
     named = chosen[:, :, None] == jnp.arange(peer_count, dtype=jnp.int32)[None, None, :]
@@ -106,22 +107,22 @@
     before = jnp.dot(earlier, incidence, preferred_element_type=jnp.float32)
     places = jnp.sum(jnp.where(named, before[:, None, :], 0.0), axis=2).astype(jnp.int32)
     ids = chosen
-    lanes = jnp.arange(rows, dtype=jnp.int32)[None, None, :]
     both = jnp.concatenate([grad_tokens, input_tokens], axis=1)
 
-    def dispatch(part):
-        local = places - part * chunk
-        inside = (local >= 0) & (local < chunk)
-        target = jnp.where(inside, ids * chunk + local, -1)
-        hits = target[:, :, None] == lanes
-        pick = jnp.any(target[None, :, :] == lanes.reshape(rows, 1, 1), axis=2)
+    def dispatch(offset, block):
+        local = places - offset
+        inside = (local >= 0) & (local < block)
+        target = jnp.where(inside, ids * block + local, -1)
+        lanes = jnp.arange(peer_count * block, dtype=jnp.int32)
+        hits = target[:, :, None] == lanes[None, None, :]
+        pick = jnp.any(target[None, :, :] == lanes[:, None, None], axis=2)
         weights = jnp.sum(jnp.where(hits, slot_probs[:, :, None], 0.0), axis=1)
         return pick, weights
 
-    pick_a, weights_a = dispatch(0)
+    pick_a, weights_a = dispatch(0, chunk)
     send_a = jnp.dot(pick_a.astype(jnp.bfloat16), both, preferred_element_type=jnp.float32)
     send_a = send_a.astype(jnp.bfloat16).reshape(peer_count, chunk, 2 * model_width)
-    unused, weights_b = dispatch(1)
+    unused, weights_b = dispatch(chunk, tail)
     rest = capacity - chunk
     local = places - chunk
     grad_row = jnp.where(local >= 0, ids * 2 * rest + local, -1)
@@ -146,7 +147,7 @@
         .transpose(0, 2, 1, 3)
         .reshape(peer_count * rest, 2 * model_width)
     )
-    back_b, gate_b = expert_call(arrived_b, gate_matrix, up_matrix, down_matrix, tile=192)
+    back_b, gate_b = expert_call(arrived_b, gate_matrix, up_matrix, down_matrix, tile=128)
     gates = jnp.concatenate(
         [gate_a.reshape(peer_count, chunk), gate_b.reshape(peer_count, rest)], axis=1
     )
@@ -155,13 +156,13 @@
         [
             back_b.reshape(peer_count, rest, model_width),
             gates[:, None, :],
-            jnp.zeros((peer_count, chunk - rest - 1, model_width), back_b.dtype),
+            jnp.zeros((peer_count, tail - rest - 1, model_width), back_b.dtype),
         ],
         axis=1,
     )
     returned_b = lax.all_to_all(back_b, "expert", 0, 0, tiled=True)
     gate_table = returned_b[:, rest, :capacity].reshape(-1)
-    returned_b = returned_b.reshape(rows, model_width)
+    returned_b = returned_b.reshape(peer_count * tail, model_width)
 
     def weighted(weights, returned):
         return jnp.dot(

time: 245 us -> 253 us (1.033)
  waiting for transfers between devices: 136 us -> 159 us
  local copies, waits for them, and re-layouts: 18.6 us -> 9.25 us
    all_to_all x1, waiting for transfers between devices: 60.6 us -> 96.4 us  [body(): lax.all_to_all(send_a, 'expert', 0, 0, tiled=True)]
    all_to_all x1, waiting for transfers between devices: 0.01 us -> 31.1 us  [body(): lax.all_to_all(back_a.reshape(peer_count, chunk, model_width), 'expert',...]
    all_to_all x1, waiting for transfers between devices: 29.8 us -> 0.01 us  [body(): arrived_b = lax.all_to_all(send_b, 'expert', 0, 0, tiled=True)]
    all_to_all x1, waiting for transfers between devices: 31.6 us -> 16.1 us  [body(): returned_b = lax.all_to_all(back_b, 'expert', 0, 0, tiled=True)]
    all_to_all x1, starting transfers between devices: 7.29 us -> 3.95 us  [body(): returned_b = lax.all_to_all(back_b, 'expert', 0, 0, tiled=True)]
    optimization_barrier x1, local copies, waits for them, and re-layouts: 3.26 us -> 0.39 us  [body(): lax.optimization_barrier((back_a, gate_a, arrived_b))]
    transpose x1, local copies, waits for them, and re-layouts: 4.04 us -> 1.35 us  [body(): arrived_b = arrived_b.reshape(peer_count, 2, rest, model_width).transpose...]
    all_to_all x1, starting transfers between devices: 5 us -> 7.69 us  [body(): lax.all_to_all(back_a.reshape(peer_count, chunk, model_width), 'expert',...]
  transfers between devices with their start and end apart: 5 -> 5, of which waited for: 4 -> 4; matrix products, arithmetic and copies ran while one was open for 12% -> 7% of each run, Pallas kernels for 16% -> 15%
where the time goes in v11:
time: 253 us; the launch traced here: 252 us
  waiting for transfers between devices  159 us (63%)
  Pallas kernels  38.5 us (15%)
  starting transfers between devices  25.6 us (10%)
  matrix products  14 us (6%)
  local copies, waits for them, and re-layouts  9.25 us (4%)
  other arithmetic  4.96 us (2%)
    all_to_all x1, waiting for transfers between devices, body(): lax.all_to_all(send_a, 'expert', 0, 0, tiled=True)  96.4 us
    pallas_call x2, Pallas kernels, expert_call(): pl.pallas_call(expert_kernel, grid=(steps,), in_specs=[pl.BlockSpec((tile...  38.5 us
    all_to_all x1, waiting for transfers between devices, body(): lax.all_to_all(back_a.reshape(peer_count, chunk, model_width), 'expert',...  31.1 us
    all_to_all x1, waiting for transfers between devices, body(): returned_b = lax.all_to_all(back_b, 'expert', 0, 0, tiled=True)  16.1 us
    ppermute x1, waiting for transfers between devices, passed_along(): lax.ppermute(value, axis, [(source, source + steps) for source in range(f...  15.2 us
    all_to_all x1, starting transfers between devices, body(): lax.all_to_all(send_a, 'expert', 0, 0, tiled=True)  8.69 us
    all_to_all x1, starting transfers between devices, body(): lax.all_to_all(back_a.reshape(peer_count, chunk, model_width), 'expert',...  7.69 us
    dot_general x1, matrix products, body(): jnp.dot(pick_a.astype(jnp.bfloat16), both, preferred_element_type=jnp.flo...  6.63 us
  transfers between devices with their start and end apart: 5, of which 4 were waited for; matrix products, arithmetic and copies ran while one was open for 7% of the time, Pallas kernels for 15%

profile of v11, /device:TPU:0, one launch (start us, length us, event | category | flops | bytes accessed | tf_op | source)
XLA Modules:
  0.0 251.9 jit_solution(16441435535504249155)
XLA Ops:
  0.6 0.7 copy.98
  1.3 0.1 fusion.17
  1.5 0.7 select_bitcast_fusion
  2.2 0.4 fusion.4
  2.6 6.6 %convolution_convert_fusion = bf16[768,5120]{1,0:T(8,128)(2,1)} fusion(pred[768,128]{1,0:T(8,128)(4,1)S(1)} %fusion.4, bf16[128,2560]{1,0:T(8,128)(2,1)} %bitcast.93, bf16[128,2560]{1,0:T(8,128)(2,1)} %bitcast.83), kind=kOutput, calls=%fused_computation | convolution fusion | flops 1013186560 | bytes 9273344 | tf_op jit(solution)/shard_map/dot_general | solution.py:123
  9.2 0.0 copy-start
  9.2 8.7 %all-to-all-start = ((bf16[32,24,5120]{2,1,0:T(8,128)(2,1)}), bf16[32,24,5120]{2,1,0:T(8,128)(2,1)}, u32[]{:S(2)}, u32[]{:S(2)}) async-start(bf16[32,24,5120]{2,1,0:T(8,128)(2,1)} %bitcast.80), calls=%async_computation | async-start | bytes 15728640 | tf_op jit(solution)/shard_map/all_to_all | solution.py:138
  17.9 0.0 copy-start.1
  18.0 0.2 fusion.9
  18.2 0.0 copy-done
  18.2 0.5 fusion.31
  18.7 0.3 copy-done.1
  19.0 1.5 fusion.1
  20.6 96.4 %all-to-all-done = bf16[32,24,5120]{2,1,0:T(8,128)(2,1)} async-done(((bf16[32,24,5120]{2,1,0:T(8,128)(2,1)}), bf16[32,24,5120]{2,1,0:T(8,128)(2,1)}, u32[]{:S(2)}, u32[]{:S(2)}) %all-to-all-start) | async-done | bytes 7864352 | tf_op jit(solution)/shard_map/all_to_all | solution.py:138
  117.0 3.9 %all-to-all-start.1 = ((bf16[32,8,2560]{2,1,0:T(8,128)(2,1)}), bf16[32,8,2560]{2,1,0:T(8,128)(2,1)S(1)}, u32[]{:S(2)}, u32[]{:S(2)}) async-start(bf16[32,8,2560]{2,1,0:T(8,128)(2,1)} %fusion.1), calls=%async_computation.1 | async-start | bytes 2621440 | tf_op jit(solution)/shard_map/all_to_all | solution.py:139
  121.0 26.9 %shard_map.86 = (bf16[768,2560]{1,0:T(8,128)(2,1)}, f32[768,128]{1,0:T(8,128)}) custom-call(bf16[768,5120]{1,0:T(8,128)(2,1)} %bitcast.5.grad_ref.input_ref, bf16[768,5120]{1,0:T(8,128)(2,1)} %bitcast.5.grad_ref.input_ref, bf16[2560,768]{1,0:T(8,128)(2,1)} %bitcast.86, bf16[2560,768]{1,0:T(8,128)(2,1)} %bitcast.88, bf16[768,2560]{1,0:T(8,128)(2,1)} %bitcast.90), custom_call_target="tpu_custom_call" | custom-call | flops 15099494400 | bytes 23592960 | tf_op jit(solution)/shard_map/pallas_call | solution.py:64
  147.9 1.2 fusion.13
  149.0 0.0 all-to-all-done.1
  149.0 7.7 %all-to-all-start.2 = ((bf16[32,24,2560]{2,1,0:T(8,128)(2,1)}), bf16[32,24,2560]{2,1,0:T(8,128)(2,1)}, u32[]{:S(2)}, u32[]{:S(2)}) async-start(bf16[32,24,2560]{2,1,0:T(8,128)(2,1)} %bitcast.92), calls=%async_computation.2 | async-start | bytes 7864320 | tf_op jit(solution)/shard_map/all_to_all | solution.py:142
  156.7 0.1 pad.7.clone
  156.8 0.4 copy.68
  157.2 1.3 copy.69
  158.6 1.3 copy.73
  159.8 11.6 %shard_map.87 = (bf16[128,2560]{1,0:T(8,128)(2,1)}, f32[128,128]{1,0:T(8,128)}) custom-call(bf16[128,5120]{1,0:T(8,128)(2,1)} %bitcast.81, bf16[128,5120]{1,0:T(8,128)(2,1)} %bitcast.82, bf16[2560,768]{1,0:T(8,128)(2,1)} %bitcast.87, bf16[2560,768]{1,0:T(8,128)(2,1)} %bitcast.89, bf16[768,2560]{1,0:T(8,128)(2,1)} %bitcast.91), custom_call_target="tpu_custom_call" | custom-call | flops 2516582400 | bytes 13762560 | tf_op jit(solution)/shard_map/pallas_call | solution.py:64
  171.4 0.9 fusion.18
  172.4 0.1 convert_element_type.89
  172.5 0.1 reshape.128
  172.6 0.1 fusion.15
  172.7 0.3 copy.70
  173.0 1.6 reshape.127
  174.6 0.0 copy-start.3
  174.6 0.0 copy-start.2
  174.6 1.8 maximum_maximum_fusion
  176.4 31.1 %all-to-all-done.2 = bf16[32,24,2560]{2,1,0:T(8,128)(2,1)} async-done(((bf16[32,24,2560]{2,1,0:T(8,128)(2,1)}), bf16[32,24,2560]{2,1,0:T(8,128)(2,1)}, u32[]{:S(2)}, u32[]{:S(2)}) %all-to-all-start.2) | async-done | bytes 3932192 | tf_op jit(solution)/shard_map/all_to_all | solution.py:142
  207.5 3.9 %all-to-all-start.3 = ((bf16[32,8,2560]{2,1,0:T(8,128)(2,1)}), bf16[32,8,2560]{2,1,0:T(8,128)(2,1)S(1)}, u32[]{:S(2)}, u32[]{:S(2)}) async-start(bf16[32,8,2560]{2,1,0:T(8,128)(2,1)} %maximum_maximum_fusion), calls=%async_computation.3 | async-start | bytes 2621440 | tf_op jit(solution)/shard_map/all_to_all | solution.py:163
  211.4 0.0 copy-done.3
  211.5 0.0 copy-done.2
  211.5 0.3 select_reduce_fusion.2
  211.8 0.3 select_reduce_fusion.1
  212.1 3.8 %convolution_add_fusion.2 = f32[128,2560]{1,0:T(8,128)S(1)} fusion(f32[128,768]{1,0:T(8,128)S(1)} %select_reduce_fusion.1, bf16[768,2560]{1,0:T(8,128)(2,1)} %bitcast.13, bf16[1,128,2560]{2,1,0:T(8,128)(2,1)S(1)} %copy-done), kind=kOutput, calls=%fused_computation.4 | convolution fusion | flops 3020554240 | bytes 6291456 | tf_op jit(solution)/shard_map/dot_general | solution.py:168
  215.9 16.1 %all-to-all-done.3 = bf16[32,8,2560]{2,1,0:T(8,128)(2,1)S(1)} async-done(((bf16[32,8,2560]{2,1,0:T(8,128)(2,1)}), bf16[32,8,2560]{2,1,0:T(8,128)(2,1)S(1)}, u32[]{:S(2)}, u32[]{:S(2)}) %all-to-all-start.3) | async-done | bytes 1310752 | tf_op jit(solution)/shard_map/all_to_all | solution.py:163
  232.0 1.4 fusion.3
  233.4 1.3 collective-permute-start
  234.7 0.1 fusion.19
  234.7 0.1 reshape.130
  234.8 1.1 select_reduce_fusion
  235.9 15.2 %collective-permute-done = bf16[1,128,2560]{2,1,0:T(8,128)(2,1)S(1)} collective-permute-done((bf16[1,128,2560]{2,1,0:T(8,128)(2,1)}, bf16[1,128,2560]{2,1,0:T(8,128)(2,1)S(1)}, u32[]{:S(2)}, u32[]{:S(2)}) %collective-permute-start) | collective-permute-done | bytes 655392 | tf_op jit(solution)/shard_map/ppermute | solution.py:11
  251.1 0.8 copy.101
  (5 shorter events, 0.1 us)
Async XLA Ops:
  9.2 8.9 %copy-start = (bf16[1,128,2560]{2,1,0:T(8,128)(2,1)S(1)}, bf16[1,128,2560]{2,1,0:T(8,128)(2,1)}, u32[]{:S(2)}) copy-start(bf16[1,128,2560]{2,1,0:T(8,128)(2,1)} %param.7) | copy-start | bytes 1966084
  9.2 107.8 %all-to-all-start = ((bf16[32,24,5120]{2,1,0:T(8,128)(2,1)}), bf16[32,24,5120]{2,1,0:T(8,128)(2,1)}, u32[]{:S(2)}, u32[]{:S(2)}) async-start(bf16[32,24,5120]{2,1,0:T(8,128)(2,1)} %bitcast.80), calls=%async_computation | async-start | bytes 15728640 | tf_op jit(solution)/shard_map/all_to_all | solution.py:138
  17.9 1.1 copy-start.1
  117.0 32.0 %all-to-all-start.1 = ((bf16[32,8,2560]{2,1,0:T(8,128)(2,1)}), bf16[32,8,2560]{2,1,0:T(8,128)(2,1)S(1)}, u32[]{:S(2)}, u32[]{:S(2)}) async-start(bf16[32,8,2560]{2,1,0:T(8,128)(2,1)} %fusion.1), calls=%async_computation.1 | async-start | bytes 2621440 | tf_op jit(solution)/shard_map/all_to_all | solution.py:139
  149.0 58.4 %all-to-all-start.2 = ((bf16[32,24,2560]{2,1,0:T(8,128)(2,1)}), bf16[32,24,2560]{2,1,0:T(8,128)(2,1)}, u32[]{:S(2)}, u32[]{:S(2)}) async-start(bf16[32,24,2560]{2,1,0:T(8,128)(2,1)} %bitcast.92), calls=%async_computation.2 | async-start | bytes 7864320 | tf_op jit(solution)/shard_map/all_to_all | solution.py:142
  174.6 36.9 %copy-start.3 = (f32[1,128,6]{1,0,2:T(1,128)S(1)}, f32[1,128,6]{1,0,2:T(1,128)}, u32[]{:S(2)}) copy-start(f32[1,128,6]{1,0,2:T(1,128)} %param.10) | copy-start | bytes 9220
  174.6 36.9 %copy-start.2 = (s32[1,128,6]{1,0,2:T(1,128)S(1)}, s32[1,128,6]{1,0,2:T(1,128)}, u32[]{:S(2)}) copy-start(s32[1,128,6]{1,0,2:T(1,128)} %param.9) | copy-start | bytes 9220
  207.5 24.5 %all-to-all-start.3 = ((bf16[32,8,2560]{2,1,0:T(8,128)(2,1)}), bf16[32,8,2560]{2,1,0:T(8,128)(2,1)S(1)}, u32[]{:S(2)}, u32[]{:S(2)}) async-start(bf16[32,8,2560]{2,1,0:T(8,128)(2,1)} %maximum_maximum_fusion), calls=%async_computation.3 | async-start | bytes 2621440 | tf_op jit(solution)/shard_map/all_to_all | solution.py:163
  233.4 17.7 %collective-permute-start = (bf16[1,128,2560]{2,1,0:T(8,128)(2,1)}, bf16[1,128,2560]{2,1,0:T(8,128)(2,1)S(1)}, u32[]{:S(2)}, u32[]{:S(2)}) collective-permute-start(bf16[1,128,2560]{2,1,0:T(8,128)(2,1)} %fusion.3), channel_id=1, source_target_pairs={{32,0},{64,32},{96,64},{33,1},{65,33},{97,65},{34,2},{66,34},{98,6... | collective-permute-start | bytes 1966088 | tf_op jit(solution)/shard_map/ppermute | solution.py:11

commit v12 on v10

--- a/solution.py
+++ b/solution.py
@@ -119,8 +119,8 @@
         return pick, weights
 
     pick_a, weights_a = dispatch(0)
-    send_a = jnp.dot(pick_a.astype(jnp.bfloat16), both, preferred_element_type=jnp.float32)
-    send_a = send_a.astype(jnp.bfloat16).reshape(peer_count, chunk, 2 * model_width)
+    send_a = jnp.dot(pick_a.astype(jnp.bfloat16), both, preferred_element_type=jnp.bfloat16)
+    send_a = send_a.reshape(peer_count, chunk, 2 * model_width)
     unused, weights_b = dispatch(1)
     rest = capacity - chunk
     local = places - chunk

time: 245 us -> 245 us (level)
  no operation moved by 1% of the time
where the time goes in v12:
time: 245 us
  waiting for transfers between devices  136 us (56%)
  Pallas kernels  39 us (16%)
  starting transfers between devices  27.1 us (11%)
  local copies, waits for them, and re-layouts  18.6 us (8%)
  matrix products  15.8 us (6%)
  other arithmetic  7.14 us (3%)
    all_to_all x1, waiting for transfers between devices, body(): lax.all_to_all(send_a, 'expert', 0, 0, tiled=True)  60.6 us
    pallas_call x2, Pallas kernels, expert_call(): pl.pallas_call(expert_kernel, grid=(steps,), in_specs=[pl.BlockSpec((tile...  39 us
    all_to_all x1, waiting for transfers between devices, body(): returned_b = lax.all_to_all(back_b, 'expert', 0, 0, tiled=True)  31.6 us
    all_to_all x1, waiting for transfers between devices, body(): arrived_b = lax.all_to_all(send_b, 'expert', 0, 0, tiled=True)  29.8 us
    ppermute x1, waiting for transfers between devices, passed_along(): lax.ppermute(value, axis, [(source, source + steps) for source in range(f...  14.2 us
    all_to_all x1, starting transfers between devices, body(): lax.all_to_all(send_a, 'expert', 0, 0, tiled=True)  8.69 us
    all_to_all x1, starting transfers between devices, body(): returned_b = lax.all_to_all(back_b, 'expert', 0, 0, tiled=True)  7.29 us
    unnamed x12, local copies, waits for them, and re-layouts  5.26 us
  transfers between devices with their start and end apart: 5, of which 4 were waited for; matrix products, arithmetic and copies ran while one was open for 12% of the time, Pallas kernels for 16%

profile of v12, /device:TPU:0, one launch (start us, length us, event | category | flops | bytes accessed | tf_op | source)
XLA Modules:
  0.0 244.7 jit_solution(5141588434109743745)
XLA Ops:
  0.6 0.7 copy.80
  1.3 0.1 fusion.15
  1.5 0.7 select_bitcast_fusion
  2.2 0.2 fusion.4
  2.4 5.1 %fusion.5 = bf16[32,16,5120]{2,1,0:T(8,128)(2,1)} fusion(pred[32,16,128]{2,1,0:T(8,128)(4,1)S(1)} %bitcast.90, bf16[128,2560]{1,0:T(8,128)(2,1)} %bitcast.88, bf16[128,2560]{1,0:T(8,128)(2,1)} %bitcast.85), kind=kOutput, calls=%fused_computation.19 | convolution fusion | flops 673710080 | bytes 6619136 | tf_op jit(solution)/shard_map/dot_general | solution.py:122
  7.6 0.0 copy-start
  7.6 8.7 %all-to-all-start = ((bf16[32,16,5120]{2,1,0:T(8,128)(2,1)}), bf16[32,16,5120]{2,1,0:T(8,128)(2,1)}, u32[]{:S(2)}, u32[]{:S(2)}) async-start(bf16[32,16,5120]{2,1,0:T(8,128)(2,1)} %fusion.5), calls=%async_computation | async-start | bytes 10485760 | tf_op jit(solution)/shard_map/all_to_all | solution.py:137
  16.3 0.8 fusion.2
  17.1 0.0 copy-done
  17.1 0.0 copy-start.1
  17.1 1.2 fusion.28
  18.3 0.0 copy-done.1
  18.3 3.2 %add_convert_fusion = bf16[768,2560]{1,0:T(8,128)(2,1)} fusion(f32[768,2560]{1,0:T(8,128)S(1)} %fusion.28, pred[768,128]{1,0:T(8,128)(4,1)S(1)} %get-tuple-element.25, bf16[1,128,2560]{2,1,0:T(8,128)(2,1)S(1)} %copy-done.1), kind=kOutput, calls=%fused_computation | convolution fusion | flops 507248640 | bytes 12550144 | tf_op jit(solution)/shard_map/dot_general | solution.py:132
  21.5 60.6 %all-to-all-done = bf16[32,16,5120]{2,1,0:T(8,128)(2,1)} async-done(((bf16[32,16,5120]{2,1,0:T(8,128)(2,1)}), bf16[32,16,5120]{2,1,0:T(8,128)(2,1)}, u32[]{:S(2)}, u32[]{:S(2)}) %all-to-all-start) | async-done | bytes 5242912 | tf_op jit(solution)/shard_map/all_to_all | solution.py:137
  82.2 4.8 %all-to-all-start.1 = ((bf16[32,24,2560]{2,1,0:T(8,128)(2,1)}), bf16[32,24,2560]{2,1,0:T(8,128)(2,1)}, u32[]{:S(2)}, u32[]{:S(2)}) async-start(bf16[32,24,2560]{2,1,0:T(8,128)(2,1)} %bitcast.81), calls=%async_computation.1 | async-start | bytes 7864320 | tf_op jit(solution)/shard_map/all_to_all | solution.py:138
  87.0 20.0 %shard_map.86 = (bf16[512,2560]{1,0:T(8,128)(2,1)}, f32[512,128]{1,0:T(8,128)}) custom-call(bf16[512,5120]{1,0:T(8,128)(2,1)} %bitcast.6.grad_ref.input_ref, bf16[512,5120]{1,0:T(8,128)(2,1)} %bitcast.6.grad_ref.input_ref, bf16[2560,768]{1,0:T(8,128)(2,1)} %bitcast.95, bf16[2560,768]{1,0:T(8,128)(2,1)} %bitcast.97, bf16[768,2560]{1,0:T(8,128)(2,1)} %bitcast.99), custom_call_target="tpu_custom_call" | custom-call | flops 10066329600 | bytes 19660800 | tf_op jit(solution)/shard_map/pallas_call | solution.py:64
  107.0 1.1 fusion.12
  108.1 29.8 %all-to-all-done.1 = bf16[32,24,2560]{2,1,0:T(8,128)(2,1)} async-done(((bf16[32,24,2560]{2,1,0:T(8,128)(2,1)}), bf16[32,24,2560]{2,1,0:T(8,128)(2,1)}, u32[]{:S(2)}, u32[]{:S(2)}) %all-to-all-start.1) | async-done | bytes 3932192 | tf_op jit(solution)/shard_map/all_to_all | solution.py:138
  137.9 5.0 %all-to-all-start.2 = ((bf16[32,16,2560]{2,1,0:T(8,128)(2,1)}), bf16[32,16,2560]{2,1,0:T(8,128)(2,1)}, u32[]{:S(2)}, u32[]{:S(2)}) async-start(bf16[32,16,2560]{2,1,0:T(8,128)(2,1)} %bitcast.89), calls=%async_computation.2 | async-start | bytes 5242880 | tf_op jit(solution)/shard_map/all_to_all | solution.py:141
  142.9 0.1 pad.7.clone
  143.0 3.3 %copy.50 = bf16[32,24,2560]{2,0,1:T(8,128)(2,1)S(1)} copy(bf16[32,24,2560]{2,1,0:T(8,128)(2,1)} %all-to-all-done.1) | data formatting | bytes 7864320 | tf_op jit(solution)/shard_map/optimization_barrier | solution.py:140
  146.3 4.0 %copy.51 = bf16[32,12,2,2560]{3,2,1,0:T(2,128)(2,1)S(1)} copy(bf16[32,12,2,2560]{3,0,1,2:T(8,128)(2,1)S(1)} %bitcast.82) | data formatting | bytes 7864320 | tf_op jit(solution)/shard_map/transpose | solution.py:146
  150.3 2.6 %copy.55 = bf16[48,8,2,2560]{3,1,2,0:T(8,128)(2,1)} copy(bf16[48,8,2,2560]{3,2,1,0:T(2,128)(2,1)S(1)} %bitcast.83) | data formatting | bytes 7864320
  152.9 19.0 %shard_map.87 = (bf16[384,2560]{1,0:T(8,128)(2,1)}, f32[384,128]{1,0:T(8,128)}) custom-call(bf16[384,5120]{1,0:T(8,128)(2,1)} %bitcast.86, bf16[384,5120]{1,0:T(8,128)(2,1)} %bitcast.87, bf16[2560,768]{1,0:T(8,128)(2,1)} %bitcast.96, bf16[2560,768]{1,0:T(8,128)(2,1)} %bitcast.98, bf16[768,2560]{1,0:T(8,128)(2,1)} %bitcast.100), custom_call_target="tpu_custom_call" | custom-call | flops 7549747200 | bytes 17694720 | tf_op jit(solution)/shard_map/pallas_call | solution.py:64
  171.9 1.1 fusion.13
  173.0 0.1 convert_element_type.85
  173.1 0.1 reshape.124
  173.2 0.1 fusion.11
  173.3 1.0 copy.52
  174.3 2.5 %reshape.123 = bf16[32,12,2560]{2,1,0:T(8,128)(2,1)S(1)} reshape(bf16[384,2560]{1,0:T(8,128)(2,1)} %get-tuple-element.13) | data formatting | bytes 3932160 | tf_op jit(solution)/shard_map/reshape | solution.py:156
  176.8 3.6 %maximum_maximum_fusion = bf16[32,16,2560]{2,1,0:T(8,128)(2,1)} fusion(bf16[32,1,2560]{2,1,0:T(2,128)(2,1)} %copy.52, bf16[32,12,2560]{2,1,0:T(8,128)(2,1)S(1)} %reshape.123, bf16[16]{0:T(256)(128)(2,1)S(1)} %pad.7.clone), kind=kLoop, calls=%fused_computation.7 | loop fusion | flops 7864320 | bytes 4751392 | tf_op jit(solution)/shard_map/concatenate | solution.py:154
  180.3 0.0 copy-start.3
  180.3 0.0 copy-start.2
  180.3 0.0 all-to-all-done.2
  180.3 7.3 %all-to-all-start.3 = ((bf16[32,16,2560]{2,1,0:T(8,128)(2,1)}), bf16[32,16,2560]{2,1,0:T(8,128)(2,1)S(1)}, u32[]{:S(2)}, u32[]{:S(2)}) async-start(bf16[32,16,2560]{2,1,0:T(8,128)(2,1)} %maximum_maximum_fusion), calls=%async_computation.3 | async-start | bytes 5242880 | tf_op jit(solution)/shard_map/all_to_all | solution.py:162
  187.6 0.0 copy-done.3
  187.7 0.0 copy-done.2
  187.7 0.5 select_reduce_fusion.1
  188.2 4.0 %convolution_add_fusion.1 = f32[128,2560]{1,0:T(8,128)} fusion(f32[128,512]{1,0:T(8,128)S(1)} %get-tuple-element.17, bf16[512,2560]{1,0:T(8,128)(2,1)} %bitcast.14, bf16[1,128,2560]{2,1,0:T(8,128)(2,1)S(1)} %copy-done), kind=kOutput, calls=%fused_computation.2 | convolution fusion | flops 2013921280 | bytes 4849664 | tf_op jit(solution)/shard_map/dot_general | solution.py:167
  192.2 31.6 %all-to-all-done.3 = bf16[32,16,2560]{2,1,0:T(8,128)(2,1)S(1)} async-done(((bf16[32,16,2560]{2,1,0:T(8,128)(2,1)}), bf16[32,16,2560]{2,1,0:T(8,128)(2,1)S(1)}, u32[]{:S(2)}, u32[]{:S(2)}) %all-to-all-start.3) | async-done | bytes 2621472 | tf_op jit(solution)/shard_map/all_to_all | solution.py:162
  223.8 2.2 fusion.1
  226.0 1.3 collective-permute-start
  227.3 0.1 fusion.16
  227.4 0.1 reshape.126
  227.5 1.1 select_reduce_fusion
  228.5 14.2 %collective-permute-done = bf16[1,128,2560]{2,1,0:T(8,128)(2,1)} collective-permute-done((bf16[1,128,2560]{2,1,0:T(8,128)(2,1)S(1)}, bf16[1,128,2560]{2,1,0:T(8,128)(2,1)}, u32[]{:S(2)}, u32[]{:S(2)}) %collective-permute-start) | collective-permute-done | bytes 655392 | tf_op jit(solution)/shard_map/ppermute | solution.py:11
  242.7 2.0 copy.83
  (5 shorter events, 0.1 us)
Async XLA Ops:
  7.6 9.5 %copy-start = (bf16[1,128,2560]{2,1,0:T(8,128)(2,1)S(1)}, bf16[1,128,2560]{2,1,0:T(8,128)(2,1)}, u32[]{:S(2)}) copy-start(bf16[1,128,2560]{2,1,0:T(8,128)(2,1)} %param.7) | copy-start | bytes 1966084
  7.6 74.6 %all-to-all-start = ((bf16[32,16,5120]{2,1,0:T(8,128)(2,1)}), bf16[32,16,5120]{2,1,0:T(8,128)(2,1)}, u32[]{:S(2)}, u32[]{:S(2)}) async-start(bf16[32,16,5120]{2,1,0:T(8,128)(2,1)} %fusion.5), calls=%async_computation | async-start | bytes 10485760 | tf_op jit(solution)/shard_map/all_to_all | solution.py:137
  17.1 1.2 copy-start.1
  82.2 55.8 %all-to-all-start.1 = ((bf16[32,24,2560]{2,1,0:T(8,128)(2,1)}), bf16[32,24,2560]{2,1,0:T(8,128)(2,1)}, u32[]{:S(2)}, u32[]{:S(2)}) async-start(bf16[32,24,2560]{2,1,0:T(8,128)(2,1)} %bitcast.81), calls=%async_computation.1 | async-start | bytes 7864320 | tf_op jit(solution)/shard_map/all_to_all | solution.py:138
  137.9 42.4 %all-to-all-start.2 = ((bf16[32,16,2560]{2,1,0:T(8,128)(2,1)}), bf16[32,16,2560]{2,1,0:T(8,128)(2,1)}, u32[]{:S(2)}, u32[]{:S(2)}) async-start(bf16[32,16,2560]{2,1,0:T(8,128)(2,1)} %bitcast.89), calls=%async_computation.2 | async-start | bytes 5242880 | tf_op jit(solution)/shard_map/all_to_all | solution.py:141
  180.3 7.3 %copy-start.3 = (f32[1,128,6]{1,0,2:T(1,128)S(1)}, f32[1,128,6]{1,0,2:T(1,128)}, u32[]{:S(2)}) copy-start(f32[1,128,6]{1,0,2:T(1,128)} %param.10) | copy-start | bytes 9220
  180.3 7.3 %copy-start.2 = (s32[1,128,6]{1,0,2:T(1,128)S(1)}, s32[1,128,6]{1,0,2:T(1,128)}, u32[]{:S(2)}) copy-start(s32[1,128,6]{1,0,2:T(1,128)} %param.9) | copy-start | bytes 9220
  180.3 43.5 %all-to-all-start.3 = ((bf16[32,16,2560]{2,1,0:T(8,128)(2,1)}), bf16[32,16,2560]{2,1,0:T(8,128)(2,1)S(1)}, u32[]{:S(2)}, u32[]{:S(2)}) async-start(bf16[32,16,2560]{2,1,0:T(8,128)(2,1)} %maximum_maximum_fusion), calls=%async_computation.3 | async-start | bytes 5242880 | tf_op jit(solution)/shard_map/all_to_all | solution.py:162
  226.0 16.7 %collective-permute-start = (bf16[1,128,2560]{2,1,0:T(8,128)(2,1)S(1)}, bf16[1,128,2560]{2,1,0:T(8,128)(2,1)}, u32[]{:S(2)}, u32[]{:S(2)}) collective-permute-start(bf16[1,128,2560]{2,1,0:T(8,128)(2,1)S(1)} %fusion.1), channel_id=1, source_target_pairs={{32,0},{64,32},{96,64},{33,1},{65,33},{97,65},{34,2},{66,34},{98,6... | collective-permute-start | bytes 1966088 | tf_op jit(solution)/shard_map/ppermute | solution.py:11

commit v13 on v10

--- a/solution.py
+++ b/solution.py
@@ -146,7 +146,7 @@
         .transpose(0, 2, 1, 3)
         .reshape(peer_count * rest, 2 * model_width)
     )
-    back_b, gate_b = expert_call(arrived_b, gate_matrix, up_matrix, down_matrix, tile=192)
+    back_b, gate_b = expert_call(arrived_b, gate_matrix, up_matrix, down_matrix, tile=384)
     gates = jnp.concatenate(
         [gate_a.reshape(peer_count, chunk), gate_b.reshape(peer_count, rest)], axis=1
     )

time: 245 us -> 244 us (level)
  transfers between devices with their start and end apart: 5 -> 5, of which waited for: 4 -> 5; matrix products, arithmetic and copies ran while one was open for 12% -> 13% of each run, Pallas kernels for 16% -> 15%
where the time goes in v13:
time: 244 us; the launch traced here: 243 us
  waiting for transfers between devices  137 us (56%)
  Pallas kernels  37.3 us (15%)
  starting transfers between devices  27 us (11%)
  local copies, waits for them, and re-layouts  18.6 us (8%)
  matrix products  15.8 us (6%)
  other arithmetic  7.14 us (3%)
    all_to_all x1, waiting for transfers between devices, body(): lax.all_to_all(send_a, 'expert', 0, 0, tiled=True)  60.6 us
    pallas_call x2, Pallas kernels, expert_call(): pl.pallas_call(expert_kernel, grid=(steps,), in_specs=[pl.BlockSpec((tile...  37.3 us
    all_to_all x1, waiting for transfers between devices, body(): returned_b = lax.all_to_all(back_b, 'expert', 0, 0, tiled=True)  31.6 us
    all_to_all x1, waiting for transfers between devices, body(): arrived_b = lax.all_to_all(send_b, 'expert', 0, 0, tiled=True)  29.8 us
    ppermute x1, waiting for transfers between devices, passed_along(): lax.ppermute(value, axis, [(source, source + steps) for source in range(f...  14.2 us
    all_to_all x1, starting transfers between devices, body(): lax.all_to_all(send_a, 'expert', 0, 0, tiled=True)  8.69 us
    all_to_all x1, starting transfers between devices, body(): returned_b = lax.all_to_all(back_b, 'expert', 0, 0, tiled=True)  7.15 us
    unnamed x12, local copies, waits for them, and re-layouts  5.26 us
  transfers between devices with their start and end apart: 5, of which 5 were waited for; matrix products, arithmetic and copies ran while one was open for 13% of the time, Pallas kernels for 15%

profile of v13, /device:TPU:0, one launch (start us, length us, event | category | flops | bytes accessed | tf_op | source)
XLA Modules:
  0.0 243.1 jit_solution(18258253446384090454)
XLA Ops:
  0.6 0.7 copy.80
  1.3 0.1 fusion.15
  1.5 0.7 select_bitcast_fusion
  2.2 0.2 fusion.4
  2.4 5.1 %convolution_convert_fusion = bf16[512,5120]{1,0:T(8,128)(2,1)} fusion(pred[512,128]{1,0:T(8,128)(4,1)S(1)} %fusion.4, bf16[128,2560]{1,0:T(8,128)(2,1)} %bitcast.86, bf16[128,2560]{1,0:T(8,128)(2,1)} %bitcast.83), kind=kOutput, calls=%fused_computation.1 | convolution fusion | flops 676331520 | bytes 6619136 | tf_op jit(solution)/shard_map/dot_general | solution.py:122
  7.6 0.0 copy-start
  7.6 8.7 %all-to-all-start = ((bf16[32,16,5120]{2,1,0:T(8,128)(2,1)}), bf16[32,16,5120]{2,1,0:T(8,128)(2,1)}, u32[]{:S(2)}, u32[]{:S(2)}) async-start(bf16[32,16,5120]{2,1,0:T(8,128)(2,1)} %bitcast.78), calls=%async_computation | async-start | bytes 10485760 | tf_op jit(solution)/shard_map/all_to_all | solution.py:137
  16.3 0.8 fusion.2
  17.1 0.0 copy-done
  17.1 0.0 copy-start.1
  17.1 1.2 fusion.28
  18.3 0.0 copy-done.1
  18.3 3.2 %add_convert_fusion = bf16[768,2560]{1,0:T(8,128)(2,1)} fusion(f32[768,2560]{1,0:T(8,128)S(1)} %fusion.28, pred[768,128]{1,0:T(8,128)(4,1)S(1)} %get-tuple-element.25, bf16[1,128,2560]{2,1,0:T(8,128)(2,1)S(1)} %copy-done.1), kind=kOutput, calls=%fused_computation | convolution fusion | flops 507248640 | bytes 12550144 | tf_op jit(solution)/shard_map/dot_general | solution.py:132
  21.5 60.6 %all-to-all-done = bf16[32,16,5120]{2,1,0:T(8,128)(2,1)} async-done(((bf16[32,16,5120]{2,1,0:T(8,128)(2,1)}), bf16[32,16,5120]{2,1,0:T(8,128)(2,1)}, u32[]{:S(2)}, u32[]{:S(2)}) %all-to-all-start) | async-done | bytes 5242912 | tf_op jit(solution)/shard_map/all_to_all | solution.py:137
  82.2 4.8 %all-to-all-start.1 = ((bf16[32,24,2560]{2,1,0:T(8,128)(2,1)}), bf16[32,24,2560]{2,1,0:T(8,128)(2,1)}, u32[]{:S(2)}, u32[]{:S(2)}) async-start(bf16[32,24,2560]{2,1,0:T(8,128)(2,1)} %bitcast.79), calls=%async_computation.1 | async-start | bytes 7864320 | tf_op jit(solution)/shard_map/all_to_all | solution.py:138
  87.0 20.0 %shard_map.86 = (bf16[512,2560]{1,0:T(8,128)(2,1)}, f32[512,128]{1,0:T(8,128)}) custom-call(bf16[512,5120]{1,0:T(8,128)(2,1)} %bitcast.5.grad_ref.input_ref, bf16[512,5120]{1,0:T(8,128)(2,1)} %bitcast.5.grad_ref.input_ref, bf16[2560,768]{1,0:T(8,128)(2,1)} %bitcast.92, bf16[2560,768]{1,0:T(8,128)(2,1)} %bitcast.94, bf16[768,2560]{1,0:T(8,128)(2,1)} %bitcast.96), custom_call_target="tpu_custom_call" | custom-call | flops 10066329600 | bytes 19660800 | tf_op jit(solution)/shard_map/pallas_call | solution.py:64
  107.0 1.1 fusion.12
  108.1 29.8 %all-to-all-done.1 = bf16[32,24,2560]{2,1,0:T(8,128)(2,1)} async-done(((bf16[32,24,2560]{2,1,0:T(8,128)(2,1)}), bf16[32,24,2560]{2,1,0:T(8,128)(2,1)}, u32[]{:S(2)}, u32[]{:S(2)}) %all-to-all-start.1) | async-done | bytes 3932192 | tf_op jit(solution)/shard_map/all_to_all | solution.py:138
  137.9 5.0 %all-to-all-start.2 = ((bf16[32,16,2560]{2,1,0:T(8,128)(2,1)}), bf16[32,16,2560]{2,1,0:T(8,128)(2,1)}, u32[]{:S(2)}, u32[]{:S(2)}) async-start(bf16[32,16,2560]{2,1,0:T(8,128)(2,1)} %bitcast.87), calls=%async_computation.2 | async-start | bytes 5242880 | tf_op jit(solution)/shard_map/all_to_all | solution.py:141
  142.9 0.1 pad.7.clone
  143.0 3.3 %copy.50 = bf16[32,24,2560]{2,0,1:T(8,128)(2,1)S(1)} copy(bf16[32,24,2560]{2,1,0:T(8,128)(2,1)} %all-to-all-done.1) | data formatting | bytes 7864320 | tf_op jit(solution)/shard_map/optimization_barrier | solution.py:140
  146.3 4.0 %copy.51 = bf16[32,12,2,2560]{3,2,1,0:T(2,128)(2,1)S(1)} copy(bf16[32,12,2,2560]{3,0,1,2:T(8,128)(2,1)S(1)} %bitcast.80) | data formatting | bytes 7864320 | tf_op jit(solution)/shard_map/transpose | solution.py:146
  150.3 2.6 %copy.55 = bf16[48,8,2,2560]{3,1,2,0:T(8,128)(2,1)} copy(bf16[48,8,2,2560]{3,2,1,0:T(2,128)(2,1)S(1)} %bitcast.81) | data formatting | bytes 7864320
  152.9 17.3 %shard_map.87 = (bf16[384,2560]{1,0:T(8,128)(2,1)}, f32[384,128]{1,0:T(8,128)}) custom-call(bf16[384,5120]{1,0:T(8,128)(2,1)} %bitcast.84, bf16[384,5120]{1,0:T(8,128)(2,1)} %bitcast.85, bf16[2560,768]{1,0:T(8,128)(2,1)} %bitcast.93, bf16[2560,768]{1,0:T(8,128)(2,1)} %bitcast.95, bf16[768,2560]{1,0:T(8,128)(2,1)} %bitcast.97), custom_call_target="tpu_custom_call" | custom-call | flops 7549747200 | bytes 17694720 | tf_op jit(solution)/shard_map/pallas_call | solution.py:64
  170.2 1.1 fusion.13
  171.3 0.1 convert_element_type.89
  171.4 0.1 reshape.126
  171.5 0.1 fusion.11
  171.6 1.0 copy.52
  172.5 2.5 %reshape.125 = bf16[32,12,2560]{2,1,0:T(8,128)(2,1)S(1)} reshape(bf16[384,2560]{1,0:T(8,128)(2,1)} %get-tuple-element.13) | data formatting | bytes 3932160 | tf_op jit(solution)/shard_map/reshape | solution.py:156
  175.0 3.6 %maximum_maximum_fusion = bf16[32,16,2560]{2,1,0:T(8,128)(2,1)} fusion(bf16[32,1,2560]{2,1,0:T(2,128)(2,1)} %copy.52, bf16[32,12,2560]{2,1,0:T(8,128)(2,1)S(1)} %reshape.125, bf16[16]{0:T(256)(128)(2,1)S(1)} %pad.7.clone), kind=kLoop, calls=%fused_computation.8 | loop fusion | flops 7864320 | bytes 4751392 | tf_op jit(solution)/shard_map/concatenate | solution.py:154
  178.6 0.0 copy-start.3
  178.6 0.0 copy-start.2
  178.6 0.3 all-to-all-done.2
  178.9 7.1 %all-to-all-start.3 = ((bf16[32,16,2560]{2,1,0:T(8,128)(2,1)}), bf16[32,16,2560]{2,1,0:T(8,128)(2,1)S(1)}, u32[]{:S(2)}, u32[]{:S(2)}) async-start(bf16[32,16,2560]{2,1,0:T(8,128)(2,1)} %maximum_maximum_fusion), calls=%async_computation.3 | async-start | bytes 5242880 | tf_op jit(solution)/shard_map/all_to_all | solution.py:162
  186.1 0.0 copy-done.3
  186.1 0.0 copy-done.2
  186.1 0.5 select_reduce_fusion.1
  186.7 4.0 %convolution_add_fusion.1 = f32[128,2560]{1,0:T(8,128)} fusion(f32[128,512]{1,0:T(8,128)S(1)} %get-tuple-element.17, bf16[512,2560]{1,0:T(8,128)(2,1)} %bitcast.13, bf16[1,128,2560]{2,1,0:T(8,128)(2,1)S(1)} %copy-done), kind=kOutput, calls=%fused_computation.3 | convolution fusion | flops 2013921280 | bytes 4849664 | tf_op jit(solution)/shard_map/dot_general | solution.py:167
  190.7 31.6 %all-to-all-done.3 = bf16[32,16,2560]{2,1,0:T(8,128)(2,1)S(1)} async-done(((bf16[32,16,2560]{2,1,0:T(8,128)(2,1)}), bf16[32,16,2560]{2,1,0:T(8,128)(2,1)S(1)}, u32[]{:S(2)}, u32[]{:S(2)}) %all-to-all-start.3) | async-done | bytes 2621472 | tf_op jit(solution)/shard_map/all_to_all | solution.py:162
  222.3 2.2 fusion.1
  224.5 1.3 collective-permute-start
  225.8 0.1 fusion.16
  225.8 0.1 reshape.128
  225.9 1.1 select_reduce_fusion
  227.0 14.2 %collective-permute-done = bf16[1,128,2560]{2,1,0:T(8,128)(2,1)} collective-permute-done((bf16[1,128,2560]{2,1,0:T(8,128)(2,1)S(1)}, bf16[1,128,2560]{2,1,0:T(8,128)(2,1)}, u32[]{:S(2)}, u32[]{:S(2)}) %collective-permute-start) | collective-permute-done | bytes 655392 | tf_op jit(solution)/shard_map/ppermute | solution.py:11
  241.1 2.0 copy.83
  (5 shorter events, 0.1 us)
Async XLA Ops:
  7.6 9.5 %copy-start = (bf16[1,128,2560]{2,1,0:T(8,128)(2,1)S(1)}, bf16[1,128,2560]{2,1,0:T(8,128)(2,1)}, u32[]{:S(2)}) copy-start(bf16[1,128,2560]{2,1,0:T(8,128)(2,1)} %param.7) | copy-start | bytes 1966084
  7.6 74.6 %all-to-all-start = ((bf16[32,16,5120]{2,1,0:T(8,128)(2,1)}), bf16[32,16,5120]{2,1,0:T(8,128)(2,1)}, u32[]{:S(2)}, u32[]{:S(2)}) async-start(bf16[32,16,5120]{2,1,0:T(8,128)(2,1)} %bitcast.78), calls=%async_computation | async-start | bytes 10485760 | tf_op jit(solution)/shard_map/all_to_all | solution.py:137
  17.1 1.2 copy-start.1
  82.2 55.8 %all-to-all-start.1 = ((bf16[32,24,2560]{2,1,0:T(8,128)(2,1)}), bf16[32,24,2560]{2,1,0:T(8,128)(2,1)}, u32[]{:S(2)}, u32[]{:S(2)}) async-start(bf16[32,24,2560]{2,1,0:T(8,128)(2,1)} %bitcast.79), calls=%async_computation.1 | async-start | bytes 7864320 | tf_op jit(solution)/shard_map/all_to_all | solution.py:138
  137.9 41.0 %all-to-all-start.2 = ((bf16[32,16,2560]{2,1,0:T(8,128)(2,1)}), bf16[32,16,2560]{2,1,0:T(8,128)(2,1)}, u32[]{:S(2)}, u32[]{:S(2)}) async-start(bf16[32,16,2560]{2,1,0:T(8,128)(2,1)} %bitcast.87), calls=%async_computation.2 | async-start | bytes 5242880 | tf_op jit(solution)/shard_map/all_to_all | solution.py:141
  178.6 7.5 %copy-start.3 = (f32[1,128,6]{1,0,2:T(1,128)S(1)}, f32[1,128,6]{1,0,2:T(1,128)}, u32[]{:S(2)}) copy-start(f32[1,128,6]{1,0,2:T(1,128)} %param.10) | copy-start | bytes 9220
  178.6 7.5 %copy-start.2 = (s32[1,128,6]{1,0,2:T(1,128)S(1)}, s32[1,128,6]{1,0,2:T(1,128)}, u32[]{:S(2)}) copy-start(s32[1,128,6]{1,0,2:T(1,128)} %param.9) | copy-start | bytes 9220
  178.9 43.3 %all-to-all-start.3 = ((bf16[32,16,2560]{2,1,0:T(8,128)(2,1)}), bf16[32,16,2560]{2,1,0:T(8,128)(2,1)S(1)}, u32[]{:S(2)}, u32[]{:S(2)}) async-start(bf16[32,16,2560]{2,1,0:T(8,128)(2,1)} %maximum_maximum_fusion), calls=%async_computation.3 | async-start | bytes 5242880 | tf_op jit(solution)/shard_map/all_to_all | solution.py:162
  224.5 16.7 %collective-permute-start = (bf16[1,128,2560]{2,1,0:T(8,128)(2,1)S(1)}, bf16[1,128,2560]{2,1,0:T(8,128)(2,1)}, u32[]{:S(2)}, u32[]{:S(2)}) collective-permute-start(bf16[1,128,2560]{2,1,0:T(8,128)(2,1)S(1)} %fusion.1), channel_id=1, source_target_pairs={{32,0},{64,32},{96,64},{33,1},{65,33},{97,65},{34,2},{66,34},{98,6... | collective-permute-start | bytes 1966088 | tf_op jit(solution)/shard_map/ppermute | solution.py:11

commit v14 on v13

--- a/solution.py
+++ b/solution.py
@@ -141,10 +141,8 @@
     returned_a = lax.all_to_all(
         back_a.reshape(peer_count, chunk, model_width), "expert", 0, 0, tiled=True
     ).reshape(rows, model_width)
-    arrived_b = (
-        arrived_b.reshape(peer_count, 2, rest, model_width)
-        .transpose(0, 2, 1, 3)
-        .reshape(peer_count * rest, 2 * model_width)
+    arrived_b = jnp.concatenate([arrived_b[:, :rest], arrived_b[:, rest:]], axis=2).reshape(
+        peer_count * rest, 2 * model_width
     )
     back_b, gate_b = expert_call(arrived_b, gate_matrix, up_matrix, down_matrix, tile=384)
     gates = jnp.concatenate(

time: 244 us -> 248 us (1.016)
  other arithmetic: 7.14 us -> 11 us
    reshape x0 -> x1, local copies, waits for them, and re-layouts: none -> 7.09 us  [body(): jnp.concatenate([arrived_b[:, :rest], arrived_b[:, rest:]], axis=2)]
    slice x0 -> x1, local copies, waits for them, and re-layouts: none -> 4.91 us  [body(): arrived_b[:, :rest]]
    concatenate x0 -> x1, other arithmetic: none -> 4.81 us  [body(): jnp.concatenate([arrived_b[:, :rest], arrived_b[:, rest:]], axis=2)]
    transpose x1 -> x0, local copies, waits for them, and re-layouts: 4.04 us -> none  [body(): arrived_b = arrived_b.reshape(peer_count, 2, rest, model_width).transpose...]
    optimization_barrier x1 -> x0, local copies, waits for them, and re-layouts: 3.26 us -> none  [body(): lax.optimization_barrier((back_a, gate_a, arrived_b))]
    unnamed x12 -> x13, local copies, waits for them, and re-layouts: 5.26 us -> 2.68 us
  transfers between devices with their start and end apart: 5 -> 5, of which waited for: 5 -> 5; matrix products, arithmetic and copies ran while one was open for 13% -> 12% of each run, Pallas kernels for 15% -> 15%
where the time goes in v14:
time: 248 us; the launch traced here: 247 us
  waiting for transfers between devices  137 us (55%)
  Pallas kernels  37 us (15%)
  starting transfers between devices  25.9 us (10%)
  local copies, waits for them, and re-layouts  19.1 us (8%)
  matrix products  15.8 us (6%)
  other arithmetic  11 us (4%)
    all_to_all x1, waiting for transfers between devices, body(): lax.all_to_all(send_a, 'expert', 0, 0, tiled=True)  60.6 us
    pallas_call x2, Pallas kernels, expert_call(): pl.pallas_call(expert_kernel, grid=(steps,), in_specs=[pl.BlockSpec((tile...  37 us
    all_to_all x1, waiting for transfers between devices, body(): returned_b = lax.all_to_all(back_b, 'expert', 0, 0, tiled=True)  31.6 us
    all_to_all x1, waiting for transfers between devices, body(): arrived_b = lax.all_to_all(send_b, 'expert', 0, 0, tiled=True)  29.8 us
    ppermute x1, waiting for transfers between devices, passed_along(): lax.ppermute(value, axis, [(source, source + steps) for source in range(f...  14.1 us
    all_to_all x1, starting transfers between devices, body(): lax.all_to_all(send_a, 'expert', 0, 0, tiled=True)  8.69 us
    reshape x1, local copies, waits for them, and re-layouts, body(): jnp.concatenate([arrived_b[:, :rest], arrived_b[:, rest:]], axis=2)  7.09 us
    all_to_all x1, starting transfers between devices, body(): returned_b = lax.all_to_all(back_b, 'expert', 0, 0, tiled=True)  6.08 us
  transfers between devices with their start and end apart: 5, of which 5 were waited for; matrix products, arithmetic and copies ran while one was open for 12% of the time, Pallas kernels for 15%

profile of v14, /device:TPU:0, one launch (start us, length us, event | category | flops | bytes accessed | tf_op | source)
XLA Modules:
  0.0 246.9 jit_solution(17724124980629034320)
XLA Ops:
  0.6 0.7 copy.61
  1.3 0.1 fusion.15
  1.5 0.7 select_bitcast_fusion
  2.2 0.2 fusion.4
  2.4 5.1 %convolution_convert_fusion = bf16[512,5120]{1,0:T(8,128)(2,1)} fusion(pred[512,128]{1,0:T(8,128)(4,1)S(1)} %fusion.4, bf16[128,2560]{1,0:T(8,128)(2,1)} %bitcast.76, bf16[128,2560]{1,0:T(8,128)(2,1)} %bitcast.75), kind=kOutput, calls=%fused_computation.1 | convolution fusion | flops 676331520 | bytes 6619136 | tf_op jit(solution)/shard_map/dot_general | solution.py:122
  7.6 0.0 copy-start
  7.6 8.7 %all-to-all-start = ((bf16[32,16,5120]{2,1,0:T(8,128)(2,1)}), bf16[32,16,5120]{2,1,0:T(8,128)(2,1)}, u32[]{:S(2)}, u32[]{:S(2)}) async-start(bf16[32,16,5120]{2,1,0:T(8,128)(2,1)} %bitcast.72), calls=%async_computation | async-start | bytes 10485760 | tf_op jit(solution)/shard_map/all_to_all | solution.py:137
  16.3 0.8 fusion.2
  17.1 0.0 copy-done
  17.1 0.0 copy-start.1
  17.1 1.2 fusion.28
  18.3 0.0 copy-done.1
  18.3 3.2 %add_convert_fusion = bf16[768,2560]{1,0:T(8,128)(2,1)} fusion(f32[768,2560]{1,0:T(8,128)S(1)} %fusion.28, pred[768,128]{1,0:T(8,128)(4,1)S(1)} %get-tuple-element.27, bf16[1,128,2560]{2,1,0:T(8,128)(2,1)S(1)} %copy-done.1), kind=kOutput, calls=%fused_computation | convolution fusion | flops 507248640 | bytes 12550144 | tf_op jit(solution)/shard_map/dot_general | solution.py:132
  21.5 60.6 %all-to-all-done = bf16[32,16,5120]{2,1,0:T(8,128)(2,1)} async-done(((bf16[32,16,5120]{2,1,0:T(8,128)(2,1)}), bf16[32,16,5120]{2,1,0:T(8,128)(2,1)}, u32[]{:S(2)}, u32[]{:S(2)}) %all-to-all-start) | async-done | bytes 5242912 | tf_op jit(solution)/shard_map/all_to_all | solution.py:137
  82.2 4.8 %all-to-all-start.1 = ((bf16[32,24,2560]{2,1,0:T(8,128)(2,1)}), bf16[32,24,2560]{2,1,0:T(8,128)(2,1)}, u32[]{:S(2)}, u32[]{:S(2)}) async-start(bf16[32,24,2560]{2,1,0:T(8,128)(2,1)} %bitcast.73), calls=%async_computation.1 | async-start | bytes 7864320 | tf_op jit(solution)/shard_map/all_to_all | solution.py:138
  87.0 0.1 pad.7.clone
  87.1 20.0 %shard_map.86 = (bf16[512,2560]{1,0:T(8,128)(2,1)}, f32[512,128]{1,0:T(8,128)}) custom-call(bf16[512,5120]{1,0:T(8,128)(2,1)} %bitcast.5.grad_ref.input_ref, bf16[512,5120]{1,0:T(8,128)(2,1)} %bitcast.5.grad_ref.input_ref, bf16[2560,768]{1,0:T(8,128)(2,1)} %bitcast.82, bf16[2560,768]{1,0:T(8,128)(2,1)} %bitcast.84, bf16[768,2560]{1,0:T(8,128)(2,1)} %bitcast.86), custom_call_target="tpu_custom_call" | custom-call | flops 10066329600 | bytes 19660800 | tf_op jit(solution)/shard_map/pallas_call | solution.py:64
  107.0 1.1 fusion.12
  108.1 29.8 %all-to-all-done.1 = bf16[32,24,2560]{2,1,0:T(8,128)(2,1)} async-done(((bf16[32,24,2560]{2,1,0:T(8,128)(2,1)}), bf16[32,24,2560]{2,1,0:T(8,128)(2,1)}, u32[]{:S(2)}, u32[]{:S(2)}) %all-to-all-start.1) | async-done | bytes 3932192 | tf_op jit(solution)/shard_map/all_to_all | solution.py:138
  137.9 4.9 %fusion.30 = (bf16[32,12,2560]{2,1,0:T(8,128)(2,1)S(1)}, bf16[32,12,2560]{2,1,0:T(8,128)(2,1)}) fusion(bf16[32,24,2560]{2,1,0:T(8,128)(2,1)} %all-to-all-done.1), kind=kLoop, calls=%fused_computation.67 | loop fusion | bytes 7864320 | tf_op jit(solution)/shard_map/slice | solution.py:144
  142.8 5.0 %all-to-all-start.2 = ((bf16[32,16,2560]{2,1,0:T(8,128)(2,1)}), bf16[32,16,2560]{2,1,0:T(8,128)(2,1)}, u32[]{:S(2)}, u32[]{:S(2)}) async-start(bf16[32,16,2560]{2,1,0:T(8,128)(2,1)} %bitcast.77), calls=%async_computation.2 | async-start | bytes 5242880 | tf_op jit(solution)/shard_map/all_to_all | solution.py:141
  147.8 4.8 %pad_maximum_fusion = bf16[32,12,5120]{2,1,0:T(8,128)(2,1)} fusion(bf16[32,12,2560]{2,1,0:T(8,128)(2,1)} %get-tuple-element.19, bf16[32,12,2560]{2,1,0:T(8,128)(2,1)S(1)} %get-tuple-element.18), kind=kLoop, calls=%fused_computation.2 | loop fusion | flops 7864320 | bytes 7864320 | tf_op jit(solution)/shard_map/concatenate | solution.py:144
  152.7 7.1 %reshape.120.grad_ref.input_ref = bf16[384,5120]{1,0:T(8,128)(2,1)} reshape(bf16[32,12,5120]{2,1,0:T(8,128)(2,1)} %pad_maximum_fusion) | data formatting | bytes 7864320 | tf_op jit(solution)/shard_map/reshape | solution.py:144
  159.7 17.0 %shard_map.87 = (bf16[384,2560]{1,0:T(8,128)(2,1)}, f32[384,128]{1,0:T(8,128)}) custom-call(bf16[384,5120]{1,0:T(8,128)(2,1)} %reshape.120.grad_ref.input_ref, bf16[384,5120]{1,0:T(8,128)(2,1)} %reshape.120.grad_ref.input_ref, bf16[2560,768]{1,0:T(8,128)(2,1)} %bitcast.83, bf16[2560,768]{1,0:T(8,128)(2,1)} %bitcast.85, bf16[768,2560]{1,0:T(8,128)(2,1)} %bitcast.87), custom_call_target="tpu_custom_call" | custom-call | flops 7549747200 | bytes 17694720 | tf_op jit(solution)/shard_map/pallas_call | solution.py:64
  176.8 0.0 copy-start.2
  176.8 2.5 %reshape.121 = bf16[32,12,2560]{2,1,0:T(8,128)(2,1)S(1)} reshape(bf16[384,2560]{1,0:T(8,128)(2,1)} %get-tuple-element.13) | data formatting | bytes 3932160 | tf_op jit(solution)/shard_map/reshape | solution.py:154
  179.3 0.0 copy-done.2
  179.3 0.1 fusion.13
  179.5 0.1 convert_element_type.89
  179.6 0.1 reshape.122
  179.7 0.1 fusion.11
  179.8 0.3 copy.34
  180.0 2.6 %maximum_maximum_fusion = bf16[32,16,2560]{2,1,0:T(8,128)(2,1)} fusion(bf16[32,1,2560]{2,1,0:T(2,128)(2,1)S(1)} %copy.34, bf16[32,12,2560]{2,1,0:T(8,128)(2,1)S(1)} %reshape.121, bf16[16]{0:T(256)(128)(2,1)S(1)} %pad.7.clone), kind=kLoop, calls=%fused_computation.9 | loop fusion | flops 7864320 | bytes 4751392 | tf_op jit(solution)/shard_map/concatenate | solution.py:152
  182.6 0.0 copy-start.4
  182.6 0.0 copy-start.3
  182.6 1.2 all-to-all-done.2
  183.8 6.1 %all-to-all-start.3 = ((bf16[32,16,2560]{2,1,0:T(8,128)(2,1)}), bf16[32,16,2560]{2,1,0:T(8,128)(2,1)S(1)}, u32[]{:S(2)}, u32[]{:S(2)}) async-start(bf16[32,16,2560]{2,1,0:T(8,128)(2,1)} %maximum_maximum_fusion), calls=%async_computation.3 | async-start | bytes 5242880 | tf_op jit(solution)/shard_map/all_to_all | solution.py:160
  189.9 0.0 copy-done.4
  189.9 0.0 copy-done.3
  190.0 0.5 select_reduce_fusion.1
  190.5 4.0 %convolution_add_fusion.1 = f32[128,2560]{1,0:T(8,128)} fusion(f32[128,512]{1,0:T(8,128)S(1)} %get-tuple-element.17, bf16[512,2560]{1,0:T(8,128)(2,1)} %bitcast.13, bf16[1,128,2560]{2,1,0:T(8,128)(2,1)S(1)} %copy-done), kind=kOutput, calls=%fused_computation.4 | convolution fusion | flops 2013921280 | bytes 4849664 | tf_op jit(solution)/shard_map/dot_general | solution.py:165
  194.5 31.6 %all-to-all-done.3 = bf16[32,16,2560]{2,1,0:T(8,128)(2,1)S(1)} async-done(((bf16[32,16,2560]{2,1,0:T(8,128)(2,1)}), bf16[32,16,2560]{2,1,0:T(8,128)(2,1)S(1)}, u32[]{:S(2)}, u32[]{:S(2)}) %all-to-all-start.3) | async-done | bytes 2621472 | tf_op jit(solution)/shard_map/all_to_all | solution.py:160
  226.1 2.2 fusion.1
  228.3 1.3 collective-permute-start
  229.6 0.1 fusion.16
  229.7 0.1 reshape.124
  229.8 1.1 select_reduce_fusion
  230.8 14.1 %collective-permute-done = bf16[1,128,2560]{2,1,0:T(8,128)(2,1)} collective-permute-done((bf16[1,128,2560]{2,1,0:T(8,128)(2,1)S(1)}, bf16[1,128,2560]{2,1,0:T(8,128)(2,1)}, u32[]{:S(2)}, u32[]{:S(2)}) %collective-permute-start) | collective-permute-done | bytes 655392 | tf_op jit(solution)/shard_map/ppermute | solution.py:11
  245.0 2.0 copy.64
  (5 shorter events, 0.1 us)
Async XLA Ops:
  7.6 9.5 %copy-start = (bf16[1,128,2560]{2,1,0:T(8,128)(2,1)S(1)}, bf16[1,128,2560]{2,1,0:T(8,128)(2,1)}, u32[]{:S(2)}) copy-start(bf16[1,128,2560]{2,1,0:T(8,128)(2,1)} %param.7) | copy-start | bytes 1966084
  7.6 74.6 %all-to-all-start = ((bf16[32,16,5120]{2,1,0:T(8,128)(2,1)}), bf16[32,16,5120]{2,1,0:T(8,128)(2,1)}, u32[]{:S(2)}, u32[]{:S(2)}) async-start(bf16[32,16,5120]{2,1,0:T(8,128)(2,1)} %bitcast.72), calls=%async_computation | async-start | bytes 10485760 | tf_op jit(solution)/shard_map/all_to_all | solution.py:137
  17.1 1.2 copy-start.1
  82.2 55.8 %all-to-all-start.1 = ((bf16[32,24,2560]{2,1,0:T(8,128)(2,1)}), bf16[32,24,2560]{2,1,0:T(8,128)(2,1)}, u32[]{:S(2)}, u32[]{:S(2)}) async-start(bf16[32,24,2560]{2,1,0:T(8,128)(2,1)} %bitcast.73), calls=%async_computation.1 | async-start | bytes 7864320 | tf_op jit(solution)/shard_map/all_to_all | solution.py:138
  142.8 41.0 %all-to-all-start.2 = ((bf16[32,16,2560]{2,1,0:T(8,128)(2,1)}), bf16[32,16,2560]{2,1,0:T(8,128)(2,1)}, u32[]{:S(2)}, u32[]{:S(2)}) async-start(bf16[32,16,2560]{2,1,0:T(8,128)(2,1)} %bitcast.77), calls=%async_computation.2 | async-start | bytes 5242880 | tf_op jit(solution)/shard_map/all_to_all | solution.py:141
  176.8 2.5 %copy-start.2 = (f32[384,128]{1,0:T(8,128)S(1)}, f32[384,128]{1,0:T(8,128)}, u32[]{:S(2)}) copy-start(f32[384,128]{1,0:T(8,128)} %get-tuple-element.15) | copy-start | bytes 589828
  182.6 7.3 %copy-start.4 = (f32[1,128,6]{1,0,2:T(1,128)S(1)}, f32[1,128,6]{1,0,2:T(1,128)}, u32[]{:S(2)}) copy-start(f32[1,128,6]{1,0,2:T(1,128)} %param.10) | copy-start | bytes 9220
  182.6 7.3 %copy-start.3 = (s32[1,128,6]{1,0,2:T(1,128)S(1)}, s32[1,128,6]{1,0,2:T(1,128)}, u32[]{:S(2)}) copy-start(s32[1,128,6]{1,0,2:T(1,128)} %param.9) | copy-start | bytes 9220
  183.8 42.3 %all-to-all-start.3 = ((bf16[32,16,2560]{2,1,0:T(8,128)(2,1)}), bf16[32,16,2560]{2,1,0:T(8,128)(2,1)S(1)}, u32[]{:S(2)}, u32[]{:S(2)}) async-start(bf16[32,16,2560]{2,1,0:T(8,128)(2,1)} %maximum_maximum_fusion), calls=%async_computation.3 | async-start | bytes 5242880 | tf_op jit(solution)/shard_map/all_to_all | solution.py:160
  228.3 16.7 %collective-permute-start = (bf16[1,128,2560]{2,1,0:T(8,128)(2,1)S(1)}, bf16[1,128,2560]{2,1,0:T(8,128)(2,1)}, u32[]{:S(2)}, u32[]{:S(2)}) collective-permute-start(bf16[1,128,2560]{2,1,0:T(8,128)(2,1)S(1)} %fusion.1), channel_id=1, source_target_pairs={{32,0},{64,32},{96,64},{33,1},{65,33},{97,65},{34,2},{66,34},{98,6... | collective-permute-start | bytes 1966088 | tf_op jit(solution)/shard_map/ppermute | solution.py:11
